TPU v7x, 256 devices: a whole 4x4x8 slice. The times are simulated.
256 devices in a mesh: dp: 2 (over y_hi), ctx: 64 (over y_lo, x, z), head: 2 (over core).
Axes of the slice: x: 4, y: 4 (y_hi: 2, y_lo: 2; y = y_hi * 2 + y_lo), z: 8, core: 2. Of those that a mesh axis runs over, the one named last changes fastest.
Arguments:
- hidden_in: bfloat16 [2, 8192, 4096], P('dp', 'ctx'), may hold values from -16 to 16
- proj_weight: bfloat16 [4096, 2, 256], P(('dp', 'ctx'), None, 'head'), may hold values from -0.0029296875 to 0.0029296875
- values_in: bfloat16 [2, 8192, 4096], P('dp', 'ctx', 'head'), may hold values from -6 to 6
- gate_in: bfloat16 [2, 8192, 4096], P('dp', 'ctx', 'head'), may hold values from -6 to 6
- log_decay: float32 [2, 64, 8192], P('dp', 'head', 'ctx'), may hold values from -1 to 0, as said below
- skip_gain: float32 [64], P('head'), may hold values from 0.5 to 2
- grad_out: bfloat16 [2, 8192, 4096], P('dp', 'ctx', 'head'), may hold values from -6 to 6
Outputs:
- grad_input: bfloat16 [2, 8192, 4096], P('dp', 'ctx', 'head')
- grad_values: bfloat16 [2, 8192, 4096], P('dp', 'ctx', 'head')
- grad_gate: bfloat16 [2, 8192, 4096], P('dp', 'ctx', 'head')
- grad_proj: float32 [4096, 2, 256], P(('dp', 'ctx'), None, 'head')
Inputs may be any that keep to these rules, and one draw needn't show every extreme that they name: `log_decay`: logarithms of the per-token decay of each head's state; all values are at most zero.
All inputs are finite; a program needn't handle non-finite values.
Results may differ from a plain program's by a relative error of at most 0.011.
Values may be sent and summed in bfloat16 or wider, within the bound.
No kernel may reach another device: no remote copies, remote signals or barrier semaphores. Data moves between devices by JAX's collectives and lax.ppermute only.
A program may use at most 192 MiB of HBM per device.

v0:
```python
import jax
import jax.numpy as jnp
from jax import lax
from jax.sharding import PartitionSpec as P

HEAD_DIM = 64
STATE = 64
SPAN = 128


def carried_in(part, axis, combine, identity, reverse):
    count = lax.axis_size(axis)
    place = lax.axis_index(axis)
    ahead = count - 1 - place if reverse else place
    gathered = jax.tree.map(lambda a: lax.all_gather(a, axis), part)
    state = jax.tree.map(lambda a, e: jnp.zeros_like(a) + jnp.asarray(e, a.dtype), part, identity)

    def one(lap, state):
        source = count - 1 - lap if reverse else lap
        return combine(
            state, jax.tree.map(lambda a: lax.dynamic_index_in_dim(a, source, 0, False), gathered)
        )

    return lax.fori_loop(0, ahead, one, state)


def span_summary(b_vals, c_vals, x_vals, dy_round, rate_vals):
    block_len = x_vals.shape[0]
    head_count = x_vals.shape[1]
    group_count = b_vals.shape[1]
    per_group = head_count // group_count
    cumlog = jnp.cumsum(rate_vals, axis=1)
    final_log = cumlog[:, -1]
    to_end = jnp.exp(final_log[:, None] - cumlog)
    from_start = jnp.exp(cumlog)
    b_wide = b_vals.astype(jnp.float32)
    c_wide = c_vals.astype(jnp.float32)
    x_scaled = (x_vals.astype(jnp.float32) * to_end.T[:, :, None]).reshape(
        block_len, group_count, per_group, HEAD_DIM
    )
    dy_scaled = (dy_round.astype(jnp.float32) * from_start.T[:, :, None]).reshape(
        block_len, group_count, per_group, HEAD_DIM
    )
    state_part = jnp.einsum("qgn,qgkp->ngkp", b_wide, x_scaled, precision=lax.Precision.HIGHEST)
    adjoint_part = jnp.einsum("qgn,qgkp->ngkp", c_wide, dy_scaled, precision=lax.Precision.HIGHEST)
    return (jnp.exp(final_log), state_part.reshape(STATE, -1), adjoint_part.reshape(STATE, -1))


def span_full(
    b_vals,
    c_vals,
    x_vals,
    dy_round,
    rate_vals,
    skip_vals,
    state_in,
    adjoint_out,
    dout_vals,
    gate_vals,
):
    block_len = x_vals.shape[0]
    head_count = x_vals.shape[1]
    group_count = b_vals.shape[1]
    per_group = head_count // group_count
    cumlog = jnp.cumsum(rate_vals, axis=1)
    final_log = cumlog[:, -1]
    to_end = jnp.exp(final_log[:, None] - cumlog)
    from_start = jnp.exp(cumlog)
    causal = jnp.arange(block_len)[:, None] >= jnp.arange(block_len)[None, :]
    log_gaps = cumlog[:, :, None] - cumlog[:, None, :]
    decays = jnp.where(causal[None], jnp.exp(jnp.where(causal[None], log_gaps, 0.0)), 0.0)
    b_wide = b_vals.astype(jnp.float32)
    c_wide = c_vals.astype(jnp.float32)
    cb_dots = jnp.einsum("tgn,sgn->gts", c_vals, b_vals, preferred_element_type=jnp.float32)
    mixer_bf = (decays * jnp.repeat(cb_dots, per_group, axis=0)).astype(jnp.bfloat16)
    state_four = state_in.reshape(STATE, group_count, per_group, HEAD_DIM)
    adjoint_four = adjoint_out.reshape(STATE, group_count, per_group, HEAD_DIM)
    y_intra = jnp.einsum("hts,shp->thp", mixer_bf, x_vals, preferred_element_type=jnp.float32)
    y_inter = jnp.einsum(
        "tgn,ngkp->tgkp", c_wide, state_four, precision=lax.Precision.HIGHEST
    ).reshape(block_len, head_count, HEAD_DIM)
    x_wide = x_vals.astype(jnp.float32)
    output_pre = y_intra + y_inter * from_start.T[:, :, None] + skip_vals[None, :, None] * x_wide
    gate_wide = gate_vals.astype(jnp.float32)
    gate_sig = jax.nn.sigmoid(gate_wide)
    grad_gate = (
        dout_vals.astype(jnp.float32) * output_pre * gate_sig * (1.0 + gate_wide * (1.0 - gate_sig))
    ).astype(jnp.bfloat16)
    dy_wide = dy_round.astype(jnp.float32)
    x_inter = jnp.einsum(
        "sgn,ngkp->sgkp", b_wide, adjoint_four, precision=lax.Precision.HIGHEST
    ).reshape(block_len, head_count, HEAD_DIM)
    grad_vals = (
        jnp.einsum("hts,thp->shp", mixer_bf, dy_round, preferred_element_type=jnp.float32)
        + x_inter * to_end.T[:, :, None]
        + skip_vals[None, :, None] * dy_wide
    )
    mix_grad = (
        jnp.einsum("thp,shp->hts", dy_round, x_vals, preferred_element_type=jnp.float32) * decays
    )
    dots_grad = (
        mix_grad.reshape(group_count, per_group, block_len, block_len)
        .sum(axis=1)
        .astype(jnp.bfloat16)
    )
    dy_scaled = (dy_wide * from_start.T[:, :, None]).reshape(
        block_len, group_count, per_group, HEAD_DIM
    )
    x_scaled = (x_wide * to_end.T[:, :, None]).reshape(block_len, group_count, per_group, HEAD_DIM)
    c_grad = jnp.einsum(
        "gts,sgn->tgn", dots_grad, b_vals, preferred_element_type=jnp.float32
    ) + jnp.einsum("tgkp,ngkp->tgn", dy_scaled, state_four, precision=lax.Precision.HIGHEST)
    b_grad = jnp.einsum(
        "gts,tgn->sgn", dots_grad, c_vals, preferred_element_type=jnp.float32
    ) + jnp.einsum("sgkp,ngkp->sgn", x_scaled, adjoint_four, precision=lax.Precision.HIGHEST)
    return (grad_vals.astype(jnp.bfloat16), grad_gate, jnp.stack([b_grad, c_grad], axis=1))


def chain(earlier, later):
    return (earlier[0] * later[0], earlier[1] * jnp.repeat(later[0], HEAD_DIM)[None, :] + later[1])


def body(hidden_in, proj_weight, values_in, gate_in, log_decay, skip_gain, grad_out):
    tokens = hidden_in[0]
    tok_rows = tokens.shape[0]
    weight_local = proj_weight.reshape(proj_weight.shape[0], -1)
    col_count = weight_local.shape[1]
    weight_full = lax.all_gather(weight_local, ("dp", "ctx"), axis=0, tiled=True)
    bc_sums = jnp.dot(tokens, weight_full, preferred_element_type=jnp.float32)
    group_count = col_count // (2 * STATE)
    head_count = values_in.shape[2] // HEAD_DIM
    nblocks = tok_rows // SPAN
    bc_vals = bc_sums.astype(jnp.bfloat16).reshape(nblocks, SPAN, 2, group_count, STATE)
    x_vals = values_in[0].reshape(nblocks, SPAN, head_count, HEAD_DIM)
    gate_vals = gate_in[0].reshape(nblocks, SPAN, head_count, HEAD_DIM)
    dout_vals = grad_out[0].reshape(nblocks, SPAN, head_count, HEAD_DIM)
    dy_round = (dout_vals.astype(jnp.float32) * jax.nn.silu(gate_vals.astype(jnp.float32))).astype(
        jnp.bfloat16
    )
    rate_vals = log_decay[0].reshape(head_count, nblocks, SPAN)
    summaries = [
        span_summary(bc_vals[0, :, 0], bc_vals[0, :, 1], x_vals[0], dy_round[0], rate_vals[:, 0])
    ]
    dev_decay = jnp.ones((head_count,), jnp.float32)
    dev_state = jnp.zeros((STATE, head_count * HEAD_DIM), jnp.float32)
    dev_adjoint = jnp.zeros((STATE, head_count * HEAD_DIM), jnp.float32)
    block_id = 0
    dev_state = (
        dev_state * jnp.repeat(summaries[block_id][0], HEAD_DIM)[None, :] + summaries[block_id][1]
    )
    dev_decay = dev_decay * summaries[block_id][0]
    for block_id in reversed(range(nblocks)):
        dev_adjoint = (
            dev_adjoint * jnp.repeat(summaries[block_id][0], HEAD_DIM)[None, :]
            + summaries[block_id][2]
        )
    identity = (
        jnp.ones((head_count,), jnp.float32),
        jnp.zeros((STATE, head_count * HEAD_DIM), jnp.float32),
    )
    state_start = carried_in((dev_decay, dev_state), "ctx", chain, identity, False)[1]
    adjoint_end = carried_in((dev_decay, dev_adjoint), "ctx", chain, identity, True)[1]
    running = state_start
    block_id = 0
    states_in = running
    adjoints_out = [None] * nblocks
    running = adjoint_end
    for block_id in reversed(range(nblocks)):
        adjoints_out[block_id] = running
        running = (
            running * jnp.repeat(summaries[block_id][0], HEAD_DIM)[None, :] + summaries[block_id][2]
        )
    results = [
        span_full(
            bc_vals[0, :, 0],
            bc_vals[0, :, 1],
            x_vals[0],
            dy_round[0],
            rate_vals[:, 0],
            skip_gain,
            states_in,
            adjoints_out[0],
            dout_vals[0],
            gate_vals[0],
        )
    ]
    grad_values = jnp.concatenate([entry[0] for entry in results], axis=0).reshape(
        1, tok_rows, head_count * HEAD_DIM
    )
    grad_gate = jnp.concatenate([entry[1] for entry in results], axis=0).reshape(
        1, tok_rows, head_count * HEAD_DIM
    )
    grad_flat = (
        jnp.concatenate([entry[2] for entry in results], axis=0)
        .reshape(tok_rows, col_count)
        .astype(jnp.bfloat16)
    )
    input_terms = jnp.einsum(
        "tc,dc->td", grad_flat, weight_full, preferred_element_type=jnp.float32
    )
    grad_input = lax.psum_scatter(
        input_terms.astype(jnp.bfloat16), "head", scatter_dimension=1, tiled=True
    )[None]
    scale = 1.0 / (lax.axis_size("dp") * lax.axis_size("ctx") * tok_rows)
    grad_proj = lax.psum_scatter(
        jnp.einsum("td,tc->dc", tokens, grad_flat, preferred_element_type=jnp.float32) * scale,
        ("dp", "ctx"),
        scatter_dimension=0,
        tiled=True,
    )
    grad_proj = grad_proj.reshape(-1, 2, col_count // 2)
    return (grad_input, grad_values, grad_gate, grad_proj)


def solution(mesh):
    return jax.shard_map(
        body,
        mesh=mesh,
        in_specs=(
            P("dp", "ctx", None),
            P(("dp", "ctx"), None, "head"),
            P("dp", "ctx", "head"),
            P("dp", "ctx", "head"),
            P("dp", "head", "ctx"),
            P("head"),
            P("dp", "ctx", "head"),
        ),
        out_specs=(
            P("dp", "ctx", "head"),
            P("dp", "ctx", "head"),
            P("dp", "ctx", "head"),
            P(("dp", "ctx"), None, "head"),
        ),
        check_vma=False,
    )
```

profile of v0, /device:TPU:24, one launch (start us, length us, event | category | flops | bytes accessed | tf_op | source)
XLA Modules:
  0.0 1722.3 jit_solution(12229518481348502227)
XLA Ops:
  7.2 1.4 copy.67
  12.9 2.0 copy.46
  16.2 113.7 %all-gather.5.cloned.1.call-done = bf16[4096,256]{1,0:T(8,128)(2,1)} async-done(((bf16[32,256]{1,0:T(8,128)(2,1)}), bf16[4096,256]{1,0:T(8,128)(2,1)}) %all-gather.5.cloned.1.call-update) | async-done | bytes 2097168 | tf_op jit(solution)/shard_map/all_gather | solution.py:128
  129.9 2.0 convolution_convert_fusion.1
  132.0 2.7 fusion.17
  134.7 2.3 copy.47
  137.0 2.7 fusion.14
  139.7 2.4 copy.50
  142.0 2.3 broadcast_add_fusion.1
  146.5 162.7 %all-reduce = f32[2048]{0:T(1024)S(1)} all-reduce(f32[2048]{0:T(1024)S(1)} %dynamic-update-slice), channel_id=2, replica_groups=mesh['dp'=2,'ctx'=64,'head'=2] {'ctx'}, use_global_device_ids=true, to_apply=%add | all-reduce | flops 2048 | bytes 16384
  311.6 212.1 %all-gather.9.cloned.1.call-done = f32[64,64,2048]{2,1,0:T(8,128)} async-done(((f32[1,64,2048]{2,1,0:T(8,128)}), f32[64,64,2048]{2,1,0:T(8,128)}) %all-gather.9.cloned.1.call-update) | async-done | bytes 33554448 | tf_op jit(solution)/shard_map/all_gather | solution.py:15
  523.8 46.0 %while.27 = (s32[]{:T(128)}, f32[64,2048]{1,0:T(8,128)S(1)}, s32[]{:T(128)}, f32[64,32]{1,0:T(8,128)S(1)}, f32[64,64,2048]{2,1,0:T(8,128)}, /*index=5*/s32[]{:T(128)}, s32[]{:T(128)}, s32[]{:T(128)}) while((s32[]{:T(128)}, f32[64,2048]{1,0:T(8,128)S(1)}, s32[]{:T(128)}, f32[64,32]{1,0:T(8,128)S(1)}, f32[64,64,2048]{2,1,0:T(8,128)}, ...), condition=%wide.region_5.6_spmd, body=%wide.region_4.5_spmd.sunk | while | flops 262149 | bytes 1606151 | solution.py:24
  569.8 1.3 copy.64
  571.1 3.1 convolution_bitcast_fusion.2
  574.2 323.6 %all-gather.7.cloned.1.call-done = f32[64,64,2048]{2,1,0:T(8,128)} async-done(((f32[1,64,2048]{2,1,0:T(8,128)}), f32[64,64,2048]{2,1,0:T(8,128)}) %all-gather.7.cloned.1.call-update) | async-done | bytes 33554448 | tf_op jit(solution)/shard_map/all_gather | solution.py:15
  897.9 44.5 %while.26 = (s32[]{:T(128)}, f32[64,2048]{1,0:T(8,128)S(1)}, s32[]{:T(128)}, f32[64,32]{1,0:T(8,128)S(1)}, f32[64,64,2048]{2,1,0:T(8,128)}, /*index=5*/s32[]{:T(128)}, s32[]{:T(128)}, s32[]{:T(128)}, s32[]{:T(128)}) while((s32[]{:T(128)}, f32[64,2048]{1,0:T(8,128)S(1)}, s32[]{:T(128)}, f32[64,32]{1,0:T(8,128)S(1)}, f32[64,64,2048]{2,1,0:T(8,128)}, ...), condition=%wide.region_3.4_spmd, body=%wide.region_2.3_spmd.sunk | while | flops 262150 | bytes 1606171 | solution.py:24
  942.4 1.4 copy.63
  943.8 3.1 convolution_bitcast_fusion.3
  947.2 2.7 fusion
  949.9 5.6 copy.61
  955.8 3.5 convolution_convert_fusion
  962.9 2.0 copy.54
  968.4 659.3 %reduce-scatter.7.cloned.1.call-done = f32[32,256]{1,0:T(8,128)} async-done(((f32[4096,256]{1,0:T(8,128)}), f32[32,256]{1,0:T(8,128)}) %reduce-scatter.7.cloned.1.call-update) | async-done | bytes 32784
  1629.2 86.6 %reduce-scatter.5.cloned.1.call-done = bf16[128,2048]{1,0:T(8,128)(2,1)} async-done(((bf16[128,4096]{1,0:T(8,128)(2,1)}), bf16[128,2048]{1,0:T(8,128)(2,1)}) %reduce-scatter.5.cloned.1.call-update) | async-done | bytes 524304 | tf_op jit(solution)/shard_map/reduce_scatter | solution.py:201
  (331 shorter events, 107.1 us)
Async XLA Ops:
  7.2 122.7 %copy-start = (bf16[1,128,4096]{2,1,0:T(8,128)(2,1)S(1)}, bf16[1,128,4096]{2,1,0:T(8,128)(2,1)}, u32[]{:S(2)}) copy-start(bf16[1,128,4096]{2,1,0:T(8,128)(2,1)} %param.11) | copy-start | bytes 3145732
  7.2 3.0 copy-start.13
  7.2 122.7 %all-gather.5.cloned.1.call-start = ((), (), s32[]{:S(2)}) async-start(), calls=%async_computation.2 | async-start | bytes 2113536 | tf_op jit(solution)/shard_map/all_gather | solution.py:128
  8.7 515.0 %all-gather.9.cloned.1.call-start = ((), (), s32[]{:S(2)}) async-start(), calls=%async_computation.4 | async-start | bytes 34078720 | tf_op jit(solution)/shard_map/all_gather | solution.py:15
  10.1 2.2 copy-start.14
  12.3 297.1 %copy-start.2 = (f32[1,128,2048]{1,2,0:T(8,128)}, f32[1,128,2048]{1,2,0:T(8,128)S(1)}, u32[]{:S(2)}) copy-start(f32[1,128,2048]{1,2,0:T(8,128)S(1)} %convert_element_type.117) | copy-start | bytes 3145732
  139.7 5.4 copy-start.16
  144.3 753.5 %all-gather.7.cloned.1.call-start = ((), (), s32[]{:S(2)}) async-start(), calls=%async_computation.3 | async-start | bytes 34078720 | tf_op jit(solution)/shard_map/all_gather | solution.py:15
  145.1 1482.6 %reduce-scatter.7.cloned.1.call-start = ((), (), s32[]{:S(2)}) async-start(), calls=%async_computation.6 | async-start | bytes 4227072
  309.3 1.1 copy-start.7
  309.7 0.8 copy-start.11
  523.8 47.3 %copy-start.6 = (bf16[128,2,16,64]{0,3,2,1:T(8,128)(2,1)S(1)}, bf16[128,2,16,64]{0,3,2,1:T(8,128)(2,1)}, u32[]{:S(2)}) copy-start(bf16[128,2,16,64]{0,3,2,1:T(8,128)(2,1)} %multiply_convert_fusion) | copy-start | bytes 1572868
  897.8 46.0 %copy-start.8 = (bf16[1,128,2048]{1,2,0:T(8,128)(2,1)S(1)}, bf16[1,128,2048]{1,2,0:T(8,128)(2,1)}, u32[]{:S(2)}) copy-start(bf16[1,128,2048]{1,2,0:T(8,128)(2,1)} %copy.46) | copy-start | bytes 1572868
  955.5 4.7 copy-start.5
  955.6 760.2 %reduce-scatter.5.cloned.1.call-start = ((), (), s32[]{:S(2)}) async-start(), calls=%async_computation.5 | async-start | bytes 1572864 | tf_op jit(solution)/shard_map/reduce_scatter | solution.py:201
  960.2 1.0 copy-start.9
  960.2 1.4 copy-start.12
  960.3 1.4 copy-start.15
  961.7 3.3 copy-start.4
  964.9 1.2 copy-start.3
  964.9 1.5 copy-start.10
  966.5 749.3 %copy-start.1 = (bf16[1,128,4096]{2,1,0:T(8,128)(2,1)S(1)}, bf16[1,128,4096]{2,1,0:T(8,128)(2,1)}, u32[]{:S(2)}) copy-start(bf16[1,128,4096]{2,1,0:T(8,128)(2,1)} %param.11) | copy-start | bytes 3145732
Sparse Core Ops, SparseCore 0:
  12.2 117.6 all-gather.4
  144.5 379.2 all-gather.8
  526.1 371.6 all-gather.6
  955.7 671.9 reduce-scatter.6
  1630.6 85.1 reduce-scatter.4
where the time goes:
time: 1730 us; the launch traced here: 1720 us
  waiting for transfers between devices  1400 us (81%)
  blocking collectives  163 us (9%)
  other arithmetic  85.1 us (5%)
  local copies, waits for them, and re-layouts  36.8 us (2%)
  matrix products  24.6 us (1%)
    unnamed x6, waiting for transfers between devices  660 us
    all_gather x2, waiting for transfers between devices, carried_in(): gathered = jax.tree.map(lambda a: lax.all_gather(a, axis), part)  536 us
    unnamed x1, blocking collectives  163 us
    all_gather x1, waiting for transfers between devices, body(): lax.all_gather(weight_local, ('dp', 'ctx'), axis=0, tiled=True)  114 us
    reduce_scatter x1, waiting for transfers between devices, body(): lax.psum_scatter(input_terms.astype(jnp.bfloat16), 'head', scatter_dimens...  86.6 us
    add x63, other arithmetic, chain(): earlier[1] * jnp.repeat(later[0], HEAD_DIM)[None, :] + later[1]  78.9 us
  transfers between devices with their start and end apart: 5, of which 5 were waited for; matrix products, arithmetic and copies ran while one was open for 4% of the time, Pallas kernels for 0%

commit v1 on v0

--- a/solution.py
+++ b/solution.py
@@ -11,17 +11,27 @@
 def carried_in(part, axis, combine, identity, reverse):
     count = lax.axis_size(axis)
     place = lax.axis_index(axis)
+
+    def shifted(tree, offset):
+        if reverse:
+            pairs = [(i + offset, i) for i in range(count - offset)]
+        else:
+            pairs = [(i, i + offset) for i in range(count - offset)]
+        return jax.tree.map(lambda a: lax.ppermute(a, axis, pairs), tree)
+
     ahead = count - 1 - place if reverse else place
-    gathered = jax.tree.map(lambda a: lax.all_gather(a, axis), part)
-    state = jax.tree.map(lambda a, e: jnp.zeros_like(a) + jnp.asarray(e, a.dtype), part, identity)
-
-    def one(lap, state):
-        source = count - 1 - lap if reverse else lap
-        return combine(
-            state, jax.tree.map(lambda a: lax.dynamic_index_in_dim(a, source, 0, False), gathered)
-        )
-
-    return lax.fori_loop(0, ahead, one, state)
+    state = jax.tree.map(
+        lambda a, e: jnp.where(ahead >= 1, a, jnp.asarray(e, a.dtype)),
+        shifted(part, 1),
+        identity,
+    )
+    offset = 1
+    while offset < count:
+        earlier = shifted(state, offset)
+        merged = combine(earlier, state)
+        state = jax.tree.map(lambda m, s: jnp.where(ahead >= offset, m, s), merged, state)
+        offset *= 2
+    return state
 
 
 def span_summary(b_vals, c_vals, x_vals, dy_round, rate_vals):
@@ -202,12 +212,16 @@
         input_terms.astype(jnp.bfloat16), "head", scatter_dimension=1, tiled=True
     )[None]
     scale = 1.0 / (lax.axis_size("dp") * lax.axis_size("ctx") * tok_rows)
-    grad_proj = lax.psum_scatter(
-        jnp.einsum("td,tc->dc", tokens, grad_flat, preferred_element_type=jnp.float32) * scale,
+    proj_terms = jnp.einsum("td,tc->dc", tokens, grad_flat, preferred_element_type=jnp.float32)
+    shard_count = lax.axis_size(("dp", "ctx"))
+    proj_parts = lax.all_to_all(
+        proj_terms.reshape(shard_count, -1, col_count),
         ("dp", "ctx"),
-        scatter_dimension=0,
+        0,
+        0,
         tiled=True,
     )
+    grad_proj = proj_parts.sum(axis=0) * scale
     grad_proj = grad_proj.reshape(-1, 2, col_count // 2)
     return (grad_input, grad_values, grad_gate, grad_proj)
 

time: 1730 us -> 448 us (0.26)
  waiting for transfers between devices: 1400 us -> 217 us
  blocking collectives: 163 us -> 0 us
  starting transfers between devices: 0.38 us -> 128 us
  other arithmetic: 85.1 us -> 28.1 us
    unnamed x6 -> x2, waiting for transfers between devices: 660 us -> 0.03 us
    all_gather x2 -> x0, waiting for transfers between devices: 536 us -> none  [carried_in(): gathered = jax.tree.map(lambda a: lax.all_gather(a, axis), part)]
    unnamed x1 -> x0, blocking collectives: 163 us -> none
    ppermute x0 -> x26, starting transfers between devices: none -> 117 us  [shifted(): return jax.tree.map(lambda a: lax.ppermute(a, axis, pairs), tree)]
    reduce_scatter x1, waiting for transfers between devices: 86.6 us -> 0.01 us  [body(): lax.psum_scatter(input_terms.astype(jnp.bfloat16), 'head', scatter_dimens...]
    add x63 -> x0, other arithmetic: 78.9 us -> none  [chain(): earlier[1] * jnp.repeat(later[0], HEAD_DIM)[None, :] + later[1]]
    all_to_all x0 -> x1, waiting for transfers between devices: none -> 68.4 us  [body(): lax.all_to_all(proj_terms.reshape(shard_count, -1, col_count), ('dp', 'ct...]
    ppermute x0 -> x26, waiting for transfers between devices: none -> 63 us  [shifted(): return jax.tree.map(lambda a: lax.ppermute(a, axis, pairs), tree)]
  transfers between devices with their start and end apart: 5 -> 29, of which waited for: 5 -> 11; matrix products, arithmetic and copies ran while one was open for 4% -> 15% of each run, Pallas kernels for 0% -> 0%
where the time goes in v1:
time: 448 us; the launch traced here: 444 us
  waiting for transfers between devices  217 us (48%)
  starting transfers between devices  128 us (29%)
  local copies, waits for them, and re-layouts  29.4 us (7%)
  other arithmetic  28.1 us (6%)
  matrix products  27 us (6%)
  between operations  14.7 us (3%)
    ppermute x26, starting transfers between devices, shifted(): return jax.tree.map(lambda a: lax.ppermute(a, axis, pairs), tree)  117 us
    all_gather x1, waiting for transfers between devices, body(): lax.all_gather(weight_local, ('dp', 'ctx'), axis=0, tiled=True)  85.7 us
    all_to_all x1, waiting for transfers between devices, body(): lax.all_to_all(proj_terms.reshape(shard_count, -1, col_count), ('dp', 'ct...  68.4 us
    ppermute x26, waiting for transfers between devices, shifted(): return jax.tree.map(lambda a: lax.ppermute(a, axis, pairs), tree)  63 us
    select_n x22, other arithmetic, carried_in(): jnp.where(ahead >= offset, m, s)  16.7 us
    unnamed x28, local copies, waits for them, and re-layouts  11.6 us
    all_to_all x1, starting transfers between devices, body(): lax.all_to_all(proj_terms.reshape(shard_count, -1, col_count), ('dp', 'ct...  11 us
  transfers between devices with their start and end apart: 29, of which 11 were waited for; matrix products, arithmetic and copies ran while one was open for 15% of the time, Pallas kernels for 0%

profile of v1, /device:TPU:24, one launch (start us, length us, event | category | flops | bytes accessed | tf_op | source)
XLA Modules:
  0.0 444.4 jit_solution(12572893252828934312)
XLA Ops:
  9.9 10.1 %collective-permute-start.2 = (f32[32]{0:T(128)S(1)}, f32[32]{0:T(128)S(1)}, u32[]{:S(2)}, u32[]{:S(2)}) collective-permute-start(f32[32]{0:T(128)S(1)} %get-tuple-element.21), channel_id=1, source_target_pairs={{2,0},{4,2},{6,4},{8,6},{10,8},{12,10},{14,12},{16,14},{18,16},{20... | collective-permute-start | bytes 392 | tf_op jit(solution)/shard_map/ppermute | solution.py:20
  30.4 8.1 %collective-permute-start.4 = (f32[32]{0:T(128)S(1)}, f32[32]{0:T(128)S(1)}, u32[]{:S(2)}, u32[]{:S(2)}) collective-permute-start(f32[32]{0:T(128)S(1)} %broadcast_select_fusion.13), channel_id=1, source_target_pairs={{2,0},{4,2},{6,4},{8,6},{10,8},{12,10},{14,12},{16,14},{18,16},{20... | collective-permute-start | bytes 392 | tf_op jit(solution)/shard_map/ppermute | solution.py:20
  40.8 3.4 collective-permute-start.6
  44.2 85.7 %all-gather.2.cloned.1.call-done = bf16[4096,256]{1,0:T(8,128)(2,1)} async-done(((bf16[32,256]{1,0:T(8,128)(2,1)}), bf16[4096,256]{1,0:T(8,128)(2,1)}) %all-gather.2.cloned.1.call-update) | async-done | bytes 2097168 | tf_op jit(solution)/shard_map/all_gather | solution.py:138
  132.0 2.7 fusion.16
  144.3 4.4 %collective-permute-start = (f32[64,2048]{1,0:T(8,128)}, f32[64,2048]{1,0:T(8,128)}, u32[]{:S(2)}, u32[]{:S(2)}) collective-permute-start(f32[64,2048]{1,0:T(8,128)} %get-tuple-element.19), channel_id=1, source_target_pairs={{2,0},{4,2},{6,4},{8,6},{10,8},{12,10},{14,12},{16,14},{18,16},{20... | collective-permute-start | bytes 1572872 | tf_op jit(solution)/shard_map/ppermute | solution.py:20
  151.0 6.3 %collective-permute-start.8 = (f32[32]{0:T(128)S(1)}, f32[32]{0:T(128)S(1)}, u32[]{:S(2)}, u32[]{:S(2)}) collective-permute-start(f32[32]{0:T(128)S(1)} %broadcast_select_fusion.11), channel_id=1, source_target_pairs={{8,0},{10,2},{12,4},{14,6},{16,8},{18,10},{20,12},{22,14},{24,16},... | collective-permute-start | bytes 392 | tf_op jit(solution)/shard_map/ppermute | solution.py:20
  165.3 8.9 %collective-permute-start.1 = (f32[64,2048]{1,0:T(8,128)S(1)}, f32[64,2048]{1,0:T(8,128)S(1)}, u32[]{:S(2)}, u32[]{:S(2)}) collective-permute-start(f32[64,2048]{1,0:T(8,128)S(1)} %broadcast_select_fusion.1), channel_id=1, source_target_pairs={{2,0},{4,2},{6,4},{8,6},{10,8},{12,10},{14,12},{16,14},{18,16},{20... | collective-permute-start | bytes 1572872 | tf_op jit(solution)/shard_map/ppermute | solution.py:20
  184.0 12.4 %collective-permute-start.3 = (f32[64,2048]{1,0:T(8,128)}, f32[64,2048]{1,0:T(8,128)}, u32[]{:S(2)}, u32[]{:S(2)}) collective-permute-start(f32[64,2048]{1,0:T(8,128)} %add_select_fusion.11), channel_id=1, source_target_pairs={{4,0},{6,2},{8,4},{10,6},{12,8},{14,10},{16,12},{18,14},{20,16},{2... | collective-permute-start | bytes 1572872 | tf_op jit(solution)/shard_map/ppermute | solution.py:20
  201.9 14.4 %collective-permute-done.3 = f32[64,2048]{1,0:T(8,128)} collective-permute-done((f32[64,2048]{1,0:T(8,128)}, f32[64,2048]{1,0:T(8,128)}, u32[]{:S(2)}, u32[]{:S(2)}) %collective-permute-start.3) | collective-permute-done | bytes 524320 | tf_op jit(solution)/shard_map/ppermute | solution.py:20
  217.6 25.0 %collective-permute-start.5 = (f32[64,2048]{1,0:T(8,128)S(1)}, f32[64,2048]{1,0:T(8,128)S(1)}, u32[]{:S(2)}, u32[]{:S(2)}) collective-permute-start(f32[64,2048]{1,0:T(8,128)S(1)} %add_select_fusion.10), channel_id=1, source_target_pairs={{8,0},{10,2},{12,4},{14,6},{16,8},{18,10},{20,12},{22,14},{24,16},... | collective-permute-start | bytes 1572872 | tf_op jit(solution)/shard_map/ppermute | solution.py:20
  247.4 8.0 %collective-permute-done.5 = f32[64,2048]{1,0:T(8,128)S(1)} collective-permute-done((f32[64,2048]{1,0:T(8,128)S(1)}, f32[64,2048]{1,0:T(8,128)S(1)}, u32[]{:S(2)}, u32[]{:S(2)}) %collective-permute-start.5) | collective-permute-done | bytes 524320 | tf_op jit(solution)/shard_map/ppermute | solution.py:20
  256.2 5.4 %collective-permute-start.7 = (f32[64,2048]{1,0:T(8,128)}, f32[64,2048]{1,0:T(8,128)}, u32[]{:S(2)}, u32[]{:S(2)}) collective-permute-start(f32[64,2048]{1,0:T(8,128)} %add_select_fusion.9), channel_id=1, source_target_pairs={{16,0},{18,2},{20,4},{22,6},{24,8},{26,10},{28,12},{30,14},{32,16}... | collective-permute-start | bytes 1572872 | tf_op jit(solution)/shard_map/ppermute | solution.py:20
  263.9 5.9 %collective-permute-done.18 = f32[64,2048]{1,0:T(8,128)} collective-permute-done((f32[64,2048]{1,0:T(8,128)}, f32[64,2048]{1,0:T(8,128)}, u32[]{:S(2)}, u32[]{:S(2)}) %collective-permute-start.18) | collective-permute-done | bytes 524320 | tf_op jit(solution)/shard_map/ppermute | solution.py:20
  273.0 6.9 %collective-permute-done.7 = f32[64,2048]{1,0:T(8,128)} collective-permute-done((f32[64,2048]{1,0:T(8,128)}, f32[64,2048]{1,0:T(8,128)}, u32[]{:S(2)}, u32[]{:S(2)}) %collective-permute-start.7) | collective-permute-done | bytes 524320 | tf_op jit(solution)/shard_map/ppermute | solution.py:20
  283.1 12.4 %collective-permute-done.20 = f32[64,2048]{1,0:T(8,128)S(1)} collective-permute-done((f32[64,2048]{1,0:T(8,128)S(1)}, f32[64,2048]{1,0:T(8,128)S(1)}, u32[]{:S(2)}, u32[]{:S(2)}) %collective-permute-start.20) | collective-permute-done | bytes 524320 | tf_op jit(solution)/shard_map/ppermute | solution.py:20
  301.5 8.6 %collective-permute-done.22 = f32[64,2048]{1,0:T(8,128)} collective-permute-done((f32[64,2048]{1,0:T(8,128)}, f32[64,2048]{1,0:T(8,128)}, u32[]{:S(2)}, u32[]{:S(2)}) %collective-permute-start.22) | collective-permute-done | bytes 524320 | tf_op jit(solution)/shard_map/ppermute | solution.py:20
  318.1 3.2 convolution_bitcast_fusion.4
  328.0 3.2 convolution_bitcast_fusion.3
  331.6 2.7 convolution_bitcast_fusion
  334.3 5.6 %copy.45 = f32[4096,256]{1,0:T(8,128)} copy(f32[4096,256]{0,1:T(8,128)} %convolution_bitcast_fusion) | data formatting | bytes 8388608 | tf_op jit(solution)/shard_map/td,tc->dc/dot_general | solution.py:215
  339.9 11.0 %all-to-all-start = ((f32[128,32,256]{2,1,0:T(8,128)}), f32[128,32,256]{2,1,0:T(8,128)}, u32[]{:S(2)}, u32[]{:S(2)}) async-start(f32[128,32,256]{2,1,0:T(8,128)} %bitcast.132), calls=%async_computation.1 | async-start | bytes 8388608 | tf_op jit(solution)/shard_map/all_to_all | solution.py:217
  350.9 3.4 convolution_convert_fusion
  366.1 68.4 %all-to-all-done = f32[128,32,256]{2,1,0:T(8,128)} async-done(((f32[128,32,256]{2,1,0:T(8,128)}), f32[128,32,256]{2,1,0:T(8,128)}, u32[]{:S(2)}, u32[]{:S(2)}) %all-to-all-start) | async-done | bytes 4194336 | tf_op jit(solution)/shard_map/all_to_all | solution.py:217
  (154 shorter events, 103.4 us)
Async XLA Ops:
  7.2 122.7 %all-gather.2.cloned.1.call-start = ((), (), s32[]{:S(2)}) async-start(), calls=%async_computation.2 | async-start | bytes 2113536 | tf_op jit(solution)/shard_map/all_gather | solution.py:138
  9.9 20.5 %collective-permute-start.2 = (f32[32]{0:T(128)S(1)}, f32[32]{0:T(128)S(1)}, u32[]{:S(2)}, u32[]{:S(2)}) collective-permute-start(f32[32]{0:T(128)S(1)} %get-tuple-element.21), channel_id=1, source_target_pairs={{2,0},{4,2},{6,4},{8,6},{10,8},{12,10},{14,12},{16,14},{18,16},{20... | collective-permute-start | bytes 392 | tf_op jit(solution)/shard_map/ppermute | solution.py:20
  20.1 18.5 %collective-permute-start.15 = (f32[32]{0:T(128)S(1)}, f32[32]{0:T(128)S(1)}, u32[]{:S(2)}, u32[]{:S(2)}) collective-permute-start(f32[32]{0:T(128)S(1)} %get-tuple-element.21), channel_id=1, source_target_pairs={{0,2},{2,4},{4,6},{6,8},{8,10},{10,12},{12,14},{14,16},{16,18},{18... | collective-permute-start | bytes 392 | tf_op jit(solution)/shard_map/ppermute | solution.py:20
  38.6 110.2 %collective-permute-start.17 = (f32[32]{0:T(128)S(1)}, f32[32]{0:T(128)S(1)}, u32[]{:S(2)}, u32[]{:S(2)}) collective-permute-start(f32[32]{0:T(128)S(1)} %broadcast_select_fusion.7), channel_id=1, source_target_pairs={{0,2},{2,4},{4,6},{6,8},{8,10},{10,12},{12,14},{14,16},{16,18},{18... | collective-permute-start | bytes 392 | tf_op jit(solution)/shard_map/ppermute | solution.py:20
  40.8 110.2 %collective-permute-start.6 = (f32[32]{0:T(128)S(1)}, f32[32]{0:T(128)S(1)}, u32[]{:S(2)}, u32[]{:S(2)}) collective-permute-start(f32[32]{0:T(128)S(1)} %broadcast_select_fusion.12), channel_id=1, source_target_pairs={{4,0},{6,2},{8,4},{10,6},{12,8},{14,10},{16,12},{18,14},{20,16},{2... | collective-permute-start | bytes 392 | tf_op jit(solution)/shard_map/ppermute | solution.py:20
  144.3 19.9 %collective-permute-start = (f32[64,2048]{1,0:T(8,128)}, f32[64,2048]{1,0:T(8,128)}, u32[]{:S(2)}, u32[]{:S(2)}) collective-permute-start(f32[64,2048]{1,0:T(8,128)} %get-tuple-element.19), channel_id=1, source_target_pairs={{2,0},{4,2},{6,4},{8,6},{10,8},{12,10},{14,12},{16,14},{18,16},{20... | collective-permute-start | bytes 1572872 | tf_op jit(solution)/shard_map/ppermute | solution.py:20
  151.0 23.2 %collective-permute-start.8 = (f32[32]{0:T(128)S(1)}, f32[32]{0:T(128)S(1)}, u32[]{:S(2)}, u32[]{:S(2)}) collective-permute-start(f32[32]{0:T(128)S(1)} %broadcast_select_fusion.11), channel_id=1, source_target_pairs={{8,0},{10,2},{12,4},{14,6},{16,8},{18,10},{20,12},{22,14},{24,16},... | collective-permute-start | bytes 392 | tf_op jit(solution)/shard_map/ppermute | solution.py:20
  159.4 37.1 %collective-permute-start.21 = (f32[32]{0:T(128)S(1)}, f32[32]{0:T(128)S(1)}, u32[]{:S(2)}, u32[]{:S(2)}) collective-permute-start(f32[32]{0:T(128)S(1)} %broadcast_select_fusion.5), channel_id=1, source_target_pairs={{0,8},{2,10},{4,12},{6,14},{8,16},{10,18},{12,20},{14,22},{16,24},... | collective-permute-start | bytes 392 | tf_op jit(solution)/shard_map/ppermute | solution.py:20
  161.6 16.9 %collective-permute-start.13 = (f32[64,2048]{1,0:T(8,128)}, f32[64,2048]{1,0:T(8,128)S(1)}, u32[]{:S(2)}, u32[]{:S(2)}) collective-permute-start(f32[64,2048]{1,0:T(8,128)} %get-tuple-element.20), channel_id=1, source_target_pairs={{0,2},{2,4},{4,6},{6,8},{8,10},{10,12},{12,14},{14,16},{16,18},{18... | collective-permute-start | bytes 1572872 | tf_op jit(solution)/shard_map/ppermute | solution.py:20
  165.3 16.8 %collective-permute-start.1 = (f32[64,2048]{1,0:T(8,128)S(1)}, f32[64,2048]{1,0:T(8,128)S(1)}, u32[]{:S(2)}, u32[]{:S(2)}) collective-permute-start(f32[64,2048]{1,0:T(8,128)S(1)} %broadcast_select_fusion.1), channel_id=1, source_target_pairs={{2,0},{4,2},{6,4},{8,6},{10,8},{12,10},{14,12},{16,14},{18,16},{20... | collective-permute-start | bytes 1572872 | tf_op jit(solution)/shard_map/ppermute | solution.py:20
  174.2 68.4 %collective-permute-start.10 = (f32[32]{0:T(128)S(1)}, f32[32]{0:T(128)S(1)}, u32[]{:S(2)}, u32[]{:S(2)}) collective-permute-start(f32[32]{0:T(128)S(1)} %broadcast_select_fusion.10), channel_id=1, source_target_pairs={{16,0},{18,2},{20,4},{22,6},{24,8},{26,10},{28,12},{30,14},{32,16}... | collective-permute-start | bytes 392 | tf_op jit(solution)/shard_map/ppermute | solution.py:20
  180.1 18.5 %collective-permute-start.14 = (f32[64,2048]{1,0:T(8,128)}, f32[64,2048]{1,0:T(8,128)}, u32[]{:S(2)}, u32[]{:S(2)}) collective-permute-start(f32[64,2048]{1,0:T(8,128)} %broadcast_select_fusion), channel_id=1, source_target_pairs={{0,2},{2,4},{4,6},{6,8},{8,10},{10,12},{12,14},{14,16},{16,18},{18... | collective-permute-start | bytes 1572872 | tf_op jit(solution)/shard_map/ppermute | solution.py:20
  184.0 32.3 %collective-permute-start.3 = (f32[64,2048]{1,0:T(8,128)}, f32[64,2048]{1,0:T(8,128)}, u32[]{:S(2)}, u32[]{:S(2)}) collective-permute-start(f32[64,2048]{1,0:T(8,128)} %add_select_fusion.11), channel_id=1, source_target_pairs={{4,0},{6,2},{8,4},{10,6},{12,8},{14,10},{16,12},{18,14},{20,16},{2... | collective-permute-start | bytes 1572872 | tf_op jit(solution)/shard_map/ppermute | solution.py:20
  196.4 65.2 %collective-permute-start.23 = (f32[32]{0:T(128)S(1)}, f32[32]{0:T(128)S(1)}, u32[]{:S(2)}, u32[]{:S(2)}) collective-permute-start(f32[32]{0:T(128)S(1)} %broadcast_select_fusion.4), channel_id=1, source_target_pairs={{0,16},{2,18},{4,20},{6,22},{8,24},{10,26},{12,28},{14,30},{16,32}... | collective-permute-start | bytes 392 | tf_op jit(solution)/shard_map/ppermute | solution.py:20
  199.9 44.6 %collective-permute-start.16 = (f32[64,2048]{1,0:T(8,128)S(1)}, f32[64,2048]{1,0:T(8,128)S(1)}, u32[]{:S(2)}, u32[]{:S(2)}) collective-permute-start(f32[64,2048]{1,0:T(8,128)S(1)} %add_select_fusion.5), channel_id=1, source_target_pairs={{0,4},{2,6},{4,8},{6,10},{8,12},{10,14},{12,16},{14,18},{16,20},{1... | collective-permute-start | bytes 1572872 | tf_op jit(solution)/shard_map/ppermute | solution.py:20
  217.6 37.8 %collective-permute-start.5 = (f32[64,2048]{1,0:T(8,128)S(1)}, f32[64,2048]{1,0:T(8,128)S(1)}, u32[]{:S(2)}, u32[]{:S(2)}) collective-permute-start(f32[64,2048]{1,0:T(8,128)S(1)} %add_select_fusion.10), channel_id=1, source_target_pairs={{8,0},{10,2},{12,4},{14,6},{16,8},{18,10},{20,12},{22,14},{24,16},... | collective-permute-start | bytes 1572872 | tf_op jit(solution)/shard_map/ppermute | solution.py:20
  242.6 40.5 %collective-permute-start.12 = (f32[32]{0:T(128)S(1)}, f32[32]{0:T(128)S(1)}, u32[]{:S(2)}, u32[]{:S(2)}) collective-permute-start(f32[32]{0:T(128)S(1)} %broadcast_select_fusion.9), channel_id=1, source_target_pairs={{32,0},{34,2},{36,4},{38,6},{40,8},{42,10},{44,12},{46,14},{48,16}... | collective-permute-start | bytes 392 | tf_op jit(solution)/shard_map/ppermute | solution.py:20
  245.4 24.4 %collective-permute-start.18 = (f32[64,2048]{1,0:T(8,128)}, f32[64,2048]{1,0:T(8,128)}, u32[]{:S(2)}, u32[]{:S(2)}) collective-permute-start(f32[64,2048]{1,0:T(8,128)} %add_select_fusion.4), channel_id=1, source_target_pairs={{0,8},{2,10},{4,12},{6,14},{8,16},{10,18},{12,20},{14,22},{16,24},... | collective-permute-start | bytes 1572872 | tf_op jit(solution)/shard_map/ppermute | solution.py:20
  256.2 23.7 %collective-permute-start.7 = (f32[64,2048]{1,0:T(8,128)}, f32[64,2048]{1,0:T(8,128)}, u32[]{:S(2)}, u32[]{:S(2)}) collective-permute-start(f32[64,2048]{1,0:T(8,128)} %add_select_fusion.9), channel_id=1, source_target_pairs={{16,0},{18,2},{20,4},{22,6},{24,8},{26,10},{28,12},{30,14},{32,16}... | collective-permute-start | bytes 1572872 | tf_op jit(solution)/shard_map/ppermute | solution.py:20
  261.7 39.6 %collective-permute-start.25 = (f32[32]{0:T(128)S(1)}, f32[32]{0:T(128)S(1)}, u32[]{:S(2)}, u32[]{:S(2)}) collective-permute-start(f32[32]{0:T(128)S(1)} %broadcast_select_fusion.3), channel_id=1, source_target_pairs={{0,32},{2,34},{4,36},{6,38},{8,40},{10,42},{12,44},{14,46},{16,48}... | collective-permute-start | bytes 392 | tf_op jit(solution)/shard_map/ppermute | solution.py:20
  271.1 24.4 %collective-permute-start.20 = (f32[64,2048]{1,0:T(8,128)S(1)}, f32[64,2048]{1,0:T(8,128)S(1)}, u32[]{:S(2)}, u32[]{:S(2)}) collective-permute-start(f32[64,2048]{1,0:T(8,128)S(1)} %add_select_fusion.3), channel_id=1, source_target_pairs={{0,16},{2,18},{4,20},{6,22},{8,24},{10,26},{12,28},{14,30},{16,32}... | collective-permute-start | bytes 1572872 | tf_op jit(solution)/shard_map/ppermute | solution.py:20
  281.2 17.1 %collective-permute-start.9 = (f32[64,2048]{1,0:T(8,128)S(1)}, f32[64,2048]{1,0:T(8,128)S(1)}, u32[]{:S(2)}, u32[]{:S(2)}) collective-permute-start(f32[64,2048]{1,0:T(8,128)S(1)} %add_select_fusion.8), channel_id=1, source_target_pairs={{32,0},{34,2},{36,4},{38,6},{40,8},{42,10},{44,12},{46,14},{48,16}... | collective-permute-start | bytes 1572872 | tf_op jit(solution)/shard_map/ppermute | solution.py:20
  339.9 94.6 %all-to-all-start = ((f32[128,32,256]{2,1,0:T(8,128)}), f32[128,32,256]{2,1,0:T(8,128)}, u32[]{:S(2)}, u32[]{:S(2)}) async-start(f32[128,32,256]{2,1,0:T(8,128)} %bitcast.132), calls=%async_computation.1 | async-start | bytes 8388608 | tf_op jit(solution)/shard_map/all_to_all | solution.py:217
  350.9 86.7 %reduce-scatter.2.cloned.1.call-start = ((), (), s32[]{:S(2)}) async-start(), calls=%async_computation.3 | async-start | bytes 1572864 | tf_op jit(solution)/shard_map/reduce_scatter | solution.py:211
  (16 other events, 214.4 us)
Sparse Core Ops, SparseCore 0:
  12.2 117.6 all-gather.1
  354.8 14.5 reduce-scatter.1

commit v2 on v1

--- a/solution.py
+++ b/solution.py
@@ -10,7 +10,6 @@
 
 def carried_in(part, axis, combine, identity, reverse):
     count = lax.axis_size(axis)
-    place = lax.axis_index(axis)
 
     def shifted(tree, offset):
         if reverse:
@@ -19,19 +18,14 @@
             pairs = [(i, i + offset) for i in range(count - offset)]
         return jax.tree.map(lambda a: lax.ppermute(a, axis, pairs), tree)
 
-    ahead = count - 1 - place if reverse else place
-    state = jax.tree.map(
-        lambda a, e: jnp.where(ahead >= 1, a, jnp.asarray(e, a.dtype)),
-        shifted(part, 1),
-        identity,
-    )
+    window = jax.tree.map(lambda a, e: jnp.zeros_like(a) + jnp.asarray(e, a.dtype), part, identity)
+    whole = part
     offset = 1
     while offset < count:
-        earlier = shifted(state, offset)
-        merged = combine(earlier, state)
-        state = jax.tree.map(lambda m, s: jnp.where(ahead >= offset, m, s), merged, state)
+        window = combine(shifted(whole, offset), window)
+        whole = combine(window, part)
         offset *= 2
-    return state
+    return window
 
 
 def span_summary(b_vals, c_vals, x_vals, dy_round, rate_vals):
@@ -135,7 +129,14 @@
     tok_rows = tokens.shape[0]
     weight_local = proj_weight.reshape(proj_weight.shape[0], -1)
     col_count = weight_local.shape[1]
-    weight_full = lax.all_gather(weight_local, ("dp", "ctx"), axis=0, tiled=True)
+    shard_count = lax.axis_size(("dp", "ctx"))
+    weight_full = lax.all_to_all(
+        jnp.broadcast_to(weight_local[None], (shard_count,) + weight_local.shape),
+        ("dp", "ctx"),
+        0,
+        0,
+        tiled=True,
+    ).reshape(-1, col_count)
     bc_sums = jnp.dot(tokens, weight_full, preferred_element_type=jnp.float32)
     group_count = col_count // (2 * STATE)
     head_count = values_in.shape[2] // HEAD_DIM
@@ -213,7 +214,6 @@
     )[None]
     scale = 1.0 / (lax.axis_size("dp") * lax.axis_size("ctx") * tok_rows)
     proj_terms = jnp.einsum("td,tc->dc", tokens, grad_flat, preferred_element_type=jnp.float32)
-    shard_count = lax.axis_size(("dp", "ctx"))
     proj_parts = lax.all_to_all(
         proj_terms.reshape(shard_count, -1, col_count),
         ("dp", "ctx"),

time: 448 us -> 468 us (1.045)
  waiting for transfers between devices: 217 us -> 257 us
  starting transfers between devices: 128 us -> 103 us
  other arithmetic: 28.1 us -> 34.3 us
    all_gather x1 -> x0, waiting for transfers between devices: 85.7 us -> none  [body(): lax.all_gather(weight_local, ('dp', 'ctx'), axis=0, tiled=True)]
    ppermute x26 -> x22, waiting for transfers between devices: 63 us -> 140 us  [shifted(): return jax.tree.map(lambda a: lax.ppermute(a, axis, pairs), tree)]
    all_to_all x0 -> x1, waiting for transfers between devices: none -> 38.5 us  [body(): lax.all_to_all(jnp.broadcast_to(weight_local[None], (shard_count,) + weig...]
    ppermute x26 -> x22, starting transfers between devices: 117 us -> 80.8 us  [shifted(): return jax.tree.map(lambda a: lax.ppermute(a, axis, pairs), tree)]
    add x0 -> x11, other arithmetic: none -> 20.3 us  [chain(): earlier[1] * jnp.repeat(later[0], HEAD_DIM)[None, :] + later[1]]
    select_n x26 -> x0, other arithmetic: 18.6 us -> none  [the longest x22 16.7 us: carried_in(): jnp.where(ahead >= offset, m, s)]
    all_to_all x0 -> x1, starting transfers between devices: none -> 15.7 us  [body(): lax.all_to_all(jnp.broadcast_to(weight_local[None], (shard_count,) + weig...]
    all_to_all x1, waiting for transfers between devices: 68.4 us -> 78.6 us  [body(): lax.all_to_all(proj_terms.reshape(shard_count, -1, col_count), ('dp', 'ct...]
  transfers between devices with their start and end apart: 29 -> 25, of which waited for: 11 -> 17; matrix products, arithmetic and copies ran while one was open for 15% -> 10% of each run, Pallas kernels for 0% -> 0%
where the time goes in v2:
time: 468 us; the launch traced here: 465 us
  waiting for transfers between devices  257 us (55%)
  starting transfers between devices  103 us (22%)
  other arithmetic  34.3 us (7%)
  local copies, waits for them, and re-layouts  31.7 us (7%)
  matrix products  23.9 us (5%)
  between operations  14.5 us (3%)
    ppermute x22, waiting for transfers between devices, shifted(): return jax.tree.map(lambda a: lax.ppermute(a, axis, pairs), tree)  140 us
    ppermute x22, starting transfers between devices, shifted(): return jax.tree.map(lambda a: lax.ppermute(a, axis, pairs), tree)  80.8 us
    all_to_all x1, waiting for transfers between devices, body(): lax.all_to_all(proj_terms.reshape(shard_count, -1, col_count), ('dp', 'ct...  78.6 us
    all_to_all x1, waiting for transfers between devices, body(): lax.all_to_all(jnp.broadcast_to(weight_local[None], (shard_count,) + weig...  38.5 us
    add x11, other arithmetic, chain(): earlier[1] * jnp.repeat(later[0], HEAD_DIM)[None, :] + later[1]  20.3 us
    all_to_all x1, starting transfers between devices, body(): lax.all_to_all(jnp.broadcast_to(weight_local[None], (shard_count,) + weig...  15.7 us
    unnamed x46, local copies, waits for them, and re-layouts  12.6 us
  transfers between devices with their start and end apart: 25, of which 17 were waited for; matrix products, arithmetic and copies ran while one was open for 10% of the time, Pallas kernels for 0%

profile of v2, /device:TPU:24, one launch (start us, length us, event | category | flops | bytes accessed | tf_op | source)
XLA Modules:
  0.0 465.3 jit_solution(9742367935441680265)
XLA Ops:
  9.6 15.7 %all-to-all-start = ((bf16[128,32,256]{2,1,0:T(8,128)(2,1)}), bf16[128,32,256]{2,1,0:T(8,128)(2,1)S(1)}, u32[]{:S(2)}, u32[]{:S(2)}) async-start(bf16[128,32,256]{2,1,0:T(8,128)(2,1)} %broadcast_in_dim.90), calls=%async_computation | async-start | bytes 4194304 | tf_op jit(solution)/shard_map/all_to_all | solution.py:133
  38.9 38.5 %all-to-all-done = bf16[128,32,256]{2,1,0:T(8,128)(2,1)S(1)} async-done(((bf16[128,32,256]{2,1,0:T(8,128)(2,1)}), bf16[128,32,256]{2,1,0:T(8,128)(2,1)S(1)}, u32[]{:S(2)}, u32[]{:S(2)}) %all-to-all-start) | async-done | bytes 2097184 | tf_op jit(solution)/shard_map/all_to_all | solution.py:133
  92.2 11.6 %collective-permute-done = f32[64,2048]{1,0:T(8,128)S(1)} collective-permute-done((f32[64,2048]{1,0:T(8,128)S(1)}, f32[64,2048]{1,0:T(8,128)S(1)}, u32[]{:S(2)}, u32[]{:S(2)}) %collective-permute-start) | collective-permute-done | bytes 524320 | tf_op jit(solution)/shard_map/ppermute | solution.py:19
  108.4 4.7 %collective-permute-start.2 = (f32[32]{0:T(128)S(1)}, f32[32]{0:T(128)S(1)}, u32[]{:S(2)}, u32[]{:S(2)}) collective-permute-start(f32[32]{0:T(128)S(1)} %exp.35), channel_id=1, source_target_pairs={{2,0},{4,2},{6,4},{8,6},{10,8},{12,10},{14,12},{16,14},{18,16},{20... | collective-permute-start | bytes 392 | tf_op jit(solution)/shard_map/ppermute | solution.py:19
  113.1 17.1 %collective-permute-done.2 = f32[32]{0:T(128)S(1)} collective-permute-done((f32[32]{0:T(128)S(1)}, f32[32]{0:T(128)S(1)}, u32[]{:S(2)}, u32[]{:S(2)}) %collective-permute-start.2) | collective-permute-done | bytes 160 | tf_op jit(solution)/shard_map/ppermute | solution.py:19
  132.6 4.2 collective-permute-start.3
  136.9 6.5 %collective-permute-start.4 = (f32[32]{0:T(128)S(1)}, f32[32]{0:T(128)S(1)}, u32[]{:S(2)}, u32[]{:S(2)}) collective-permute-start(f32[32]{0:T(128)S(1)} %exponential_multiply_fusion.7), channel_id=1, source_target_pairs={{4,0},{6,2},{8,4},{10,6},{12,8},{14,10},{16,12},{18,14},{20,16},{2... | collective-permute-start | bytes 392 | tf_op jit(solution)/shard_map/ppermute | solution.py:19
  147.4 4.1 collective-permute-done.3
  154.2 13.6 %collective-permute-start.5 = (f32[64,2048]{1,0:T(8,128)}, f32[64,2048]{1,0:T(8,128)}, u32[]{:S(2)}, u32[]{:S(2)}) collective-permute-start(f32[64,2048]{1,0:T(8,128)} %get-tuple-element.24), channel_id=1, source_target_pairs={{16,0},{18,2},{20,4},{22,6},{24,8},{26,10},{28,12},{30,14},{32,16}... | collective-permute-start | bytes 1572872 | tf_op jit(solution)/shard_map/ppermute | solution.py:19
  167.9 6.9 %collective-permute-start.6 = (f32[32]{0:T(128)S(1)}, f32[32]{0:T(128)S(1)}, u32[]{:S(2)}, u32[]{:S(2)}) collective-permute-start(f32[32]{0:T(128)S(1)} %get-tuple-element.22), channel_id=1, source_target_pairs={{8,0},{10,2},{12,4},{14,6},{16,8},{18,10},{20,12},{22,14},{24,16},... | collective-permute-start | bytes 392 | tf_op jit(solution)/shard_map/ppermute | solution.py:19
  189.5 4.4 collective-permute-start.8
  193.9 9.2 %collective-permute-done.13 = f32[32]{0:T(128)S(1)} collective-permute-done((f32[32]{0:T(128)S(1)}, f32[32]{0:T(128)S(1)}, u32[]{:S(2)}, u32[]{:S(2)}) %collective-permute-start.13) | collective-permute-done | bytes 160 | tf_op jit(solution)/shard_map/ppermute | solution.py:19
  203.3 4.9 %collective-permute-done.7 = f32[64,2048]{1,0:T(8,128)} collective-permute-done((f32[64,2048]{1,0:T(8,128)}, f32[64,2048]{1,0:T(8,128)}, u32[]{:S(2)}, u32[]{:S(2)}) %collective-permute-start.7) | collective-permute-done | bytes 524320 | tf_op jit(solution)/shard_map/ppermute | solution.py:19
  213.4 6.8 %collective-permute-start.10 = (f32[32]{0:T(128)S(1)}, f32[32]{0:T(128)S(1)}, u32[]{:S(2)}, u32[]{:S(2)}) collective-permute-start(f32[32]{0:T(128)S(1)} %get-tuple-element.16), channel_id=1, source_target_pairs={{32,0},{34,2},{36,4},{38,6},{40,8},{42,10},{44,12},{46,14},{48,16}... | collective-permute-start | bytes 392 | tf_op jit(solution)/shard_map/ppermute | solution.py:19
  222.2 18.6 %collective-permute-done.12 = f32[64,2048]{1,0:T(8,128)} collective-permute-done((f32[64,2048]{1,0:T(8,128)}, f32[64,2048]{1,0:T(8,128)}, u32[]{:S(2)}, u32[]{:S(2)}) %collective-permute-start.12) | collective-permute-done | bytes 524320 | tf_op jit(solution)/shard_map/ppermute | solution.py:19
  247.2 29.6 %collective-permute-done.17 = f32[32]{0:T(128)S(1)} collective-permute-done((f32[32]{0:T(128)S(1)}, f32[32]{0:T(128)S(1)}, u32[]{:S(2)}, u32[]{:S(2)}) %collective-permute-start.17) | collective-permute-done | bytes 160 | tf_op jit(solution)/shard_map/ppermute | solution.py:19
  278.9 5.5 %collective-permute-done.19 = f32[32]{0:T(128)S(1)} collective-permute-done((f32[32]{0:T(128)S(1)}, f32[32]{0:T(128)S(1)}, u32[]{:S(2)}, u32[]{:S(2)}) %collective-permute-start.19) | collective-permute-done | bytes 160 | tf_op jit(solution)/shard_map/ppermute | solution.py:19
  286.5 5.8 %collective-permute-done.21 = f32[32]{0:T(128)S(1)} collective-permute-done((f32[32]{0:T(128)S(1)}, f32[32]{0:T(128)S(1)}, u32[]{:S(2)}, u32[]{:S(2)}) %collective-permute-start.21) | collective-permute-done | bytes 160 | tf_op jit(solution)/shard_map/ppermute | solution.py:19
  298.5 5.0 %collective-permute-done.9 = f32[64,2048]{1,0:T(8,128)S(1)} collective-permute-done((f32[64,2048]{1,0:T(8,128)}, f32[64,2048]{1,0:T(8,128)S(1)}, u32[]{:S(2)}, u32[]{:S(2)}) %collective-permute-start.9) | collective-permute-done | bytes 524320 | tf_op jit(solution)/shard_map/ppermute | solution.py:19
  318.1 10.6 %collective-permute-done.18 = f32[64,2048]{1,0:T(8,128)S(1)} collective-permute-done((f32[64,2048]{1,0:T(8,128)S(1)}, f32[64,2048]{1,0:T(8,128)S(1)}, u32[]{:S(2)}, u32[]{:S(2)}) %collective-permute-start.18) | collective-permute-done | bytes 524320 | tf_op jit(solution)/shard_map/ppermute | solution.py:19
  333.5 8.1 %collective-permute-done.20 = f32[64,2048]{1,0:T(8,128)S(1)} collective-permute-done((f32[64,2048]{1,0:T(8,128)S(1)}, f32[64,2048]{1,0:T(8,128)S(1)}, u32[]{:S(2)}, u32[]{:S(2)}) %collective-permute-start.20) | collective-permute-done | bytes 524320 | tf_op jit(solution)/shard_map/ppermute | solution.py:19
  350.8 5.6 %copy.45 = f32[4096,256]{1,0:T(8,128)} copy(f32[4096,256]{0,1:T(8,128)} %convolution_bitcast_fusion) | data formatting | bytes 8388608 | tf_op jit(solution)/shard_map/td,tc->dc/dot_general | solution.py:216
  356.4 6.8 %all-to-all-start.1 = ((f32[128,32,256]{2,1,0:T(8,128)}), f32[128,32,256]{2,1,0:T(8,128)}, u32[]{:S(2)}, u32[]{:S(2)}) async-start(f32[128,32,256]{2,1,0:T(8,128)} %bitcast.147), calls=%async_computation.2 | async-start | bytes 8388608 | tf_op jit(solution)/shard_map/all_to_all | solution.py:217
  376.7 78.6 %all-to-all-done.1 = f32[128,32,256]{2,1,0:T(8,128)} async-done(((f32[128,32,256]{2,1,0:T(8,128)}), f32[128,32,256]{2,1,0:T(8,128)}, u32[]{:S(2)}, u32[]{:S(2)}) %all-to-all-start.1) | async-done | bytes 4194336 | tf_op jit(solution)/shard_map/all_to_all | solution.py:217
  (154 shorter events, 128.3 us)
Async XLA Ops:
  9.6 67.8 %all-to-all-start = ((bf16[128,32,256]{2,1,0:T(8,128)(2,1)}), bf16[128,32,256]{2,1,0:T(8,128)(2,1)S(1)}, u32[]{:S(2)}, u32[]{:S(2)}) async-start(bf16[128,32,256]{2,1,0:T(8,128)(2,1)} %broadcast_in_dim.90), calls=%async_computation | async-start | bytes 4194304 | tf_op jit(solution)/shard_map/all_to_all | solution.py:133
  90.1 13.7 %collective-permute-start = (f32[64,2048]{1,0:T(8,128)S(1)}, f32[64,2048]{1,0:T(8,128)S(1)}, u32[]{:S(2)}, u32[]{:S(2)}) collective-permute-start(f32[64,2048]{1,0:T(8,128)S(1)} %get-tuple-element.40), channel_id=1, source_target_pairs={{2,0},{4,2},{6,4},{8,6},{10,8},{12,10},{14,12},{16,14},{18,16},{20... | collective-permute-start | bytes 1572872 | tf_op jit(solution)/shard_map/ppermute | solution.py:19
  104.8 25.6 %collective-permute-start.1 = (f32[64,2048]{1,0:T(8,128)}, f32[64,2048]{1,0:T(8,128)}, u32[]{:S(2)}, u32[]{:S(2)}) collective-permute-start(f32[64,2048]{1,0:T(8,128)} %multiply_add_fusion.19), channel_id=1, source_target_pairs={{4,0},{6,2},{8,4},{10,6},{12,8},{14,10},{16,12},{18,14},{20,16},{2... | collective-permute-start | bytes 1572872 | tf_op jit(solution)/shard_map/ppermute | solution.py:19
  108.4 21.8 %collective-permute-start.2 = (f32[32]{0:T(128)S(1)}, f32[32]{0:T(128)S(1)}, u32[]{:S(2)}, u32[]{:S(2)}) collective-permute-start(f32[32]{0:T(128)S(1)} %exp.35), channel_id=1, source_target_pairs={{2,0},{4,2},{6,4},{8,6},{10,8},{12,10},{14,12},{16,14},{18,16},{20... | collective-permute-start | bytes 392 | tf_op jit(solution)/shard_map/ppermute | solution.py:19
  132.6 18.9 %collective-permute-start.3 = (f32[64,2048]{1,0:T(8,128)}, f32[64,2048]{1,0:T(8,128)}, u32[]{:S(2)}, u32[]{:S(2)}) collective-permute-start(f32[64,2048]{1,0:T(8,128)} %multiply_add_fusion.17), channel_id=1, source_target_pairs={{8,0},{10,2},{12,4},{14,6},{16,8},{18,10},{20,12},{22,14},{24,16},... | collective-permute-start | bytes 1572872 | tf_op jit(solution)/shard_map/ppermute | solution.py:19
  136.9 10.4 %collective-permute-start.4 = (f32[32]{0:T(128)S(1)}, f32[32]{0:T(128)S(1)}, u32[]{:S(2)}, u32[]{:S(2)}) collective-permute-start(f32[32]{0:T(128)S(1)} %exponential_multiply_fusion.7), channel_id=1, source_target_pairs={{4,0},{6,2},{8,4},{10,6},{12,8},{14,10},{16,12},{18,14},{20,16},{2... | collective-permute-start | bytes 392 | tf_op jit(solution)/shard_map/ppermute | solution.py:19
  154.2 27.3 %collective-permute-start.5 = (f32[64,2048]{1,0:T(8,128)}, f32[64,2048]{1,0:T(8,128)}, u32[]{:S(2)}, u32[]{:S(2)}) collective-permute-start(f32[64,2048]{1,0:T(8,128)} %get-tuple-element.24), channel_id=1, source_target_pairs={{16,0},{18,2},{20,4},{22,6},{24,8},{26,10},{28,12},{30,14},{32,16}... | collective-permute-start | bytes 1572872 | tf_op jit(solution)/shard_map/ppermute | solution.py:19
  167.9 9.4 %collective-permute-start.6 = (f32[32]{0:T(128)S(1)}, f32[32]{0:T(128)S(1)}, u32[]{:S(2)}, u32[]{:S(2)}) collective-permute-start(f32[32]{0:T(128)S(1)} %get-tuple-element.22), channel_id=1, source_target_pairs={{8,0},{10,2},{12,4},{14,6},{16,8},{18,10},{20,12},{22,14},{24,16},... | collective-permute-start | bytes 392 | tf_op jit(solution)/shard_map/ppermute | solution.py:19
  177.4 25.9 %collective-permute-start.11 = (f32[64,2048]{1,0:T(8,128)}, f32[64,2048]{1,0:T(8,128)}, u32[]{:S(2)}, u32[]{:S(2)}) collective-permute-start(f32[64,2048]{1,0:T(8,128)} %get-tuple-element.41), channel_id=1, source_target_pairs={{0,2},{2,4},{4,6},{6,8},{8,10},{10,12},{12,14},{14,16},{16,18},{18... | collective-permute-start | bytes 1572872 | tf_op jit(solution)/shard_map/ppermute | solution.py:19
  183.7 24.5 %collective-permute-start.7 = (f32[64,2048]{1,0:T(8,128)}, f32[64,2048]{1,0:T(8,128)}, u32[]{:S(2)}, u32[]{:S(2)}) collective-permute-start(f32[64,2048]{1,0:T(8,128)} %multiply_add_fusion.13), channel_id=1, source_target_pairs={{32,0},{34,2},{36,4},{38,6},{40,8},{42,10},{44,12},{46,14},{48,16}... | collective-permute-start | bytes 1572872 | tf_op jit(solution)/shard_map/ppermute | solution.py:19
  185.9 17.2 %collective-permute-start.13 = (f32[32]{0:T(128)S(1)}, f32[32]{0:T(128)S(1)}, u32[]{:S(2)}, u32[]{:S(2)}) collective-permute-start(f32[32]{0:T(128)S(1)} %exp.35), channel_id=1, source_target_pairs={{0,2},{2,4},{4,6},{6,8},{8,10},{10,12},{12,14},{14,16},{16,18},{18... | collective-permute-start | bytes 392 | tf_op jit(solution)/shard_map/ppermute | solution.py:19
  189.5 13.6 %collective-permute-start.8 = (f32[32]{0:T(128)S(1)}, f32[32]{0:T(128)S(1)}, u32[]{:S(2)}, u32[]{:S(2)}) collective-permute-start(f32[32]{0:T(128)S(1)} %get-tuple-element.20), channel_id=1, source_target_pairs={{16,0},{18,2},{20,4},{22,6},{24,8},{26,10},{28,12},{30,14},{32,16}... | collective-permute-start | bytes 392 | tf_op jit(solution)/shard_map/ppermute | solution.py:19
  211.4 29.4 %collective-permute-start.12 = (f32[64,2048]{1,0:T(8,128)}, f32[64,2048]{1,0:T(8,128)}, u32[]{:S(2)}, u32[]{:S(2)}) collective-permute-start(f32[64,2048]{1,0:T(8,128)} %get-tuple-element.39), channel_id=1, source_target_pairs={{0,4},{2,6},{4,8},{6,10},{8,12},{10,14},{12,16},{14,18},{16,20},{1... | collective-permute-start | bytes 1572872 | tf_op jit(solution)/shard_map/ppermute | solution.py:19
  213.4 31.6 %collective-permute-start.10 = (f32[32]{0:T(128)S(1)}, f32[32]{0:T(128)S(1)}, u32[]{:S(2)}, u32[]{:S(2)}) collective-permute-start(f32[32]{0:T(128)S(1)} %get-tuple-element.16), channel_id=1, source_target_pairs={{32,0},{34,2},{36,4},{38,6},{40,8},{42,10},{44,12},{46,14},{48,16}... | collective-permute-start | bytes 392 | tf_op jit(solution)/shard_map/ppermute | solution.py:19
  220.2 24.8 %collective-permute-start.15 = (f32[32]{0:T(128)S(1)}, f32[32]{0:T(128)S(1)}, u32[]{:S(2)}, u32[]{:S(2)}) collective-permute-start(f32[32]{0:T(128)S(1)} %get-tuple-element.42), channel_id=1, source_target_pairs={{0,4},{2,6},{4,8},{6,10},{8,12},{10,14},{12,16},{14,18},{16,20},{1... | collective-permute-start | bytes 392 | tf_op jit(solution)/shard_map/ppermute | solution.py:19
  243.1 50.8 %collective-permute-start.14 = (f32[64,2048]{1,0:T(8,128)}, f32[64,2048]{1,0:T(8,128)}, u32[]{:S(2)}, u32[]{:S(2)}) collective-permute-start(f32[64,2048]{1,0:T(8,128)} %multiply_add_fusion.7), channel_id=1, source_target_pairs={{0,8},{2,10},{4,12},{6,14},{8,16},{10,18},{12,20},{14,22},{16,24},... | collective-permute-start | bytes 1572872 | tf_op jit(solution)/shard_map/ppermute | solution.py:19
  245.2 31.7 %collective-permute-start.17 = (f32[32]{0:T(128)S(1)}, f32[32]{0:T(128)S(1)}, u32[]{:S(2)}, u32[]{:S(2)}) collective-permute-start(f32[32]{0:T(128)S(1)} %get-tuple-element.32), channel_id=1, source_target_pairs={{0,8},{2,10},{4,12},{6,14},{8,16},{10,18},{12,20},{14,22},{16,24},... | collective-permute-start | bytes 392 | tf_op jit(solution)/shard_map/ppermute | solution.py:19
  284.4 7.9 %collective-permute-start.21 = (f32[32]{0:T(128)S(1)}, f32[32]{0:T(128)S(1)}, u32[]{:S(2)}, u32[]{:S(2)}) collective-permute-start(f32[32]{0:T(128)S(1)} %get-tuple-element.26), channel_id=1, source_target_pairs={{0,32},{2,34},{4,36},{6,38},{8,40},{10,42},{12,44},{14,46},{16,48}... | collective-permute-start | bytes 392 | tf_op jit(solution)/shard_map/ppermute | solution.py:19
  292.4 11.1 %collective-permute-start.9 = (f32[64,2048]{1,0:T(8,128)}, f32[64,2048]{1,0:T(8,128)S(1)}, u32[]{:S(2)}, u32[]{:S(2)}) collective-permute-start(f32[64,2048]{1,0:T(8,128)} %get-tuple-element.18), channel_id=1, source_target_pairs={{64,0},{66,2},{68,4},{70,6},{72,8},{74,10},{76,12},{78,14},{80,16}... | collective-permute-start | bytes 1572872 | tf_op jit(solution)/shard_map/ppermute | solution.py:19
  296.6 15.9 %collective-permute-start.16 = (f32[64,2048]{1,0:T(8,128)}, f32[64,2048]{1,0:T(8,128)}, u32[]{:S(2)}, u32[]{:S(2)}) collective-permute-start(f32[64,2048]{1,0:T(8,128)} %get-tuple-element.34), channel_id=1, source_target_pairs={{0,16},{2,18},{4,20},{6,22},{8,24},{10,26},{12,28},{14,30},{16,32}... | collective-permute-start | bytes 1572872 | tf_op jit(solution)/shard_map/ppermute | solution.py:19
  313.7 15.0 %collective-permute-start.18 = (f32[64,2048]{1,0:T(8,128)S(1)}, f32[64,2048]{1,0:T(8,128)S(1)}, u32[]{:S(2)}, u32[]{:S(2)}) collective-permute-start(f32[64,2048]{1,0:T(8,128)S(1)} %multiply_add_fusion.3), channel_id=1, source_target_pairs={{0,32},{2,34},{4,36},{6,38},{8,40},{10,42},{12,44},{14,46},{16,48}... | collective-permute-start | bytes 1572872 | tf_op jit(solution)/shard_map/ppermute | solution.py:19
  329.9 11.7 %collective-permute-start.20 = (f32[64,2048]{1,0:T(8,128)S(1)}, f32[64,2048]{1,0:T(8,128)S(1)}, u32[]{:S(2)}, u32[]{:S(2)}) collective-permute-start(f32[64,2048]{1,0:T(8,128)S(1)} %get-tuple-element.28), channel_id=1, source_target_pairs={{0,64},{2,66},{4,68},{6,70},{8,72},{10,74},{12,76},{14,78},{16,80}... | collective-permute-start | bytes 1572872 | tf_op jit(solution)/shard_map/ppermute | solution.py:19
  356.4 98.9 %all-to-all-start.1 = ((f32[128,32,256]{2,1,0:T(8,128)}), f32[128,32,256]{2,1,0:T(8,128)}, u32[]{:S(2)}, u32[]{:S(2)}) async-start(f32[128,32,256]{2,1,0:T(8,128)} %bitcast.147), calls=%async_computation.2 | async-start | bytes 8388608 | tf_op jit(solution)/shard_map/all_to_all | solution.py:217
  363.2 95.2 %reduce-scatter.2.cloned.1.call-start = ((), (), s32[]{:S(2)}) async-start(), calls=%async_computation.3 | async-start | bytes 1572864 | tf_op jit(solution)/shard_map/reduce_scatter | solution.py:212
  (21 other events, 172.8 us)
Sparse Core Ops, SparseCore 0:
  367.1 14.5 reduce-scatter.1

commit v3 on v2

--- a/solution.py
+++ b/solution.py
@@ -8,24 +8,41 @@
 SPAN = 128
 
 
-def carried_in(part, axis, combine, identity, reverse):
+def carried_both(decay, state, adjoint, axis):
     count = lax.axis_size(axis)
-
-    def shifted(tree, offset):
-        if reverse:
-            pairs = [(i + offset, i) for i in range(count - offset)]
-        else:
-            pairs = [(i, i + offset) for i in range(count - offset)]
-        return jax.tree.map(lambda a: lax.ppermute(a, axis, pairs), tree)
-
-    window = jax.tree.map(lambda a, e: jnp.zeros_like(a) + jnp.asarray(e, a.dtype), part, identity)
-    whole = part
+    rows, cols = state.shape
+    chunk = cols // count
+    decay_row = jnp.repeat(decay, cols // decay.shape[0])[None, :]
+    packed = jnp.stack(
+        [jnp.concatenate([state, decay_row], 0), jnp.concatenate([adjoint, decay_row], 0)]
+    )
+    packed = packed.reshape(2, rows + 1, count, chunk).transpose(2, 0, 1, 3)
+    got = lax.all_to_all(packed, axis, 0, 0, tiled=True)
+    decays = got[:, :, rows:, :]
+    parts = got[:, :, :rows, :]
+
+    def chain_cols(earlier, later):
+        return (earlier[0] * later[0], earlier[1] * later[0] + later[1])
+
+    decays = jnp.stack([decays[:, 0], decays[::-1, 1]], 1)
+    parts = jnp.stack([parts[:, 0], parts[::-1, 1]], 1)
+
+    def moved(a, offset):
+        return jnp.concatenate([jnp.zeros_like(a[:offset]), a[:-offset]], 0)
+
+    win_decay, win_part = jnp.ones_like(decays), jnp.zeros_like(parts)
+    whole = (decays, parts)
     offset = 1
     while offset < count:
-        window = combine(shifted(whole, offset), window)
-        whole = combine(window, part)
+        win_decay, win_part = chain_cols(
+            (moved(whole[0], offset), moved(whole[1], offset)), (win_decay, win_part)
+        )
+        whole = chain_cols((win_decay, win_part), (decays, parts))
         offset *= 2
-    return window
+    scanned = jnp.stack([win_part[:, 0], win_part[::-1, 1]], 1)
+    back = lax.all_to_all(scanned, axis, 0, 0, tiled=True)
+    back = back.transpose(1, 2, 0, 3).reshape(2, rows, cols)
+    return back[0], back[1]
 
 
 def span_summary(b_vals, c_vals, x_vals, dy_round, rate_vals):
@@ -165,12 +182,7 @@
             dev_adjoint * jnp.repeat(summaries[block_id][0], HEAD_DIM)[None, :]
             + summaries[block_id][2]
         )
-    identity = (
-        jnp.ones((head_count,), jnp.float32),
-        jnp.zeros((STATE, head_count * HEAD_DIM), jnp.float32),
-    )
-    state_start = carried_in((dev_decay, dev_state), "ctx", chain, identity, False)[1]
-    adjoint_end = carried_in((dev_decay, dev_adjoint), "ctx", chain, identity, True)[1]
+    state_start, adjoint_end = carried_both(dev_decay, dev_state, dev_adjoint, "ctx")
     running = state_start
     block_id = 0
     states_in = running

time: 468 us -> 340 us (0.73)
  waiting for transfers between devices: 257 us -> 152 us
  starting transfers between devices: 103 us -> 31 us
  blocking collectives: 0 us -> 54.9 us
  local copies, waits for them, and re-layouts: 31.7 us -> 40.3 us
  other arithmetic: 34.3 us -> 26.3 us
  matrix products: 23.9 us -> 18.6 us
    ppermute x22 -> x0, waiting for transfers between devices: 140 us -> none  [shifted(): return jax.tree.map(lambda a: lax.ppermute(a, axis, pairs), tree)]
    ppermute x22 -> x0, starting transfers between devices: 80.8 us -> none  [shifted(): return jax.tree.map(lambda a: lax.ppermute(a, axis, pairs), tree)]
    all_to_all x0 -> x1, blocking collectives: none -> 54.9 us  [carried_both(): got = lax.all_to_all(packed, axis, 0, 0, tiled=True)]
    all_to_all x0 -> x1, waiting for transfers between devices: none -> 28.5 us  [carried_both(): back = lax.all_to_all(scanned, axis, 0, 0, tiled=True)]
    add x12 -> x11, other arithmetic: 22.4 us -> 7.39 us  [the longest x10 7.19 us: chain_cols(): return (earlier[0] * later[0], earlier[1] * later[0] + later[1])]
    unnamed x46 -> x71, local copies, waits for them, and re-layouts: 12.6 us -> 22.4 us
    reshape x4 -> x0, local copies, waits for them, and re-layouts: 9.37 us -> none  [the longest x1 2.35 us: span_full(): state_four = state_in.reshape(STATE, group_count, per_group, HEAD_DIM)]
    all_to_all x0 -> x1, starting transfers between devices: none -> 6.03 us  [carried_both(): back = lax.all_to_all(scanned, axis, 0, 0, tiled=True)]
  transfers between devices with their start and end apart: 25 -> 4, of which waited for: 17 -> 3; matrix products, arithmetic and copies ran while one was open for 10% -> 7% of each run, Pallas kernels for 0% -> 0%
where the time goes in v3:
time: 340 us; the launch traced here: 338 us
  waiting for transfers between devices  152 us (45%)
  blocking collectives  54.9 us (16%)
  local copies, waits for them, and re-layouts  40.3 us (12%)
  starting transfers between devices  31 us (9%)
  other arithmetic  26.3 us (8%)
  matrix products  18.6 us (5%)
  between operations  14.6 us (4%)
    all_to_all x1, waiting for transfers between devices, body(): lax.all_to_all(proj_terms.reshape(shard_count, -1, col_count), ('dp', 'ct...  83.6 us
    all_to_all x1, blocking collectives, carried_both(): got = lax.all_to_all(packed, axis, 0, 0, tiled=True)  54.9 us
    all_to_all x1, waiting for transfers between devices, body(): lax.all_to_all(jnp.broadcast_to(weight_local[None], (shard_count,) + weig...  40 us
    all_to_all x1, waiting for transfers between devices, carried_both(): back = lax.all_to_all(scanned, axis, 0, 0, tiled=True)  28.5 us
    unnamed x71, local copies, waits for them, and re-layouts  22.4 us
    all_to_all x1, starting transfers between devices, body(): lax.all_to_all(jnp.broadcast_to(weight_local[None], (shard_count,) + weig...  15.8 us
    all_to_all x1, starting transfers between devices, body(): lax.all_to_all(proj_terms.reshape(shard_count, -1, col_count), ('dp', 'ct...  9.14 us
    add x10, other arithmetic, chain_cols(): return (earlier[0] * later[0], earlier[1] * later[0] + later[1])  7.19 us
  transfers between devices with their start and end apart: 4, of which 3 were waited for; matrix products, arithmetic and copies ran while one was open for 7% of the time, Pallas kernels for 0%

profile of v3, /device:TPU:24, one launch (start us, length us, event | category | flops | bytes accessed | tf_op | source)
XLA Modules:
  0.0 337.8 jit_solution(1323714665796017930)
XLA Ops:
  9.6 15.8 %all-to-all-start = ((bf16[128,32,256]{2,1,0:T(8,128)(2,1)}), bf16[128,32,256]{2,1,0:T(8,128)(2,1)S(1)}, u32[]{:S(2)}, u32[]{:S(2)}) async-start(bf16[128,32,256]{2,1,0:T(8,128)(2,1)} %broadcast_in_dim.33), calls=%async_computation | async-start | bytes 4194304 | tf_op jit(solution)/shard_map/all_to_all | solution.py:150
  26.1 2.0 copy.63
  28.1 2.0 copy.61
  30.1 2.1 convert_element_type.116
  32.2 2.0 copy.62
  37.6 40.0 %all-to-all-done = bf16[128,32,256]{2,1,0:T(8,128)(2,1)S(1)} async-done(((bf16[128,32,256]{2,1,0:T(8,128)(2,1)}), bf16[128,32,256]{2,1,0:T(8,128)(2,1)S(1)}, u32[]{:S(2)}, u32[]{:S(2)}) %all-to-all-start) | async-done | bytes 2097184 | tf_op jit(solution)/shard_map/all_to_all | solution.py:150
  78.1 1.8 fusion.25
  82.6 54.9 %all_to_all.20 = f32[64,2,65,32]{2,3,1,0:T(8,128)S(1)} all-to-all(f32[64,2,65,32]{2,3,1,0:T(8,128)S(1)} %maximum_bitcast_fusion), channel_id=1, replica_groups=mesh['dp'=2,'ctx'=64,'head'=2] {'ctx'}, dimensions={0} | all-to-all | bytes 2129920 | tf_op jit(solution)/shard_map/all_to_all | solution.py:20
  140.2 2.7 fusion.68
  163.2 2.3 reshape.180
  165.5 6.0 %all-to-all-start.2 = ((f32[64,1,4096]{2,1,0:T(1,128)}), f32[64,1,4096]{2,1,0:T(1,128)S(1)}, u32[]{:S(2)}, u32[]{:S(2)}) async-start(f32[64,1,4096]{2,1,0:T(1,128)} %reshape.180), calls=%async_computation.2 | async-start | bytes 2097152 | tf_op jit(solution)/shard_map/all_to_all | solution.py:43
  171.5 28.5 %all-to-all-done.2 = f32[64,1,4096]{2,1,0:T(1,128)S(1)} async-done(((f32[64,1,4096]{2,1,0:T(1,128)}), f32[64,1,4096]{2,1,0:T(1,128)S(1)}, u32[]{:S(2)}, u32[]{:S(2)}) %all-to-all-start.2) | async-done | bytes 1048608 | tf_op jit(solution)/shard_map/all_to_all | solution.py:43
  200.6 4.5 %reduce.2 = f32[64,4096]{1,0:T(8,128)} reduce(f32[64,1,4096]{2,1,0:T(1,128)S(1)} %all-to-all-done.2, f32[]{:T(128)} %broadcast.84), dimensions={1}, to_apply=%all_to_all.14.reduce_sub_computation | reduce | bytes 2097156 | tf_op jit(solution)/shard_map/all_to_all | solution.py:43
  205.1 2.0 reshape.181
  208.9 1.9 convolution_bitcast_fusion.4
  210.8 1.9 convolution_bitcast_fusion.3
  215.4 2.7 convolution_bitcast_fusion
  218.2 5.6 %copy.78 = f32[4096,256]{1,0:T(8,128)} copy(f32[4096,256]{0,1:T(8,128)} %convolution_bitcast_fusion) | data formatting | bytes 8388608 | tf_op jit(solution)/shard_map/td,tc->dc/dot_general | solution.py:228
  223.8 9.1 %all-to-all-start.3 = ((f32[128,32,256]{2,1,0:T(8,128)}), f32[128,32,256]{2,1,0:T(8,128)}, u32[]{:S(2)}, u32[]{:S(2)}) async-start(f32[128,32,256]{2,1,0:T(8,128)} %bitcast.163), calls=%async_computation.4 | async-start | bytes 8388608 | tf_op jit(solution)/shard_map/all_to_all | solution.py:229
  233.0 1.9 convolution_convert_fusion
  236.1 2.5 fusion.19
  238.6 2.1 copy.79
  244.3 83.6 %all-to-all-done.3 = f32[128,32,256]{2,1,0:T(8,128)} async-done(((f32[128,32,256]{2,1,0:T(8,128)}), f32[128,32,256]{2,1,0:T(8,128)}, u32[]{:S(2)}, u32[]{:S(2)}) %all-to-all-start.3) | async-done | bytes 4194336 | tf_op jit(solution)/shard_map/all_to_all | solution.py:229
  327.9 2.5 reduce_sum.19
  (132 shorter events, 42.7 us)
Async XLA Ops:
  7.2 70.4 %copy-start = (bf16[1,128,4096]{2,1,0:T(8,128)(2,1)S(1)}, bf16[1,128,4096]{2,1,0:T(8,128)(2,1)}, u32[]{:S(2)}) copy-start(bf16[1,128,4096]{2,1,0:T(8,128)(2,1)} %param.7) | copy-start | bytes 3145732
  9.6 15.8 %copy-start.26 = (f32[1,32,128]{2,1,0:T(8,128)S(1)}, f32[1,32,128]{2,1,0:T(8,128)}, u32[]{:S(2)}) copy-start(f32[1,32,128]{2,1,0:T(8,128)} %param.11) | copy-start | bytes 49156
  9.6 67.9 %all-to-all-start = ((bf16[128,32,256]{2,1,0:T(8,128)(2,1)}), bf16[128,32,256]{2,1,0:T(8,128)(2,1)S(1)}, u32[]{:S(2)}, u32[]{:S(2)}) async-start(bf16[128,32,256]{2,1,0:T(8,128)(2,1)} %broadcast_in_dim.33), calls=%async_computation | async-start | bytes 4194304 | tf_op jit(solution)/shard_map/all_to_all | solution.py:150
  34.3 2.2 copy-start.4
  36.2 43.8 %copy-start.22 = (f32[32,128]{1,0:T(8,128)}, f32[32,128]{1,0:T(8,128)S(1)}, u32[]{:S(2)}) copy-start(f32[32,128]{1,0:T(8,128)S(1)} %get-tuple-element.32) | copy-start | bytes 49156
  77.5 2.4 copy-start.1
  137.5 1.3 copy-start.3
  165.5 34.6 %all-to-all-start.2 = ((f32[64,1,4096]{2,1,0:T(1,128)}), f32[64,1,4096]{2,1,0:T(1,128)S(1)}, u32[]{:S(2)}, u32[]{:S(2)}) async-start(f32[64,1,4096]{2,1,0:T(1,128)} %reshape.180), calls=%async_computation.2 | async-start | bytes 2097152 | tf_op jit(solution)/shard_map/all_to_all | solution.py:43
  207.4 5.2 %copy-start.10 = (f32[1,64,64,32]{1,3,2,0:T(8,128)}, f32[1,64,64,32]{1,3,2,0:T(8,128)S(1)}, u32[]{:S(2)}) copy-start(f32[1,64,64,32]{1,3,2,0:T(8,128)S(1)} %get-tuple-element.21) | copy-start | bytes 1572868
  207.5 1.4 copy-start.13
  207.5 3.3 copy-start.12
  207.5 3.3 copy-start.23
  208.9 3.8 %copy-start.5 = (f32[1,128,2048]{1,2,0:T(8,128)S(1)}, f32[1,128,2048]{1,2,0:T(8,128)}, u32[]{:S(2)}) copy-start(f32[1,128,2048]{1,2,0:T(8,128)} %convert_element_type.116) | copy-start | bytes 3145732
  208.9 3.8 %copy-start.8 = (f32[1,128,2048]{1,2,0:T(8,128)S(1)}, f32[1,128,2048]{1,2,0:T(8,128)}, u32[]{:S(2)}) copy-start(f32[1,128,2048]{1,2,0:T(8,128)} %copy-done.7) | copy-start | bytes 3145732
  223.8 9.2 %copy-start.2 = (bf16[128,32,256]{2,1,0:T(8,128)(2,1)S(1)}, bf16[128,32,256]{2,1,0:T(8,128)(2,1)}, u32[]{:S(2)}) copy-start(bf16[128,32,256]{2,1,0:T(8,128)(2,1)} %copy-done.1) | copy-start | bytes 6291460
  223.8 104.1 %all-to-all-start.3 = ((f32[128,32,256]{2,1,0:T(8,128)}), f32[128,32,256]{2,1,0:T(8,128)}, u32[]{:S(2)}, u32[]{:S(2)}) async-start(f32[128,32,256]{2,1,0:T(8,128)} %bitcast.163), calls=%async_computation.4 | async-start | bytes 8388608 | tf_op jit(solution)/shard_map/all_to_all | solution.py:229
  232.9 2.9 copy-start.27
  232.9 98.1 %reduce-scatter.2.cloned.1.call-start = ((), (), s32[]{:S(2)}) async-start(), calls=%async_computation.5 | async-start | bytes 1572864 | tf_op jit(solution)/shard_map/reduce_scatter | solution.py:224
  234.9 1.2 copy-start.15
  236.1 4.6 %copy-start.11 = (f32[1,64,64,32]{1,3,2,0:T(8,128)S(1)}, f32[1,64,64,32]{1,3,2,0:T(8,128)}, u32[]{:S(2)}) copy-start(f32[1,64,64,32]{1,3,2,0:T(8,128)} %copy-done.10) | copy-start | bytes 1572868
  238.6 2.7 copy-start.25
  240.7 1.2 copy-start.6
  240.7 1.5 copy-start.9
  240.7 1.7 copy-start.14
  (8 other events, 7.1 us)
Sparse Core Ops, SparseCore 0:
  236.8 14.5 reduce-scatter.1

commit v4 on v3

--- a/solution.py
+++ b/solution.py
@@ -6,41 +6,39 @@
 HEAD_DIM = 64
 STATE = 64
 SPAN = 128
-
-
-def carried_both(decay, state, adjoint, axis):
+CTX_PARTS = (("ylo", 2), ("x", 4), ("z", 8))
+CTX = tuple(name for name, _ in CTX_PARTS)
+ROWS = ("dp",) + CTX
+OUTER = ROWS[:-1]
+INNER = ROWS[-1]
+
+
+def carried_both(log_total, state, adjoint, axis):
     count = lax.axis_size(axis)
     rows, cols = state.shape
     chunk = cols // count
-    decay_row = jnp.repeat(decay, cols // decay.shape[0])[None, :]
-    packed = jnp.stack(
-        [jnp.concatenate([state, decay_row], 0), jnp.concatenate([adjoint, decay_row], 0)]
+    assert HEAD_DIM % chunk == 0
+    log_row = jnp.repeat(log_total, cols // log_total.shape[0])[None, :]
+    packed = jnp.concatenate(
+        [jnp.concatenate([state, log_row], 0)[None], jnp.pad(adjoint, ((0, 1), (0, 0)))[None]], 0
     )
     packed = packed.reshape(2, rows + 1, count, chunk).transpose(2, 0, 1, 3)
     got = lax.all_to_all(packed, axis, 0, 0, tiled=True)
-    decays = got[:, :, rows:, :]
-    parts = got[:, :, :rows, :]
-
-    def chain_cols(earlier, later):
-        return (earlier[0] * later[0], earlier[1] * later[0] + later[1])
-
-    decays = jnp.stack([decays[:, 0], decays[::-1, 1]], 1)
-    parts = jnp.stack([parts[:, 0], parts[::-1, 1]], 1)
-
-    def moved(a, offset):
-        return jnp.concatenate([jnp.zeros_like(a[:offset]), a[:-offset]], 0)
-
-    win_decay, win_part = jnp.ones_like(decays), jnp.zeros_like(parts)
-    whole = (decays, parts)
-    offset = 1
-    while offset < count:
-        win_decay, win_part = chain_cols(
-            (moved(whole[0], offset), moved(whole[1], offset)), (win_decay, win_part)
-        )
-        whole = chain_cols((win_decay, win_part), (decays, parts))
-        offset *= 2
-    scanned = jnp.stack([win_part[:, 0], win_part[::-1, 1]], 1)
-    back = lax.all_to_all(scanned, axis, 0, 0, tiled=True)
+    logs = got[:, 0, rows, 0]
+    place = jnp.arange(count)
+    inside = (place[None, :, None] < place[None, None, :]) & (
+        place[None, None, :] < place[:, None, None]
+    )
+    gaps = jnp.sum(jnp.where(inside, logs[None, None, :], 0.0), axis=-1)
+    before = place[None, :] < place[:, None]
+    carry = jnp.where(before, jnp.exp(jnp.where(before, gaps, 0.0)), 0.0)
+    fwd = jnp.einsum(
+        "ik,knc->inc", carry, got[:, 0, :rows], precision=lax.Precision.HIGHEST
+    )
+    bwd = jnp.einsum(
+        "ki,knc->inc", carry, got[:, 1, :rows], precision=lax.Precision.HIGHEST
+    )
+    back = lax.all_to_all(jnp.stack([fwd, bwd], 1), axis, 0, 0, tiled=True)
     back = back.transpose(1, 2, 0, 3).reshape(2, rows, cols)
     return back[0], back[1]
 
@@ -146,10 +144,18 @@
     tok_rows = tokens.shape[0]
     weight_local = proj_weight.reshape(proj_weight.shape[0], -1)
     col_count = weight_local.shape[1]
-    shard_count = lax.axis_size(("dp", "ctx"))
+    inner_count = lax.axis_size(INNER)
+    outer_count = lax.axis_size(OUTER)
+    weight_inner = lax.all_to_all(
+        jnp.broadcast_to(weight_local[None], (inner_count,) + weight_local.shape),
+        INNER,
+        0,
+        0,
+        tiled=True,
+    )
     weight_full = lax.all_to_all(
-        jnp.broadcast_to(weight_local[None], (shard_count,) + weight_local.shape),
-        ("dp", "ctx"),
+        jnp.broadcast_to(weight_inner[None], (outer_count,) + weight_inner.shape),
+        OUTER,
         0,
         0,
         tiled=True,
@@ -177,12 +183,13 @@
         dev_state * jnp.repeat(summaries[block_id][0], HEAD_DIM)[None, :] + summaries[block_id][1]
     )
     dev_decay = dev_decay * summaries[block_id][0]
+    dev_log = jnp.sum(jnp.cumsum(rate_vals, axis=2)[:, :, -1], axis=1)
     for block_id in reversed(range(nblocks)):
         dev_adjoint = (
             dev_adjoint * jnp.repeat(summaries[block_id][0], HEAD_DIM)[None, :]
             + summaries[block_id][2]
         )
-    state_start, adjoint_end = carried_both(dev_decay, dev_state, dev_adjoint, "ctx")
+    state_start, adjoint_end = carried_both(dev_log, dev_state, dev_adjoint, CTX)
     running = state_start
     block_id = 0
     states_in = running
@@ -224,38 +231,40 @@
     grad_input = lax.psum_scatter(
         input_terms.astype(jnp.bfloat16), "head", scatter_dimension=1, tiled=True
     )[None]
-    scale = 1.0 / (lax.axis_size("dp") * lax.axis_size("ctx") * tok_rows)
+    scale = 1.0 / (lax.axis_size(ROWS) * tok_rows)
     proj_terms = jnp.einsum("td,tc->dc", tokens, grad_flat, preferred_element_type=jnp.float32)
     proj_parts = lax.all_to_all(
-        proj_terms.reshape(shard_count, -1, col_count),
-        ("dp", "ctx"),
-        0,
-        0,
-        tiled=True,
-    )
+        proj_terms.reshape(outer_count, inner_count, -1, col_count), OUTER, 0, 0, tiled=True
+    ).sum(axis=0)
+    proj_parts = lax.all_to_all(proj_parts, INNER, 0, 0, tiled=True)
     grad_proj = proj_parts.sum(axis=0) * scale
     grad_proj = grad_proj.reshape(-1, 2, col_count // 2)
     return (grad_input, grad_values, grad_gate, grad_proj)
 
 
 def solution(mesh):
+    sizes = tuple(size for _, size in CTX_PARTS)
+    fine = jax.sharding.Mesh(
+        mesh.devices.reshape(mesh.shape["dp"], *sizes, mesh.shape["head"]),
+        ("dp",) + CTX + ("head",),
+    )
     return jax.shard_map(
         body,
-        mesh=mesh,
+        mesh=fine,
         in_specs=(
-            P("dp", "ctx", None),
-            P(("dp", "ctx"), None, "head"),
-            P("dp", "ctx", "head"),
-            P("dp", "ctx", "head"),
-            P("dp", "head", "ctx"),
+            P("dp", CTX, None),
+            P(ROWS, None, "head"),
+            P("dp", CTX, "head"),
+            P("dp", CTX, "head"),
+            P("dp", "head", CTX),
             P("head"),
-            P("dp", "ctx", "head"),
+            P("dp", CTX, "head"),
         ),
         out_specs=(
-            P("dp", "ctx", "head"),
-            P("dp", "ctx", "head"),
-            P("dp", "ctx", "head"),
-            P(("dp", "ctx"), None, "head"),
+            P("dp", CTX, "head"),
+            P("dp", CTX, "head"),
+            P("dp", CTX, "head"),
+            P(ROWS, None, "head"),
         ),
         check_vma=False,
     )

time: 340 us -> 289 us (0.85)
  blocking collectives: 54.9 us -> 17.4 us
  waiting for transfers between devices: 152 us -> 133 us
  starting transfers between devices: 31 us -> 36.6 us
  matrix products: 18.6 us -> 22.7 us
  other arithmetic: 26.3 us -> 22.8 us
    all_to_all x1, blocking collectives: 54.9 us -> 17.4 us  [body(): lax.all_to_all(jnp.broadcast_to(weight_local[None], (inner_count,) + weig...]
    all_to_all x3 -> x5, waiting for transfers between devices: 152 us -> 133 us  [the longest x1 50.8 us: carried_both(): got = lax.all_to_all(packed, axis, 0, 0, tiled=True)]
    add x10 -> x1, other arithmetic: 7.19 us -> 0.33 us  [body(): dev_adjoint * jnp.repeat(summaries[block_id][0], HEAD_DIM)[None, :]]
    all_to_all x3 -> x5, starting transfers between devices: 31 us -> 36.3 us  [the longest x1 10.1 us: body(): proj_parts = lax.all_to_all(proj_parts, INNER, 0, 0, tiled=True)]
    reduce_sum x0 -> x2, other arithmetic: none -> 3.83 us  [the longest x1 3.2 us: body(): proj_parts = lax.all_to_all(proj_terms.reshape(outer_count, inner_count,...]
    convert_element_type x1 -> x2, other arithmetic: 1.08 us -> 4.5 us  [body(): (dout_vals.astype(jnp.float32) * jax.nn.silu(gate_vals.astype(jnp.float32...]
    unnamed x71 -> x40, local copies, waits for them, and re-layouts: 22.4 us -> 21.1 us
  transfers between devices with their start and end apart: 4 -> 6, of which waited for: 3 -> 5; matrix products, arithmetic and copies ran while one was open for 7% -> 13% of each run, Pallas kernels for 0% -> 0%
where the time goes in v4:
time: 289 us; the launch traced here: 287 us
  waiting for transfers between devices  133 us (46%)
  local copies, waits for them, and re-layouts  40.1 us (14%)
  starting transfers between devices  36.6 us (13%)
  other arithmetic  22.8 us (8%)
  matrix products  22.7 us (8%)
  blocking collectives  17.4 us (6%)
  between operations  14.4 us (5%)
    all_to_all x1, waiting for transfers between devices, carried_both(): got = lax.all_to_all(packed, axis, 0, 0, tiled=True)  50.8 us
    all_to_all x1, waiting for transfers between devices, body(): lax.all_to_all(proj_terms.reshape(outer_count, inner_count, -1, col_count...  45.2 us
    all_to_all x1, waiting for transfers between devices, carried_both(): back = lax.all_to_all(jnp.stack([fwd, bwd], 1), axis, 0, 0, tiled=True)  24.9 us
    unnamed x40, local copies, waits for them, and re-layouts  21.1 us
    all_to_all x1, blocking collectives, body(): lax.all_to_all(jnp.broadcast_to(weight_local[None], (inner_count,) + weig...  17.4 us
    all_to_all x1, waiting for transfers between devices, body(): lax.all_to_all(jnp.broadcast_to(weight_inner[None], (outer_count,) + weig...  12 us
    all_to_all x1, starting transfers between devices, body(): proj_parts = lax.all_to_all(proj_parts, INNER, 0, 0, tiled=True)  10.1 us
    all_to_all x1, starting transfers between devices, body(): lax.all_to_all(jnp.broadcast_to(weight_inner[None], (outer_count,) + weig...  7.17 us
  transfers between devices with their start and end apart: 6, of which 5 were waited for; matrix products, arithmetic and copies ran while one was open for 13% of the time, Pallas kernels for 0%

profile of v4, /device:TPU:24, one launch (start us, length us, event | category | flops | bytes accessed | tf_op | source)
XLA Modules:
  0.0 287.4 jit_solution(1371541935858720926)
XLA Ops:
  8.0 17.4 %all_to_all.30 = bf16[8,32,256]{2,1,0:T(8,128)(2,1)S(1)} all-to-all(bf16[8,32,256]{2,1,0:T(8,128)(2,1)S(1)} %broadcast_in_dim.92), channel_id=1, replica_groups=mesh['dp'=2,'ylo'=2,'x'=4,'z'=8,'head'=2] {'z'}, dimensions={0} | all-to-all | bytes 262144 | tf_op jit(solution)/shard_map/all_to_all | solution.py:149
  27.0 7.2 %all-to-all-start.1 = ((bf16[16,8,32,256]{3,2,1,0:T(8,128)(2,1)}), bf16[16,8,32,256]{3,2,1,0:T(8,128)(2,1)S(1)}, u32[]{:S(2)}, u32[]{:S(2)}) async-start(bf16[16,8,32,256]{3,2,1,0:T(8,128)(2,1)} %broadcast_in_dim.93), calls=%async_computation.1 | async-start | bytes 4194304 | tf_op jit(solution)/shard_map/all_to_all | solution.py:156
  36.2 2.2 convert_element_type.118
  40.4 2.1 convert_element_type.119
  43.4 2.0 copy.63
  45.7 2.6 multiply_convert_fusion
  48.3 12.0 %all-to-all-done.1 = bf16[16,8,32,256]{3,2,1,0:T(8,128)(2,1)S(1)} async-done(((bf16[16,8,32,256]{3,2,1,0:T(8,128)(2,1)}), bf16[16,8,32,256]{3,2,1,0:T(8,128)(2,1)S(1)}, u32[]{:S(2)}, u32[]{:S(2)}) %all-to-all-start.1) | async-done | bytes 2097184 | tf_op jit(solution)/shard_map/all_to_all | solution.py:156
  66.4 6.5 %all-to-all-start.2 = ((f32[64,2,65,32]{2,3,1,0:T(8,128)}), f32[64,2,65,32]{2,3,1,0:T(8,128)}, u32[]{:S(2)}, u32[]{:S(2)}) async-start(f32[64,2,65,32]{2,3,1,0:T(8,128)} %copy.65), calls=%async_computation.2 | async-start | bytes 4194304 | tf_op jit(solution)/shard_map/all_to_all | solution.py:26
  72.9 50.8 %all-to-all-done.2 = f32[64,2,65,32]{2,3,1,0:T(8,128)} async-done(((f32[64,2,65,32]{2,3,1,0:T(8,128)}), f32[64,2,65,32]{2,3,1,0:T(8,128)}, u32[]{:S(2)}, u32[]{:S(2)}) %all-to-all-start.2) | async-done | bytes 1064992 | tf_op jit(solution)/shard_map/all_to_all | solution.py:26
  131.4 2.6 copy.95
  133.9 3.5 %reshape.208 = f32[64,1,4096]{2,1,0:T(1,128)} reshape(f32[64,2,32,64]{3,2,1,0:T(8,128)} %bitcast.174) | data formatting | bytes 2097152
  137.4 6.6 %all-to-all-start.3 = ((f32[64,1,4096]{2,1,0:T(1,128)}), f32[64,1,4096]{2,1,0:T(1,128)}, u32[]{:S(2)}, u32[]{:S(2)}) async-start(f32[64,1,4096]{2,1,0:T(1,128)} %reshape.208), calls=%async_computation.3 | async-start | bytes 2097152 | tf_op jit(solution)/shard_map/all_to_all | solution.py:41
  147.8 24.9 %all-to-all-done.3 = f32[64,1,4096]{2,1,0:T(1,128)} async-done(((f32[64,1,4096]{2,1,0:T(1,128)}), f32[64,1,4096]{2,1,0:T(1,128)}, u32[]{:S(2)}, u32[]{:S(2)}) %all-to-all-start.3) | async-done | bytes 1048608 | tf_op jit(solution)/shard_map/all_to_all | solution.py:41
  173.2 5.4 %reduce.7 = f32[64,4096]{1,0:T(8,128)} reduce(f32[64,1,4096]{2,1,0:T(1,128)} %all-to-all-done.3, f32[]{:T(128)} %broadcast.83), dimensions={1}, to_apply=%all_to_all.21.reduce_sub_computation | reduce | bytes 2097156 | tf_op jit(solution)/shard_map/all_to_all | solution.py:41
  178.6 3.1 %reshape.209 = f32[64,2,32,64]{3,2,1,0:T(8,128)} reshape(f32[64,4096]{1,0:T(8,128)} %reduce.7) | data formatting | bytes 2097152
  188.8 2.6 convolution_bitcast_fusion
  191.5 5.6 %copy.73 = f32[4096,256]{1,0:T(8,128)} copy(f32[4096,256]{0,1:T(8,128)} %convolution_bitcast_fusion) | data formatting | bytes 8388608 | tf_op jit(solution)/shard_map/td,tc->dc/dot_general | solution.py:235
  197.1 6.0 %all-to-all-start.4 = ((f32[16,8,32,256]{3,2,1,0:T(8,128)}), f32[16,8,32,256]{3,2,1,0:T(8,128)}, u32[]{:S(2)}, u32[]{:S(2)}) async-start(f32[16,8,32,256]{3,2,1,0:T(8,128)} %bitcast.163), calls=%async_computation.5 | async-start | bytes 8388608 | tf_op jit(solution)/shard_map/all_to_all | solution.py:236
  210.9 45.2 %all-to-all-done.4 = f32[16,8,32,256]{3,2,1,0:T(8,128)} async-done(((f32[16,8,32,256]{3,2,1,0:T(8,128)}), f32[16,8,32,256]{3,2,1,0:T(8,128)}, u32[]{:S(2)}, u32[]{:S(2)}) %all-to-all-start.4) | async-done | bytes 4194336 | tf_op jit(solution)/shard_map/all_to_all | solution.py:236
  256.1 3.2 %reduce_sum.42 = f32[8,32,256]{2,1,0:T(8,128)} reduce(f32[16,8,32,256]{3,2,1,0:T(8,128)} %all-to-all-done.4, f32[]{:T(128)} %constant.16.clone.1), dimensions={0}, to_apply=%region_5.6 | reduce | flops 983040 | bytes 4456452 | tf_op jit(solution)/shard_map/reduce_sum | solution.py:238
  259.3 10.1 %all-to-all-start.5 = ((f32[8,32,256]{2,1,0:T(8,128)}), f32[8,32,256]{2,1,0:T(8,128)S(1)}, u32[]{:S(2)}, u32[]{:S(2)}) async-start(f32[8,32,256]{2,1,0:T(8,128)} %reduce_sum.42), calls=%async_computation.6 | async-start | bytes 524288 | tf_op jit(solution)/shard_map/all_to_all | solution.py:239
  269.4 2.3 bitcast_multiply_fusion.1
  271.7 2.0 copy.74
  273.8 3.5 %fusion.9 = bf16[128,32,64]{0,2,1:T(8,128)(2,1)} fusion(f32[128,32,64]{0,2,1:T(8,128)S(1)} %bitcast.166, f32[128,32,64]{0,2,1:T(8,128)} %bitcast_multiply_fusion.1, bf16[32,128,128]{2,1,0:T(8,128)(2,1)} %copy-done.11, bf16[128,32,64]{0,2,1:T(8,128)(2,1)} %bitcast.175, f32[128,32,64]{0,2,1:T(8,128)S(1)} %bitcast.169, f32[32]{0:T(128)S(1)} %copy-done.15), kind=kOutput, calls=%fused_computation.22 | convolution fusion | flops 70778880 | bytes 5243008 | tf_op jit(solution)/shard_map/hts,shp->thp/dot_general | solution.py:97
  (91 shorter events, 43.8 us)
Async XLA Ops:
  7.2 53.1 %copy-start = (bf16[1,128,4096]{2,1,0:T(8,128)(2,1)S(1)}, bf16[1,128,4096]{2,1,0:T(8,128)(2,1)}, u32[]{:S(2)}) copy-start(bf16[1,128,4096]{2,1,0:T(8,128)(2,1)} %param.7) | copy-start | bytes 3145732
  27.0 33.3 %all-to-all-start.1 = ((bf16[16,8,32,256]{3,2,1,0:T(8,128)(2,1)}), bf16[16,8,32,256]{3,2,1,0:T(8,128)(2,1)S(1)}, u32[]{:S(2)}, u32[]{:S(2)}) async-start(bf16[16,8,32,256]{3,2,1,0:T(8,128)(2,1)} %broadcast_in_dim.93), calls=%async_computation.1 | async-start | bytes 4194304 | tf_op jit(solution)/shard_map/all_to_all | solution.py:156
  36.2 6.3 %copy-start.14 = (f32[1,32,128]{2,1,0:T(8,128)S(1)}, f32[1,32,128]{2,1,0:T(8,128)}, u32[]{:S(2)}) copy-start(f32[1,32,128]{2,1,0:T(8,128)} %param.11) | copy-start | bytes 49156
  62.5 1.0 copy-start.8
  66.4 57.2 %all-to-all-start.2 = ((f32[64,2,65,32]{2,3,1,0:T(8,128)}), f32[64,2,65,32]{2,3,1,0:T(8,128)}, u32[]{:S(2)}, u32[]{:S(2)}) async-start(f32[64,2,65,32]{2,3,1,0:T(8,128)} %copy.65), calls=%async_computation.2 | async-start | bytes 4194304 | tf_op jit(solution)/shard_map/all_to_all | solution.py:26
  137.4 35.3 %all-to-all-start.3 = ((f32[64,1,4096]{2,1,0:T(1,128)}), f32[64,1,4096]{2,1,0:T(1,128)}, u32[]{:S(2)}, u32[]{:S(2)}) async-start(f32[64,1,4096]{2,1,0:T(1,128)} %reshape.208), calls=%async_computation.3 | async-start | bytes 2097152 | tf_op jit(solution)/shard_map/all_to_all | solution.py:41
  144.0 2.7 copy-start.9
  145.9 0.8 copy-start.12
  183.5 1.2 copy-start.7
  183.5 3.1 %copy-start.10 = (bf16[1,128,2048]{1,2,0:T(8,128)(2,1)S(1)}, bf16[1,128,2048]{1,2,0:T(8,128)(2,1)}, u32[]{:S(2)}) copy-start(bf16[1,128,2048]{1,2,0:T(8,128)(2,1)} %copy.63) | copy-start | bytes 1572868
  183.7 1.0 copy-start.3
  183.7 2.9 %copy-start.5 = (f32[1,64,64,32]{1,3,2,0:T(8,128)}, f32[1,64,64,32]{1,3,2,0:T(8,128)S(1)}, u32[]{:S(2)}) copy-start(f32[1,64,64,32]{1,3,2,0:T(8,128)S(1)} %get-tuple-element.20) | copy-start | bytes 1572868
  197.1 59.0 %all-to-all-start.4 = ((f32[16,8,32,256]{3,2,1,0:T(8,128)}), f32[16,8,32,256]{3,2,1,0:T(8,128)}, u32[]{:S(2)}, u32[]{:S(2)}) async-start(f32[16,8,32,256]{3,2,1,0:T(8,128)} %bitcast.163), calls=%async_computation.5 | async-start | bytes 8388608 | tf_op jit(solution)/shard_map/all_to_all | solution.py:236
  203.1 77.5 %reduce-scatter.2.cloned.1.call-start = ((), (), s32[]{:S(2)}) async-start(), calls=%async_computation.7 | async-start | bytes 1572864 | tf_op jit(solution)/shard_map/reduce_scatter | solution.py:231
  205.2 1.2 copy-start.6
  206.4 3.3 %copy-start.11 = (bf16[32,128,128]{2,1,0:T(8,128)(2,1)}, bf16[32,128,128]{2,1,0:T(8,128)(2,1)S(1)}, u32[]{:S(2)}) copy-start(bf16[32,128,128]{2,1,0:T(8,128)(2,1)S(1)} %fusion) | copy-start | bytes 3145732
  206.4 1.6 copy-start.4
  207.0 2.6 copy-start.13
  207.0 2.6 copy-start.15
  259.3 14.5 %copy-start.1 = (f32[1,128,2048]{1,2,0:T(8,128)S(1)}, f32[1,128,2048]{1,2,0:T(8,128)}, u32[]{:S(2)}) copy-start(f32[1,128,2048]{1,2,0:T(8,128)} %convert_element_type.118) | copy-start | bytes 3145732
  259.3 14.5 %copy-start.2 = (f32[1,128,2048]{1,2,0:T(8,128)S(1)}, f32[1,128,2048]{1,2,0:T(8,128)}, u32[]{:S(2)}) copy-start(f32[1,128,2048]{1,2,0:T(8,128)} %convert_element_type.119) | copy-start | bytes 3145732
  259.3 20.6 %all-to-all-start.5 = ((f32[8,32,256]{2,1,0:T(8,128)}), f32[8,32,256]{2,1,0:T(8,128)S(1)}, u32[]{:S(2)}, u32[]{:S(2)}) async-start(f32[8,32,256]{2,1,0:T(8,128)} %reduce_sum.42), calls=%async_computation.6 | async-start | bytes 524288 | tf_op jit(solution)/shard_map/all_to_all | solution.py:239
Sparse Core Ops, SparseCore 0:
  206.9 11.1 reduce-scatter.1

commit v5 on v4

--- a/solution.py
+++ b/solution.py
@@ -18,27 +18,30 @@
     rows, cols = state.shape
     chunk = cols // count
     assert HEAD_DIM % chunk == 0
-    log_row = jnp.repeat(log_total, cols // log_total.shape[0])[None, :]
+    lanes = 128
+    slabs = jnp.stack([state, adjoint]).reshape(2, rows, count, chunk).transpose(2, 0, 1, 3)
+    slabs = slabs.reshape(count, -1, lanes)
+    chunk_logs = jnp.repeat(log_total, cols // log_total.shape[0]).reshape(count, chunk)[:, :1]
     packed = jnp.concatenate(
-        [jnp.concatenate([state, log_row], 0)[None], jnp.pad(adjoint, ((0, 1), (0, 0)))[None]], 0
-    )
-    packed = packed.reshape(2, rows + 1, count, chunk).transpose(2, 0, 1, 3)
+        [slabs, jnp.broadcast_to(chunk_logs[:, :, None], (count, 1, lanes))], 1
+    )
     got = lax.all_to_all(packed, axis, 0, 0, tiled=True)
-    logs = got[:, 0, rows, 0]
+    logs = got[:, -1, 0]
+    parts = got[:, :-1].reshape(count, 2, rows, chunk)
     place = jnp.arange(count)
-    inside = (place[None, :, None] < place[None, None, :]) & (
-        place[None, None, :] < place[:, None, None]
-    )
-    gaps = jnp.sum(jnp.where(inside, logs[None, None, :], 0.0), axis=-1)
     before = place[None, :] < place[:, None]
+    gaps = jnp.dot(
+        jnp.where(before, logs[None, :], 0.0),
+        before.astype(jnp.float32),
+        precision=lax.Precision.HIGHEST,
+    )
     carry = jnp.where(before, jnp.exp(jnp.where(before, gaps, 0.0)), 0.0)
-    fwd = jnp.einsum(
-        "ik,knc->inc", carry, got[:, 0, :rows], precision=lax.Precision.HIGHEST
-    )
-    bwd = jnp.einsum(
-        "ki,knc->inc", carry, got[:, 1, :rows], precision=lax.Precision.HIGHEST
-    )
-    back = lax.all_to_all(jnp.stack([fwd, bwd], 1), axis, 0, 0, tiled=True)
+    fwd = jnp.einsum("ik,knc->inc", carry, parts[:, 0], precision=lax.Precision.HIGHEST)
+    bwd = jnp.einsum("ki,knc->inc", carry, parts[:, 1], precision=lax.Precision.HIGHEST)
+    back = lax.all_to_all(
+        jnp.stack([fwd, bwd], 1).reshape(count, -1, lanes), axis, 0, 0, tiled=True
+    )
+    back = back.reshape(count, 2, rows, chunk)
     back = back.transpose(1, 2, 0, 3).reshape(2, rows, cols)
     return back[0], back[1]
 

time: 289 us -> 306 us (1.059)
  waiting for transfers between devices: 133 us -> 90 us
  blocking collectives: 17.4 us -> 58.4 us
  local copies, waits for them, and re-layouts: 40.1 us -> 63.5 us
  starting transfers between devices: 36.6 us -> 29.1 us
  matrix products: 22.7 us -> 29.7 us
  other arithmetic: 22.8 us -> 19.3 us
    all_to_all x2 -> x1, waiting for transfers between devices: 75.6 us -> 28.6 us  [carried_both(): lax.all_to_all(jnp.stack([fwd, bwd], 1).reshape(count, -1, lanes), axis,...]
    all_to_all x0 -> x1, blocking collectives: none -> 41.1 us  [carried_both(): got = lax.all_to_all(packed, axis, 0, 0, tiled=True)]
    reshape x0 -> x3, local copies, waits for them, and re-layouts: none -> 9.69 us  [the longest x1 3.37 us: carried_both(): jnp.stack([fwd, bwd], 1).reshape(count, -1, lanes)]
    slice x1 -> x3, local copies, waits for them, and re-layouts: 0.17 us -> 9.39 us  [carried_both(): return (back[0], back[1])]
    all_to_all x2 -> x1, starting transfers between devices: 13.1 us -> 5.81 us  [carried_both(): lax.all_to_all(jnp.stack([fwd, bwd], 1).reshape(count, -1, lanes), axis,...]
    all_to_all x1 -> x0, other arithmetic: 5.37 us -> none  [carried_both(): back = lax.all_to_all(jnp.stack([fwd, bwd], 1), axis, 0, 0, tiled=True)]
    convert_element_type x2 -> x1, other arithmetic: 4.5 us -> 1.08 us  [body(): (dout_vals.astype(jnp.float32) * jax.nn.silu(gate_vals.astype(jnp.float32...]
    transpose x2 -> x0, local copies, waits for them, and re-layouts: 3.25 us -> none  [the longest x1 1.77 us: carried_both(): back = back.transpose(1, 2, 0, 3).reshape(2, rows, cols)]
  transfers between devices with their start and end apart: 6 -> 5, of which waited for: 5 -> 4; matrix products, arithmetic and copies ran while one was open for 13% -> 10% of each run, Pallas kernels for 0% -> 0%
where the time goes in v5:
time: 306 us; the launch traced here: 304 us
  waiting for transfers between devices  90 us (29%)
  local copies, waits for them, and re-layouts  63.5 us (21%)
  blocking collectives  58.4 us (19%)
  matrix products  29.7 us (10%)
  starting transfers between devices  29.1 us (10%)
  other arithmetic  19.3 us (6%)
  between operations  14.3 us (5%)
    all_to_all x1, waiting for transfers between devices, body(): lax.all_to_all(proj_terms.reshape(outer_count, inner_count, -1, col_count...  47.2 us
    all_to_all x1, blocking collectives, carried_both(): got = lax.all_to_all(packed, axis, 0, 0, tiled=True)  41.1 us
    all_to_all x1, waiting for transfers between devices, carried_both(): lax.all_to_all(jnp.stack([fwd, bwd], 1).reshape(count, -1, lanes), axis,...  28.6 us
    unnamed x43, local copies, waits for them, and re-layouts  20.9 us
    all_to_all x1, blocking collectives, body(): lax.all_to_all(jnp.broadcast_to(weight_local[None], (inner_count,) + weig...  17.4 us
    all_to_all x1, waiting for transfers between devices, body(): lax.all_to_all(jnp.broadcast_to(weight_inner[None], (outer_count,) + weig...  13.6 us
    all_to_all x1, starting transfers between devices, body(): proj_parts = lax.all_to_all(proj_parts, INNER, 0, 0, tiled=True)  10 us
    slice x3, local copies, waits for them, and re-layouts, carried_both(): return (back[0], back[1])  9.39 us
  transfers between devices with their start and end apart: 5, of which 4 were waited for; matrix products, arithmetic and copies ran while one was open for 10% of the time, Pallas kernels for 0%

profile of v5, /device:TPU:24, one launch (start us, length us, event | category | flops | bytes accessed | tf_op | source)
XLA Modules:
  0.0 304.4 jit_solution(17384952718105391752)
XLA Ops:
  8.0 17.4 %all_to_all.30 = bf16[8,32,256]{2,1,0:T(8,128)(2,1)S(1)} all-to-all(bf16[8,32,256]{2,1,0:T(8,128)(2,1)S(1)} %broadcast_in_dim.86), channel_id=1, replica_groups=mesh['dp'=2,'ylo'=2,'x'=4,'z'=8,'head'=2] {'z'}, dimensions={0} | all-to-all | bytes 262144 | tf_op jit(solution)/shard_map/all_to_all | solution.py:152
  27.0 7.3 %all-to-all-start.1 = ((bf16[16,8,32,256]{3,2,1,0:T(8,128)(2,1)}), bf16[16,8,32,256]{3,2,1,0:T(8,128)(2,1)S(1)}, u32[]{:S(2)}, u32[]{:S(2)}) async-start(bf16[16,8,32,256]{3,2,1,0:T(8,128)(2,1)} %broadcast_in_dim.87), calls=%async_computation.1 | async-start | bytes 4194304 | tf_op jit(solution)/shard_map/all_to_all | solution.py:159
  46.8 13.6 %all-to-all-done.1 = bf16[16,8,32,256]{3,2,1,0:T(8,128)(2,1)S(1)} async-done(((bf16[16,8,32,256]{3,2,1,0:T(8,128)(2,1)}), bf16[16,8,32,256]{3,2,1,0:T(8,128)(2,1)S(1)}, u32[]{:S(2)}, u32[]{:S(2)}) %all-to-all-start.1) | async-done | bytes 2097184 | tf_op jit(solution)/shard_map/all_to_all | solution.py:159
  63.7 3.1 %copy.90 = f32[1,64,64,32]{2,3,1,0:T(8,128)} copy(f32[1,64,64,32]{1,3,2,0:T(8,128)} %bitcast.177) | data formatting | bytes 1048576 | tf_op jit(solution)/shard_map/reshape | solution.py:68
  69.5 3.2 %copy.91 = f32[1,64,64,32]{2,3,1,0:T(8,128)} copy(f32[1,64,64,32]{1,3,2,0:T(8,128)} %bitcast.178) | data formatting | bytes 1048576 | tf_op jit(solution)/shard_map/reshape | solution.py:68
  76.2 3.2 %copy.92 = f32[64,33,128]{2,1,0:T(8,128)} copy(f32[64,33,128]{0,2,1:T(8,128)} %pad_maximum_fusion) | data formatting | bytes 2162688 | tf_op jit(solution)/shard_map/concatenate | solution.py:25
  79.4 41.1 %all_to_all.31 = f32[64,33,128]{2,1,0:T(8,128)S(1)} all-to-all(f32[64,33,128]{2,1,0:T(8,128)} %copy.92), channel_id=1, replica_groups=mesh['dp'=2,'ylo'=2,'x'=4,'z'=8,'head'=2] {'ylo','x','z'}, dimensions={0} | all-to-all | bytes 2162688 | tf_op jit(solution)/shard_map/all_to_all | solution.py:28
  122.4 3.2 %copy.115 = f32[64,32,128]{0,2,1:T(8,128)} copy(f32[64,32,128]{2,1,0:T(8,128)} %slice.52) | data formatting | bytes 2097152
  125.6 3.0 fusion.54
  139.0 3.8 %copy.97 = f32[64,2,64,32]{0,3,2,1:T(8,128)} copy(f32[64,2,64,32]{2,0,3,1:T(8,128)} %pad_maximum_fusion.2) | data formatting | bytes 2097152 | tf_op jit(solution)/shard_map/stack | solution.py:42
  142.8 3.4 %copy.98 = f32[64,32,128]{2,1,0:T(8,128)} copy(f32[64,32,128]{0,2,1:T(8,128)} %bitcast.172) | data formatting | bytes 2097152 | tf_op jit(solution)/shard_map/reshape | solution.py:42
  146.2 5.8 %all-to-all-start.3 = ((f32[64,32,128]{2,1,0:T(8,128)}), f32[64,32,128]{2,1,0:T(8,128)}, u32[]{:S(2)}, u32[]{:S(2)}) async-start(f32[64,32,128]{2,1,0:T(8,128)} %copy.98), calls=%async_computation.3 | async-start | bytes 2097152 | tf_op jit(solution)/shard_map/all_to_all | solution.py:41
  152.0 28.6 %all-to-all-done.3 = f32[64,32,128]{2,1,0:T(8,128)} async-done(((f32[64,32,128]{2,1,0:T(8,128)}), f32[64,32,128]{2,1,0:T(8,128)}, u32[]{:S(2)}, u32[]{:S(2)}) %all-to-all-start.3) | async-done | bytes 1048608 | tf_op jit(solution)/shard_map/all_to_all | solution.py:41
  180.6 3.2 %copy.99 = f32[64,32,128]{0,2,1:T(8,128)} copy(f32[64,32,128]{2,1,0:T(8,128)} %all-to-all-done.3) | data formatting | bytes 2097152 | tf_op jit(solution)/shard_map/all_to_all | solution.py:41
  183.8 3.0 fusion.53
  186.9 3.2 %copy.100 = f32[1,64,64,32]{1,3,2,0:T(8,128)} copy(f32[1,64,64,32]{2,3,1,0:T(8,128)} %get-tuple-element.24) | data formatting | bytes 1048576 | tf_op jit(solution)/shard_map/slice | solution.py:46
  194.8 3.2 %copy.102 = f32[1,64,64,32]{1,3,2,0:T(8,128)} copy(f32[1,64,64,32]{2,3,1,0:T(8,128)} %get-tuple-element.25) | data formatting | bytes 1048576 | tf_op jit(solution)/shard_map/slice | solution.py:46
  198.0 3.3 %convolution_bitcast_fusion.5 = f32[2,64,128]{2,1,0:T(8,128)S(1)} fusion(f32[64,2,16,64]{0,3,2,1:T(8,128)} %bitcast.159, bf16[128,2,16,64]{0,3,2,1:T(8,128)(2,1)} %multiply_convert_fusion, f32[128,2,16]{0,2,1:T(8,128)S(1)} %bitcast.194), kind=kOutput, calls=%fused_computation.24 | convolution fusion | flops 201850880 | bytes 1130496 | tf_op jit(solution)/shard_map/tgkp,ngkp->tgn/dot_general | solution.py:134
  208.4 5.6 %copy.104 = f32[4096,256]{1,0:T(8,128)} copy(f32[4096,256]{0,1:T(8,128)} %convolution_bitcast_fusion) | data formatting | bytes 8388608 | tf_op jit(solution)/shard_map/td,tc->dc/dot_general | solution.py:238
  214.1 6.0 %all-to-all-start.4 = ((f32[16,8,32,256]{3,2,1,0:T(8,128)}), f32[16,8,32,256]{3,2,1,0:T(8,128)}, u32[]{:S(2)}, u32[]{:S(2)}) async-start(f32[16,8,32,256]{3,2,1,0:T(8,128)} %bitcast.158), calls=%async_computation.5 | async-start | bytes 8388608 | tf_op jit(solution)/shard_map/all_to_all | solution.py:239
  226.0 47.2 %all-to-all-done.4 = f32[16,8,32,256]{3,2,1,0:T(8,128)} async-done(((f32[16,8,32,256]{3,2,1,0:T(8,128)}), f32[16,8,32,256]{3,2,1,0:T(8,128)}, u32[]{:S(2)}, u32[]{:S(2)}) %all-to-all-start.4) | async-done | bytes 4194336 | tf_op jit(solution)/shard_map/all_to_all | solution.py:239
  273.2 3.2 %reduce_sum.32 = f32[8,32,256]{2,1,0:T(8,128)} reduce(f32[16,8,32,256]{3,2,1,0:T(8,128)} %all-to-all-done.4, f32[]{:T(128)} %constant.14.clone.1), dimensions={0}, to_apply=%region_4.5 | reduce | flops 983040 | bytes 4456452 | tf_op jit(solution)/shard_map/reduce_sum | solution.py:241
  276.4 10.0 %all-to-all-start.5 = ((f32[8,32,256]{2,1,0:T(8,128)}), f32[8,32,256]{2,1,0:T(8,128)S(1)}, u32[]{:S(2)}, u32[]{:S(2)}) async-start(f32[8,32,256]{2,1,0:T(8,128)} %reduce_sum.32), calls=%async_computation.6 | async-start | bytes 524288 | tf_op jit(solution)/shard_map/all_to_all | solution.py:242
  290.9 3.5 %fusion.9 = bf16[128,32,64]{0,2,1:T(8,128)(2,1)} fusion(f32[128,32,64]{0,2,1:T(8,128)S(1)} %bitcast.165, f32[128,32,64]{0,2,1:T(8,128)} %bitcast_multiply_fusion.1, bf16[32,128,128]{2,1,0:T(8,128)(2,1)} %copy-done.10, bf16[128,32,64]{0,2,1:T(8,128)(2,1)} %bitcast.174, f32[128,32,64]{0,2,1:T(8,128)S(1)} %bitcast.168, f32[32]{0:T(128)S(1)} %copy-done.16), kind=kOutput, calls=%fused_computation.21 | convolution fusion | flops 70778880 | bytes 5243008 | tf_op jit(solution)/shard_map/hts,shp->thp/dot_general | solution.py:100
  (92 shorter events, 61.9 us)
Async XLA Ops:
  7.2 53.3 %copy-start = (bf16[1,128,4096]{2,1,0:T(8,128)(2,1)S(1)}, bf16[1,128,4096]{2,1,0:T(8,128)(2,1)}, u32[]{:S(2)}) copy-start(bf16[1,128,4096]{2,1,0:T(8,128)(2,1)} %param.7) | copy-start | bytes 3145732
  27.0 7.3 %copy-start.15 = (f32[1,32,128]{2,1,0:T(8,128)S(1)}, f32[1,32,128]{2,1,0:T(8,128)}, u32[]{:S(2)}) copy-start(f32[1,32,128]{2,1,0:T(8,128)} %param.11) | copy-start | bytes 49156
  27.0 33.5 %all-to-all-start.1 = ((bf16[16,8,32,256]{3,2,1,0:T(8,128)(2,1)}), bf16[16,8,32,256]{3,2,1,0:T(8,128)(2,1)S(1)}, u32[]{:S(2)}, u32[]{:S(2)}) async-start(bf16[16,8,32,256]{3,2,1,0:T(8,128)(2,1)} %broadcast_in_dim.87), calls=%async_computation.1 | async-start | bytes 4194304 | tf_op jit(solution)/shard_map/all_to_all | solution.py:159
  43.5 2.2 copy-start.3
  44.7 1.0 copy-start.6
  134.1 2.3 copy-start.11
  146.2 34.5 %all-to-all-start.3 = ((f32[64,32,128]{2,1,0:T(8,128)}), f32[64,32,128]{2,1,0:T(8,128)}, u32[]{:S(2)}, u32[]{:S(2)}) async-start(f32[64,32,128]{2,1,0:T(8,128)} %copy.98), calls=%async_computation.3 | async-start | bytes 2097152 | tf_op jit(solution)/shard_map/all_to_all | solution.py:41
  190.0 2.9 copy-start.2
  190.0 2.9 copy-start.8
  198.0 3.3 %copy-start.4 = (f32[1,128,2048]{1,2,0:T(8,128)S(1)}, f32[1,128,2048]{1,2,0:T(8,128)}, u32[]{:S(2)}) copy-start(f32[1,128,2048]{1,2,0:T(8,128)} %convert_element_type.117) | copy-start | bytes 3145732
  201.3 3.0 copy-start.9
  204.4 1.1 copy-start.13
  214.1 59.1 %all-to-all-start.4 = ((f32[16,8,32,256]{3,2,1,0:T(8,128)}), f32[16,8,32,256]{3,2,1,0:T(8,128)}, u32[]{:S(2)}, u32[]{:S(2)}) async-start(f32[16,8,32,256]{3,2,1,0:T(8,128)} %bitcast.158), calls=%async_computation.5 | async-start | bytes 8388608 | tf_op jit(solution)/shard_map/all_to_all | solution.py:239
  220.1 77.5 %reduce-scatter.2.cloned.1.call-start = ((), (), s32[]{:S(2)}) async-start(), calls=%async_computation.7 | async-start | bytes 1572864 | tf_op jit(solution)/shard_map/reduce_scatter | solution.py:234
  221.9 1.2 copy-start.1
  221.9 2.8 copy-start.16
  221.9 2.8 copy-start.12
  221.9 2.8 copy-start.14
  223.1 2.8 copy-start.10
  276.4 14.5 %copy-start.5 = (f32[1,128,2048]{1,2,0:T(8,128)S(1)}, f32[1,128,2048]{1,2,0:T(8,128)}, u32[]{:S(2)}) copy-start(f32[1,128,2048]{1,2,0:T(8,128)} %convert_element_type.117) | copy-start | bytes 3145732
  276.4 14.5 %copy-start.7 = (f32[1,128,2048]{1,2,0:T(8,128)S(1)}, f32[1,128,2048]{1,2,0:T(8,128)}, u32[]{:S(2)}) copy-start(f32[1,128,2048]{1,2,0:T(8,128)} %copy-done.6) | copy-start | bytes 3145732
  276.4 20.5 %all-to-all-start.5 = ((f32[8,32,256]{2,1,0:T(8,128)}), f32[8,32,256]{2,1,0:T(8,128)S(1)}, u32[]{:S(2)}, u32[]{:S(2)}) async-start(f32[8,32,256]{2,1,0:T(8,128)} %reduce_sum.32), calls=%async_computation.6 | async-start | bytes 524288 | tf_op jit(solution)/shard_map/all_to_all | solution.py:242
Sparse Core Ops, SparseCore 0:
  223.9 11.1 reduce-scatter.1

commit v6 on v4

--- a/solution.py
+++ b/solution.py
@@ -26,11 +26,12 @@
     got = lax.all_to_all(packed, axis, 0, 0, tiled=True)
     logs = got[:, 0, rows, 0]
     place = jnp.arange(count)
-    inside = (place[None, :, None] < place[None, None, :]) & (
-        place[None, None, :] < place[:, None, None]
-    )
-    gaps = jnp.sum(jnp.where(inside, logs[None, None, :], 0.0), axis=-1)
     before = place[None, :] < place[:, None]
+    gaps = jnp.dot(
+        jnp.where(before, logs[None, :], 0.0),
+        before.astype(jnp.float32),
+        precision=lax.Precision.HIGHEST,
+    )
     carry = jnp.where(before, jnp.exp(jnp.where(before, gaps, 0.0)), 0.0)
     fwd = jnp.einsum(
         "ik,knc->inc", carry, got[:, 0, :rows], precision=lax.Precision.HIGHEST
@@ -92,46 +93,54 @@
     c_wide = c_vals.astype(jnp.float32)
     cb_dots = jnp.einsum("tgn,sgn->gts", c_vals, b_vals, preferred_element_type=jnp.float32)
     mixer_bf = (decays * jnp.repeat(cb_dots, per_group, axis=0)).astype(jnp.bfloat16)
+    x_wide = x_vals.astype(jnp.float32)
+    dy_wide = dy_round.astype(jnp.float32)
+    y_local = (
+        jnp.einsum("hts,shp->thp", mixer_bf, x_vals, preferred_element_type=jnp.float32)
+        + skip_vals[None, :, None] * x_wide
+    )
+    vals_local = (
+        jnp.einsum("hts,thp->shp", mixer_bf, dy_round, preferred_element_type=jnp.float32)
+        + skip_vals[None, :, None] * dy_wide
+    )
+    mix_grad = (
+        jnp.einsum("thp,shp->hts", dy_round, x_vals, preferred_element_type=jnp.float32) * decays
+    )
+    dots_grad = (
+        mix_grad.reshape(group_count, per_group, block_len, block_len)
+        .sum(axis=1)
+        .astype(jnp.bfloat16)
+    )
+    c_local = jnp.einsum("gts,sgn->tgn", dots_grad, b_vals, preferred_element_type=jnp.float32)
+    b_local = jnp.einsum("gts,tgn->sgn", dots_grad, c_vals, preferred_element_type=jnp.float32)
+    (y_local, vals_local, c_local, b_local), state_in, adjoint_out = lax.optimization_barrier(
+        ((y_local, vals_local, c_local, b_local), state_in, adjoint_out)
+    )
     state_four = state_in.reshape(STATE, group_count, per_group, HEAD_DIM)
     adjoint_four = adjoint_out.reshape(STATE, group_count, per_group, HEAD_DIM)
-    y_intra = jnp.einsum("hts,shp->thp", mixer_bf, x_vals, preferred_element_type=jnp.float32)
     y_inter = jnp.einsum(
         "tgn,ngkp->tgkp", c_wide, state_four, precision=lax.Precision.HIGHEST
     ).reshape(block_len, head_count, HEAD_DIM)
-    x_wide = x_vals.astype(jnp.float32)
-    output_pre = y_intra + y_inter * from_start.T[:, :, None] + skip_vals[None, :, None] * x_wide
+    output_pre = y_local + y_inter * from_start.T[:, :, None]
     gate_wide = gate_vals.astype(jnp.float32)
     gate_sig = jax.nn.sigmoid(gate_wide)
     grad_gate = (
         dout_vals.astype(jnp.float32) * output_pre * gate_sig * (1.0 + gate_wide * (1.0 - gate_sig))
     ).astype(jnp.bfloat16)
-    dy_wide = dy_round.astype(jnp.float32)
     x_inter = jnp.einsum(
         "sgn,ngkp->sgkp", b_wide, adjoint_four, precision=lax.Precision.HIGHEST
     ).reshape(block_len, head_count, HEAD_DIM)
-    grad_vals = (
-        jnp.einsum("hts,thp->shp", mixer_bf, dy_round, preferred_element_type=jnp.float32)
-        + x_inter * to_end.T[:, :, None]
-        + skip_vals[None, :, None] * dy_wide
-    )
-    mix_grad = (
-        jnp.einsum("thp,shp->hts", dy_round, x_vals, preferred_element_type=jnp.float32) * decays
-    )
-    dots_grad = (
-        mix_grad.reshape(group_count, per_group, block_len, block_len)
-        .sum(axis=1)
-        .astype(jnp.bfloat16)
-    )
+    grad_vals = vals_local + x_inter * to_end.T[:, :, None]
     dy_scaled = (dy_wide * from_start.T[:, :, None]).reshape(
         block_len, group_count, per_group, HEAD_DIM
     )
     x_scaled = (x_wide * to_end.T[:, :, None]).reshape(block_len, group_count, per_group, HEAD_DIM)
-    c_grad = jnp.einsum(
-        "gts,sgn->tgn", dots_grad, b_vals, preferred_element_type=jnp.float32
-    ) + jnp.einsum("tgkp,ngkp->tgn", dy_scaled, state_four, precision=lax.Precision.HIGHEST)
-    b_grad = jnp.einsum(
-        "gts,tgn->sgn", dots_grad, c_vals, preferred_element_type=jnp.float32
-    ) + jnp.einsum("sgkp,ngkp->sgn", x_scaled, adjoint_four, precision=lax.Precision.HIGHEST)
+    c_grad = c_local + jnp.einsum(
+        "tgkp,ngkp->tgn", dy_scaled, state_four, precision=lax.Precision.HIGHEST
+    )
+    b_grad = b_local + jnp.einsum(
+        "sgkp,ngkp->sgn", x_scaled, adjoint_four, precision=lax.Precision.HIGHEST
+    )
     return (grad_vals.astype(jnp.bfloat16), grad_gate, jnp.stack([b_grad, c_grad], axis=1))
 
 

time: 289 us -> 284 us (0.983)
  blocking collectives: 17.4 us -> 74.3 us
  waiting for transfers between devices: 133 us -> 82.2 us
  starting transfers between devices: 36.6 us -> 30.3 us
  local copies, waits for them, and re-layouts: 40.1 us -> 34.4 us
    all_to_all x0 -> x1, blocking collectives: none -> 56.9 us  [carried_both(): got = lax.all_to_all(packed, axis, 0, 0, tiled=True)]
    all_to_all x1 -> x0, waiting for transfers between devices: 50.8 us -> none  [carried_both(): got = lax.all_to_all(packed, axis, 0, 0, tiled=True)]
    all_to_all x1 -> x0, starting transfers between devices: 6.46 us -> none  [carried_both(): got = lax.all_to_all(packed, axis, 0, 0, tiled=True)]
    all_to_all x1, waiting for transfers between devices: 24.9 us -> 21.2 us  [carried_both(): back = lax.all_to_all(jnp.stack([fwd, bwd], 1), axis, 0, 0, tiled=True)]
    convert_element_type x0 -> x1, other arithmetic: none -> 3.52 us  [span_full(): grad_gate = (dout_vals.astype(jnp.float32) * output_pre * gate_sig * (1.0...]
    unnamed x40 -> x30, local copies, waits for them, and re-layouts: 21.1 us -> 19 us
  transfers between devices with their start and end apart: 6 -> 5, of which waited for: 5 -> 4; matrix products, arithmetic and copies ran while one was open for 13% -> 14% of each run, Pallas kernels for 0% -> 0%
where the time goes in v6:
time: 284 us; the launch traced here: 283 us
  waiting for transfers between devices  82.2 us (29%)
  blocking collectives  74.3 us (26%)
  local copies, waits for them, and re-layouts  34.4 us (12%)
  starting transfers between devices  30.3 us (11%)
  matrix products  23.9 us (8%)
  other arithmetic  23.2 us (8%)
  between operations  14.4 us (5%)
    all_to_all x1, blocking collectives, carried_both(): got = lax.all_to_all(packed, axis, 0, 0, tiled=True)  56.9 us
    all_to_all x1, waiting for transfers between devices, body(): lax.all_to_all(proj_terms.reshape(outer_count, inner_count, -1, col_count...  48 us
    all_to_all x1, waiting for transfers between devices, carried_both(): back = lax.all_to_all(jnp.stack([fwd, bwd], 1), axis, 0, 0, tiled=True)  21.2 us
    unnamed x30, local copies, waits for them, and re-layouts  19 us
    all_to_all x1, blocking collectives, body(): lax.all_to_all(jnp.broadcast_to(weight_local[None], (inner_count,) + weig...  17.4 us
    all_to_all x1, waiting for transfers between devices, body(): lax.all_to_all(jnp.broadcast_to(weight_inner[None], (outer_count,) + weig...  11.9 us
    all_to_all x1, starting transfers between devices, body(): proj_parts = lax.all_to_all(proj_parts, INNER, 0, 0, tiled=True)  10.1 us
    all_to_all x1, starting transfers between devices, body(): lax.all_to_all(jnp.broadcast_to(weight_inner[None], (outer_count,) + weig...  7.3 us
  transfers between devices with their start and end apart: 5, of which 4 were waited for; matrix products, arithmetic and copies ran while one was open for 14% of the time, Pallas kernels for 0%

profile of v6, /device:TPU:24, one launch (start us, length us, event | category | flops | bytes accessed | tf_op | source)
XLA Modules:
  0.0 282.7 jit_solution(4597258855531019670)
XLA Ops:
  8.0 17.4 %all_to_all.30 = bf16[8,32,256]{2,1,0:T(8,128)(2,1)S(1)} all-to-all(bf16[8,32,256]{2,1,0:T(8,128)(2,1)S(1)} %broadcast_in_dim.88), channel_id=1, replica_groups=mesh['dp'=2,'ylo'=2,'x'=4,'z'=8,'head'=2] {'z'}, dimensions={0} | all-to-all | bytes 262144 | tf_op jit(solution)/shard_map/all_to_all | solution.py:158
  27.0 7.3 %all-to-all-start.1 = ((bf16[16,8,32,256]{3,2,1,0:T(8,128)(2,1)}), bf16[16,8,32,256]{3,2,1,0:T(8,128)(2,1)S(1)}, u32[]{:S(2)}, u32[]{:S(2)}) async-start(bf16[16,8,32,256]{3,2,1,0:T(8,128)(2,1)} %broadcast_in_dim.89), calls=%async_computation.1 | async-start | bytes 4194304 | tf_op jit(solution)/shard_map/all_to_all | solution.py:165
  34.7 2.0 copy.57
  38.8 2.2 convert_element_type.119
  43.0 2.1 convert_element_type.120
  45.9 2.6 multiply_convert_fusion
  48.5 11.9 %all-to-all-done.1 = bf16[16,8,32,256]{3,2,1,0:T(8,128)(2,1)S(1)} async-done(((bf16[16,8,32,256]{3,2,1,0:T(8,128)(2,1)}), bf16[16,8,32,256]{3,2,1,0:T(8,128)(2,1)S(1)}, u32[]{:S(2)}, u32[]{:S(2)}) %all-to-all-start.1) | async-done | bytes 2097184 | tf_op jit(solution)/shard_map/all_to_all | solution.py:165
  65.3 56.9 %all_to_all.31 = f32[64,2,65,32]{2,3,1,0:T(8,128)S(1)} all-to-all(f32[64,2,65,32]{2,3,1,0:T(8,128)S(1)} %copy.61), channel_id=1, replica_groups=mesh['dp'=2,'ylo'=2,'x'=4,'z'=8,'head'=2] {'ylo','x','z'}, dimensions={0} | all-to-all | bytes 2129920 | tf_op jit(solution)/shard_map/all_to_all | solution.py:26
  127.1 2.6 copy.89
  129.7 3.4 %reshape.187 = f32[64,1,4096]{2,1,0:T(1,128)} reshape(f32[64,2,32,64]{3,2,1,0:T(8,128)} %bitcast.194) | data formatting | bytes 2097152
  133.1 6.6 %all-to-all-start.3 = ((f32[64,1,4096]{2,1,0:T(1,128)}), f32[64,1,4096]{2,1,0:T(1,128)}, u32[]{:S(2)}, u32[]{:S(2)}) async-start(f32[64,1,4096]{2,1,0:T(1,128)} %reshape.187), calls=%async_computation.3 | async-start | bytes 2097152 | tf_op jit(solution)/shard_map/all_to_all | solution.py:42
  147.2 21.2 %all-to-all-done.3 = f32[64,1,4096]{2,1,0:T(1,128)} async-done(((f32[64,1,4096]{2,1,0:T(1,128)}), f32[64,1,4096]{2,1,0:T(1,128)}, u32[]{:S(2)}, u32[]{:S(2)}) %all-to-all-start.3) | async-done | bytes 1048608 | tf_op jit(solution)/shard_map/all_to_all | solution.py:42
  168.9 5.4 %reduce.7 = f32[64,4096]{1,0:T(8,128)} reduce(f32[64,1,4096]{2,1,0:T(1,128)} %all-to-all-done.3, f32[]{:T(128)} %broadcast.66), dimensions={1}, to_apply=%all_to_all.21.reduce_sub_computation | reduce | bytes 2097156 | tf_op jit(solution)/shard_map/all_to_all | solution.py:42
  174.3 3.1 %reshape.188 = f32[64,2,32,64]{3,2,1,0:T(8,128)} reshape(f32[64,4096]{1,0:T(8,128)} %reduce.7) | data formatting | bytes 2097152
  184.1 2.6 convolution_bitcast_fusion
  186.8 5.6 %copy.68 = f32[4096,256]{1,0:T(8,128)} copy(f32[4096,256]{0,1:T(8,128)} %convolution_bitcast_fusion) | data formatting | bytes 8388608 | tf_op jit(solution)/shard_map/td,tc->dc/dot_general | solution.py:244
  192.4 6.0 %all-to-all-start.4 = ((f32[16,8,32,256]{3,2,1,0:T(8,128)}), f32[16,8,32,256]{3,2,1,0:T(8,128)}, u32[]{:S(2)}, u32[]{:S(2)}) async-start(f32[16,8,32,256]{3,2,1,0:T(8,128)} %bitcast.185), calls=%async_computation.5 | async-start | bytes 8388608 | tf_op jit(solution)/shard_map/all_to_all | solution.py:245
  200.5 2.8 fusion.29
  203.4 48.0 %all-to-all-done.4 = f32[16,8,32,256]{3,2,1,0:T(8,128)} async-done(((f32[16,8,32,256]{3,2,1,0:T(8,128)}), f32[16,8,32,256]{3,2,1,0:T(8,128)}, u32[]{:S(2)}, u32[]{:S(2)}) %all-to-all-start.4) | async-done | bytes 4194336 | tf_op jit(solution)/shard_map/all_to_all | solution.py:245
  251.4 3.2 %reduce_sum.32 = f32[8,32,256]{2,1,0:T(8,128)} reduce(f32[16,8,32,256]{3,2,1,0:T(8,128)} %all-to-all-done.4, f32[]{:T(128)} %constant.9.clone.1), dimensions={0}, to_apply=%region_4.5 | reduce | flops 983040 | bytes 4456452 | tf_op jit(solution)/shard_map/reduce_sum | solution.py:247
  254.6 10.1 %all-to-all-start.5 = ((f32[8,32,256]{2,1,0:T(8,128)}), f32[8,32,256]{2,1,0:T(8,128)S(1)}, u32[]{:S(2)}, u32[]{:S(2)}) async-start(f32[8,32,256]{2,1,0:T(8,128)} %reduce_sum.32), calls=%async_computation.6 | async-start | bytes 524288 | tf_op jit(solution)/shard_map/all_to_all | solution.py:248
  266.6 3.5 %fusion.17 = (bf16[128,32,64]{0,2,1:T(8,128)(2,1)}, bf16[128,32,64]{0,2,1:T(8,128)(2,1)}) fusion(f32[128,32,64]{0,2,1:T(8,128)S(1)} %bitcast.181, f32[128,32,64]{0,2,1:T(8,128)} %fusion.3, f32[2,16,64,128]{3,2,1,0:T(8,128)} %fusion.29, f32[128,32,64]{0,2,1:T(8,128)S(1)} %bitcast.184, f32[128,32]{0,1:T(8,128)S(1)} %get-tuple-element.36, ...), kind=kLoop, calls=%fused_computation.37 | loop fusion | flops 3932160 | bytes 7372800 | tf_op jit(solution)/shard_map/convert_element_type | solution.py:129
  270.1 2.0 copy.69
  272.1 2.0 copy.70
  (78 shorter events, 37.6 us)
Async XLA Ops:
  7.2 53.3 %copy-start = (bf16[1,128,4096]{2,1,0:T(8,128)(2,1)S(1)}, bf16[1,128,4096]{2,1,0:T(8,128)(2,1)}, u32[]{:S(2)}) copy-start(bf16[1,128,4096]{2,1,0:T(8,128)(2,1)} %param.7) | copy-start | bytes 3145732
  27.0 7.3 %copy-start.9 = (f32[1,32,128]{2,1,0:T(8,128)S(1)}, f32[1,32,128]{2,1,0:T(8,128)}, u32[]{:S(2)}) copy-start(f32[1,32,128]{2,1,0:T(8,128)} %param.11) | copy-start | bytes 49156
  27.0 33.5 %all-to-all-start.1 = ((bf16[16,8,32,256]{3,2,1,0:T(8,128)(2,1)}), bf16[16,8,32,256]{3,2,1,0:T(8,128)(2,1)S(1)}, u32[]{:S(2)}, u32[]{:S(2)}) async-start(bf16[16,8,32,256]{3,2,1,0:T(8,128)(2,1)} %broadcast_in_dim.89), calls=%async_computation.1 | async-start | bytes 4194304 | tf_op jit(solution)/shard_map/all_to_all | solution.py:165
  62.7 1.0 copy-start.5
  133.1 35.3 %all-to-all-start.3 = ((f32[64,1,4096]{2,1,0:T(1,128)}), f32[64,1,4096]{2,1,0:T(1,128)}, u32[]{:S(2)}, u32[]{:S(2)}) async-start(f32[64,1,4096]{2,1,0:T(1,128)} %reshape.187), calls=%async_computation.3 | async-start | bytes 2097152 | tf_op jit(solution)/shard_map/all_to_all | solution.py:42
  139.7 1.9 copy-start.6
  141.6 2.4 copy-start.10
  179.2 1.0 copy-start.8
  179.3 2.9 %copy-start.7 = (bf16[1,128,2048]{1,2,0:T(8,128)(2,1)S(1)}, bf16[1,128,2048]{1,2,0:T(8,128)(2,1)}, u32[]{:S(2)}) copy-start(bf16[1,128,2048]{1,2,0:T(8,128)(2,1)} %copy.57) | copy-start | bytes 1572868
  179.5 2.7 copy-start.3
  179.5 4.6 %copy-start.4 = (f32[1,64,64,32]{1,3,0,2:T(8,128)}, f32[1,64,64,32]{1,3,0,2:T(8,128)S(1)}, u32[]{:S(2)}) copy-start(f32[1,64,64,32]{1,3,0,2:T(8,128)S(1)} %get-tuple-element.33) | copy-start | bytes 1572868
  192.4 59.0 %all-to-all-start.4 = ((f32[16,8,32,256]{3,2,1,0:T(8,128)}), f32[16,8,32,256]{3,2,1,0:T(8,128)}, u32[]{:S(2)}, u32[]{:S(2)}) async-start(f32[16,8,32,256]{3,2,1,0:T(8,128)} %bitcast.185), calls=%async_computation.5 | async-start | bytes 8388608 | tf_op jit(solution)/shard_map/all_to_all | solution.py:245
  198.3 77.5 %reduce-scatter.2.cloned.1.call-start = ((), (), s32[]{:S(2)}) async-start(), calls=%async_computation.7 | async-start | bytes 1572864 | tf_op jit(solution)/shard_map/reduce_scatter | solution.py:240
  254.6 12.0 %copy-start.1 = (f32[1,128,2048]{1,2,0:T(8,128)S(1)}, f32[1,128,2048]{1,2,0:T(8,128)}, u32[]{:S(2)}) copy-start(f32[1,128,2048]{1,2,0:T(8,128)} %convert_element_type.119) | copy-start | bytes 3145732
  254.6 12.0 %copy-start.2 = (f32[1,128,2048]{1,2,0:T(8,128)S(1)}, f32[1,128,2048]{1,2,0:T(8,128)}, u32[]{:S(2)}) copy-start(f32[1,128,2048]{1,2,0:T(8,128)} %convert_element_type.120) | copy-start | bytes 3145732
  254.6 20.6 %all-to-all-start.5 = ((f32[8,32,256]{2,1,0:T(8,128)}), f32[8,32,256]{2,1,0:T(8,128)S(1)}, u32[]{:S(2)}, u32[]{:S(2)}) async-start(f32[8,32,256]{2,1,0:T(8,128)} %reduce_sum.32), calls=%async_computation.6 | async-start | bytes 524288 | tf_op jit(solution)/shard_map/all_to_all | solution.py:248
Sparse Core Ops, SparseCore 0:
  202.2 11.2 reduce-scatter.1

commit v7 on v6

--- a/solution.py
+++ b/solution.py
@@ -16,32 +16,35 @@
 def carried_both(log_total, state, adjoint, axis):
     count = lax.axis_size(axis)
     rows, cols = state.shape
-    chunk = cols // count
-    assert HEAD_DIM % chunk == 0
-    log_row = jnp.repeat(log_total, cols // log_total.shape[0])[None, :]
+    share = rows // count
+    heads = log_total.shape[0]
+    log_row = jnp.repeat(log_total, cols // heads)[None, None, :]
     packed = jnp.concatenate(
-        [jnp.concatenate([state, log_row], 0)[None], jnp.pad(adjoint, ((0, 1), (0, 0)))[None]], 0
-    )
-    packed = packed.reshape(2, rows + 1, count, chunk).transpose(2, 0, 1, 3)
+        [
+            state.reshape(count, share, cols),
+            adjoint.reshape(count, share, cols),
+            jnp.broadcast_to(log_row, (count, 1, cols)),
+        ],
+        1,
+    )
     got = lax.all_to_all(packed, axis, 0, 0, tiled=True)
-    logs = got[:, 0, rows, 0]
+    logs = got[:, 2 * share, :: cols // heads]
     place = jnp.arange(count)
     before = place[None, :] < place[:, None]
-    gaps = jnp.dot(
-        jnp.where(before, logs[None, :], 0.0),
+    gaps = jnp.einsum(
+        "him,mk->hik",
+        jnp.where(before[None], logs.T[:, None, :], 0.0),
         before.astype(jnp.float32),
         precision=lax.Precision.HIGHEST,
     )
-    carry = jnp.where(before, jnp.exp(jnp.where(before, gaps, 0.0)), 0.0)
-    fwd = jnp.einsum(
-        "ik,knc->inc", carry, got[:, 0, :rows], precision=lax.Precision.HIGHEST
-    )
-    bwd = jnp.einsum(
-        "ki,knc->inc", carry, got[:, 1, :rows], precision=lax.Precision.HIGHEST
-    )
-    back = lax.all_to_all(jnp.stack([fwd, bwd], 1), axis, 0, 0, tiled=True)
-    back = back.transpose(1, 2, 0, 3).reshape(2, rows, cols)
-    return back[0], back[1]
+    carry = jnp.where(before[None], jnp.exp(jnp.where(before[None], gaps, 0.0)), 0.0)
+    parts = got[:, : 2 * share].reshape(count, 2, share, heads, cols // heads)
+    fwd = jnp.einsum("hik,krhp->irhp", carry, parts[:, 0], precision=lax.Precision.HIGHEST)
+    bwd = jnp.einsum("hki,krhp->irhp", carry, parts[:, 1], precision=lax.Precision.HIGHEST)
+    back = lax.all_to_all(
+        jnp.stack([fwd, bwd], 1).reshape(count, 2, share, cols), axis, 0, 0, tiled=True
+    )
+    return back[:, 0].reshape(rows, cols), back[:, 1].reshape(rows, cols)
 
 
 def span_summary(b_vals, c_vals, x_vals, dy_round, rate_vals):

time: 284 us -> 306 us (1.077)
  blocking collectives: 74.3 us -> 17.4 us
  waiting for transfers between devices: 82.2 us -> 133 us
  local copies, waits for them, and re-layouts: 34.4 us -> 48.3 us
  matrix products: 23.9 us -> 32.8 us
  starting transfers between devices: 30.3 us -> 36.5 us
    all_to_all x1 -> x0, blocking collectives: 56.9 us -> none  [carried_both(): got = lax.all_to_all(packed, axis, 0, 0, tiled=True)]
    all_to_all x1 -> x2, waiting for transfers between devices: 21.2 us -> 72 us  [the longest x1 50.8 us: carried_both(): got = lax.all_to_all(packed, axis, 0, 0, tiled=True)]
    slice x3 -> x4, local copies, waits for them, and re-layouts: 1.33 us -> 11.3 us  [the longest x2 5.7 us: carried_both(): parts = got[:, :2 * share].reshape(count, 2, share, heads, cols // heads)]
    reshape x0 -> x4, local copies, waits for them, and re-layouts: none -> 9.47 us  [the longest x1 2.41 us: span_full(): state_four = state_in.reshape(STATE, group_count, per_group, HEAD_DIM)]
    unnamed x30 -> x25, local copies, waits for them, and re-layouts: 19 us -> 12.3 us
    all_to_all x1 -> x2, starting transfers between devices: 6.61 us -> 13.1 us  [the longest x1 6.61 us: carried_both(): lax.all_to_all(jnp.stack([fwd, bwd], 1).reshape(count, 2, share, cols), a...]
    all_to_all x1 -> x0, other arithmetic: 5.36 us -> none  [carried_both(): back = lax.all_to_all(jnp.stack([fwd, bwd], 1), axis, 0, 0, tiled=True)]
    dot_general x3, matrix products: 3.38 us -> 6.83 us  [the longest x1 3.38 us: carried_both(): jnp.einsum('hki,krhp->irhp', carry, parts[:, 1], precision=lax.Precision....]
  transfers between devices with their start and end apart: 5 -> 6, of which waited for: 4 -> 5; matrix products, arithmetic and copies ran while one was open for 14% -> 13% of each run, Pallas kernels for 0% -> 0%
where the time goes in v7:
time: 306 us; the launch traced here: 304 us
  waiting for transfers between devices  133 us (43%)
  local copies, waits for them, and re-layouts  48.3 us (16%)
  starting transfers between devices  36.5 us (12%)
  matrix products  32.8 us (11%)
  other arithmetic  21.6 us (7%)
  blocking collectives  17.4 us (6%)
  between operations  14.3 us (5%)
    all_to_all x1, waiting for transfers between devices, carried_both(): got = lax.all_to_all(packed, axis, 0, 0, tiled=True)  50.8 us
    all_to_all x1, waiting for transfers between devices, body(): lax.all_to_all(proj_terms.reshape(outer_count, inner_count, -1, col_count...  48.2 us
    all_to_all x1, waiting for transfers between devices, carried_both(): lax.all_to_all(jnp.stack([fwd, bwd], 1).reshape(count, 2, share, cols), a...  21.2 us
    all_to_all x1, blocking collectives, body(): lax.all_to_all(jnp.broadcast_to(weight_local[None], (inner_count,) + weig...  17.4 us
    unnamed x25, local copies, waits for them, and re-layouts  12.3 us
    all_to_all x1, waiting for transfers between devices, body(): lax.all_to_all(jnp.broadcast_to(weight_inner[None], (outer_count,) + weig...  12.2 us
    all_to_all x1, starting transfers between devices, body(): proj_parts = lax.all_to_all(proj_parts, INNER, 0, 0, tiled=True)  10.1 us
    all_to_all x1, starting transfers between devices, body(): lax.all_to_all(jnp.broadcast_to(weight_inner[None], (outer_count,) + weig...  7.3 us
  transfers between devices with their start and end apart: 6, of which 5 were waited for; matrix products, arithmetic and copies ran while one was open for 13% of the time, Pallas kernels for 0%

profile of v7, /device:TPU:24, one launch (start us, length us, event | category | flops | bytes accessed | tf_op | source)
XLA Modules:
  0.0 303.9 jit_solution(11880812544899392233)
XLA Ops:
  8.0 17.4 %all_to_all.30 = bf16[8,32,256]{2,1,0:T(8,128)(2,1)S(1)} all-to-all(bf16[8,32,256]{2,1,0:T(8,128)(2,1)S(1)} %broadcast_in_dim.110), channel_id=1, replica_groups=mesh['dp'=2,'ylo'=2,'x'=4,'z'=8,'head'=2] {'z'}, dimensions={0} | all-to-all | bytes 262144 | tf_op jit(solution)/shard_map/all_to_all | solution.py:161
  27.0 7.3 %all-to-all-start.1 = ((bf16[16,8,32,256]{3,2,1,0:T(8,128)(2,1)}), bf16[16,8,32,256]{3,2,1,0:T(8,128)(2,1)S(1)}, u32[]{:S(2)}, u32[]{:S(2)}) async-start(bf16[16,8,32,256]{3,2,1,0:T(8,128)(2,1)} %broadcast_in_dim.111), calls=%async_computation.1 | async-start | bytes 4194304 | tf_op jit(solution)/shard_map/all_to_all | solution.py:168
  48.2 12.2 %all-to-all-done.1 = bf16[16,8,32,256]{3,2,1,0:T(8,128)(2,1)S(1)} async-done(((bf16[16,8,32,256]{3,2,1,0:T(8,128)(2,1)}), bf16[16,8,32,256]{3,2,1,0:T(8,128)(2,1)S(1)}, u32[]{:S(2)}, u32[]{:S(2)}) %all-to-all-start.1) | async-done | bytes 2097184 | tf_op jit(solution)/shard_map/all_to_all | solution.py:168
  61.0 2.7 fusion.21
  74.8 6.5 %all-to-all-start.2 = ((f32[64,3,2048]{2,1,0:T(4,128)}), f32[64,3,2048]{2,1,0:T(4,128)}, u32[]{:S(2)}, u32[]{:S(2)}) async-start(f32[64,3,2048]{2,1,0:T(4,128)} %copy.77), calls=%async_computation.2 | async-start | bytes 4194304 | tf_op jit(solution)/shard_map/all_to_all | solution.py:30
  81.3 50.8 %all-to-all-done.2 = f32[64,3,2048]{2,1,0:T(4,128)} async-done(((f32[64,3,2048]{2,1,0:T(4,128)}), f32[64,3,2048]{2,1,0:T(4,128)}, u32[]{:S(2)}, u32[]{:S(2)}) %all-to-all-start.2) | async-done | bytes 1572896 | tf_op jit(solution)/shard_map/all_to_all | solution.py:30
  132.1 3.0 slice.41
  135.1 3.0 slice.48
  138.1 2.7 copy.78
  141.5 3.4 %fusion.12 = f32[32,64,64]{2,1,0:T(8,128)} fusion(f32[32,64,64]{2,1,0:T(8,128)S(1)} %fusion.3, f32[64,2,1,32,64]{0,4,3,2,1:T(8,128)} %bitcast.191), kind=kOutput, calls=%fused_computation.27 | convolution fusion | flops 100663296 | bytes 2097152 | tf_op jit(solution)/shard_map/hki,krhp->irhp/dot_general | solution.py:43
  144.9 2.8 fusion.13
  151.9 3.1 %pad_maximum_fusion.1 = f32[64,2,1,2048]{3,1,2,0:T(2,128)} fusion(f32[64,1,1,2048]{3,1,2,0:T(1,128)} %copy.81, f32[64,1,1,2048]{3,1,2,0:T(1,128)} %copy.80), kind=kLoop, calls=%fused_computation.30 | loop fusion | flops 262144 | bytes 2097152 | tf_op jit(solution)/shard_map/stack | solution.py:45
  155.0 6.6 %all-to-all-start.3 = ((f32[64,2,1,2048]{3,1,2,0:T(2,128)}), f32[64,2,1,2048]{3,1,2,0:T(2,128)}, u32[]{:S(2)}, u32[]{:S(2)}) async-start(f32[64,2,1,2048]{3,1,2,0:T(2,128)} %pad_maximum_fusion.1), calls=%async_computation.3 | async-start | bytes 2097152 | tf_op jit(solution)/shard_map/all_to_all | solution.py:44
  169.1 21.2 %all-to-all-done.3 = f32[64,2,1,2048]{3,1,2,0:T(2,128)} async-done(((f32[64,2,1,2048]{3,1,2,0:T(2,128)}), f32[64,2,1,2048]{3,1,2,0:T(2,128)}, u32[]{:S(2)}, u32[]{:S(2)}) %all-to-all-start.3) | async-done | bytes 1048608 | tf_op jit(solution)/shard_map/all_to_all | solution.py:44
  190.3 2.7 fusion.56
  199.1 3.3 %fusion.11 = bf16[128,1,2,64]{0,3,2,1:T(8,128)(2,1)S(1)} fusion(f32[128,2,64]{0,2,1:T(8,128)S(1)} %convolution_bitcast_fusion.6, f32[64,2,16,64]{0,3,2,1:T(8,128)} %bitcast.187, bf16[128,2,16,64]{0,3,2,1:T(8,128)(2,1)} %multiply_convert_fusion, f32[128,2,16]{0,2,1:T(8,128)S(1)} %bitcast.216), kind=kOutput, calls=%fused_computation.25 | convolution fusion | flops 201883648 | bytes 1163264 | tf_op jit(solution)/shard_map/tgkp,ngkp->tgn/dot_general | solution.py:141
  202.4 2.9 fusion.10
  208.0 5.6 %copy.86 = f32[4096,256]{1,0:T(8,128)} copy(f32[4096,256]{0,1:T(8,128)} %convolution_bitcast_fusion) | data formatting | bytes 8388608 | tf_op jit(solution)/shard_map/td,tc->dc/dot_general | solution.py:247
  213.6 6.0 %all-to-all-start.4 = ((f32[16,8,32,256]{3,2,1,0:T(8,128)}), f32[16,8,32,256]{3,2,1,0:T(8,128)}, u32[]{:S(2)}, u32[]{:S(2)}) async-start(f32[16,8,32,256]{3,2,1,0:T(8,128)} %bitcast.180), calls=%async_computation.5 | async-start | bytes 8388608 | tf_op jit(solution)/shard_map/all_to_all | solution.py:248
  224.4 48.2 %all-to-all-done.4 = f32[16,8,32,256]{3,2,1,0:T(8,128)} async-done(((f32[16,8,32,256]{3,2,1,0:T(8,128)}), f32[16,8,32,256]{3,2,1,0:T(8,128)}, u32[]{:S(2)}, u32[]{:S(2)}) %all-to-all-start.4) | async-done | bytes 4194336 | tf_op jit(solution)/shard_map/all_to_all | solution.py:248
  272.6 3.2 %reduce_sum.32 = f32[8,32,256]{2,1,0:T(8,128)} reduce(f32[16,8,32,256]{3,2,1,0:T(8,128)} %all-to-all-done.4, f32[]{:T(128)} %constant.8.clone.1), dimensions={0}, to_apply=%region_4.5 | reduce | flops 983040 | bytes 4456452 | tf_op jit(solution)/shard_map/reduce_sum | solution.py:250
  275.8 10.1 %all-to-all-start.5 = ((f32[8,32,256]{2,1,0:T(8,128)}), f32[8,32,256]{2,1,0:T(8,128)S(1)}, u32[]{:S(2)}, u32[]{:S(2)}) async-start(f32[8,32,256]{2,1,0:T(8,128)} %reduce_sum.32), calls=%async_computation.6 | async-start | bytes 524288 | tf_op jit(solution)/shard_map/all_to_all | solution.py:251
  285.9 2.8 fusion.33
  290.7 2.9 fusion.18
  (76 shorter events, 59.5 us)
Async XLA Ops:
  7.2 53.3 %copy-start = (bf16[1,128,4096]{2,1,0:T(8,128)(2,1)S(1)}, bf16[1,128,4096]{2,1,0:T(8,128)(2,1)}, u32[]{:S(2)}) copy-start(bf16[1,128,4096]{2,1,0:T(8,128)(2,1)} %param.7) | copy-start | bytes 3145732
  27.0 7.3 %copy-start.7 = (f32[1,32,128]{2,1,0:T(8,128)S(1)}, f32[1,32,128]{2,1,0:T(8,128)}, u32[]{:S(2)}) copy-start(f32[1,32,128]{2,1,0:T(8,128)} %param.11) | copy-start | bytes 49156
  27.0 33.5 %all-to-all-start.1 = ((bf16[16,8,32,256]{3,2,1,0:T(8,128)(2,1)}), bf16[16,8,32,256]{3,2,1,0:T(8,128)(2,1)S(1)}, u32[]{:S(2)}, u32[]{:S(2)}) async-start(bf16[16,8,32,256]{3,2,1,0:T(8,128)(2,1)} %broadcast_in_dim.111), calls=%async_computation.1 | async-start | bytes 4194304 | tf_op jit(solution)/shard_map/all_to_all | solution.py:168
  74.8 57.2 %all-to-all-start.2 = ((f32[64,3,2048]{2,1,0:T(4,128)}), f32[64,3,2048]{2,1,0:T(4,128)}, u32[]{:S(2)}, u32[]{:S(2)}) async-start(f32[64,3,2048]{2,1,0:T(4,128)} %copy.77), calls=%async_computation.2 | async-start | bytes 4194304 | tf_op jit(solution)/shard_map/all_to_all | solution.py:30
  140.8 4.1 %copy-start.4 = (f32[64,2,2048]{0,2,1:T(8,128)S(1)}, f32[64,2,2048]{0,2,1:T(8,128)}, u32[]{:S(2)}) copy-start(f32[64,2,2048]{0,2,1:T(8,128)} %copy.78) | copy-start | bytes 3145732
  155.0 35.3 %all-to-all-start.3 = ((f32[64,2,1,2048]{3,1,2,0:T(2,128)}), f32[64,2,1,2048]{3,1,2,0:T(2,128)}, u32[]{:S(2)}, u32[]{:S(2)}) async-start(f32[64,2,1,2048]{3,1,2,0:T(2,128)} %pad_maximum_fusion.1), calls=%async_computation.3 | async-start | bytes 2097152 | tf_op jit(solution)/shard_map/all_to_all | solution.py:44
  161.6 1.9 copy-start.5
  163.6 2.4 copy-start.8
  199.1 3.3 %copy-start.3 = (f32[64,2048]{0,1:T(8,128)S(1)}, f32[64,2048]{0,1:T(8,128)}, u32[]{:S(2)}) copy-start(f32[64,2048]{0,1:T(8,128)} %copy.97) | copy-start | bytes 1572868
  213.6 59.0 %all-to-all-start.4 = ((f32[16,8,32,256]{3,2,1,0:T(8,128)}), f32[16,8,32,256]{3,2,1,0:T(8,128)}, u32[]{:S(2)}, u32[]{:S(2)}) async-start(f32[16,8,32,256]{3,2,1,0:T(8,128)} %bitcast.180), calls=%async_computation.5 | async-start | bytes 8388608 | tf_op jit(solution)/shard_map/all_to_all | solution.py:248
  219.6 77.5 %reduce-scatter.2.cloned.1.call-start = ((), (), s32[]{:S(2)}) async-start(), calls=%async_computation.7 | async-start | bytes 1572864 | tf_op jit(solution)/shard_map/reduce_scatter | solution.py:243
  221.4 2.0 copy-start.6
  275.8 14.9 %copy-start.1 = (f32[1,128,2048]{1,2,0:T(8,128)S(1)}, f32[1,128,2048]{1,2,0:T(8,128)}, u32[]{:S(2)}) copy-start(f32[1,128,2048]{1,2,0:T(8,128)} %convert_element_type.117) | copy-start | bytes 3145732
  275.8 14.9 %copy-start.2 = (f32[1,128,2048]{1,2,0:T(8,128)S(1)}, f32[1,128,2048]{1,2,0:T(8,128)}, u32[]{:S(2)}) copy-start(f32[1,128,2048]{1,2,0:T(8,128)} %convert_element_type.118) | copy-start | bytes 3145732
  275.8 20.6 %all-to-all-start.5 = ((f32[8,32,256]{2,1,0:T(8,128)}), f32[8,32,256]{2,1,0:T(8,128)S(1)}, u32[]{:S(2)}, u32[]{:S(2)}) async-start(f32[8,32,256]{2,1,0:T(8,128)} %reduce_sum.32), calls=%async_computation.6 | async-start | bytes 524288 | tf_op jit(solution)/shard_map/all_to_all | solution.py:251
Sparse Core Ops, SparseCore 0:
  223.4 11.1 reduce-scatter.1

commit v8 on v6

--- a/solution.py
+++ b/solution.py
@@ -241,11 +241,14 @@
         input_terms.astype(jnp.bfloat16), "head", scatter_dimension=1, tiled=True
     )[None]
     scale = 1.0 / (lax.axis_size(ROWS) * tok_rows)
-    proj_terms = jnp.einsum("td,tc->dc", tokens, grad_flat, preferred_element_type=jnp.float32)
+    proj_terms = jnp.einsum("tc,td->cd", grad_flat, tokens, preferred_element_type=jnp.float32)
     proj_parts = lax.all_to_all(
-        proj_terms.reshape(outer_count, inner_count, -1, col_count), OUTER, 0, 0, tiled=True
-    ).sum(axis=0)
-    proj_parts = lax.all_to_all(proj_parts, INNER, 0, 0, tiled=True)
+        proj_terms.reshape(col_count, outer_count, -1), OUTER, 1, 1, tiled=True
+    ).sum(axis=1)
+    proj_parts = lax.all_to_all(
+        proj_parts.reshape(col_count, inner_count, -1), INNER, 1, 1, tiled=True
+    )
+    proj_parts = proj_parts.sum(axis=1).T[None]
     grad_proj = proj_parts.sum(axis=0) * scale
     grad_proj = grad_proj.reshape(-1, 2, col_count // 2)
     return (grad_input, grad_values, grad_gate, grad_proj)

time: 284 us -> 279 us (0.982)
  local copies, waits for them, and re-layouts: 34.4 us -> 28.5 us
  waiting for transfers between devices: 82.2 us -> 87.8 us
  other arithmetic: 23.2 us -> 19.3 us
    all_to_all x2, waiting for transfers between devices: 49 us -> 53.1 us  [the longest x1 48.1 us: body(): lax.all_to_all(proj_terms.reshape(col_count, outer_count, -1), OUTER, 1,...]
    all_to_all x1, waiting for transfers between devices: 11.9 us -> 15.3 us  [body(): lax.all_to_all(jnp.broadcast_to(weight_inner[None], (outer_count,) + weig...]
    unnamed x30 -> x38, local copies, waits for them, and re-layouts: 19 us -> 15.7 us
    dot_general x1, local copies, waits for them, and re-layouts: 5.6 us -> 2.26 us  [body(): jnp.einsum('tc,td->cd', grad_flat, tokens, preferred_element_type=jnp.flo...]
  transfers between devices with their start and end apart: 5 -> 5, of which waited for: 4 -> 4; matrix products, arithmetic and copies ran while one was open for 14% -> 12% of each run, Pallas kernels for 0% -> 0%
where the time goes in v8:
time: 279 us; the launch traced here: 278 us
  waiting for transfers between devices  87.8 us (31%)
  blocking collectives  74.3 us (27%)
  starting transfers between devices  30.1 us (11%)
  local copies, waits for them, and re-layouts  28.5 us (10%)
  matrix products  23.8 us (9%)
  other arithmetic  19.3 us (7%)
  between operations  14.4 us (5%)
    all_to_all x1, blocking collectives, carried_both(): got = lax.all_to_all(packed, axis, 0, 0, tiled=True)  56.9 us
    all_to_all x1, waiting for transfers between devices, body(): lax.all_to_all(proj_terms.reshape(col_count, outer_count, -1), OUTER, 1,...  48.1 us
    all_to_all x1, waiting for transfers between devices, carried_both(): back = lax.all_to_all(jnp.stack([fwd, bwd], 1), axis, 0, 0, tiled=True)  19.3 us
    all_to_all x1, blocking collectives, body(): lax.all_to_all(jnp.broadcast_to(weight_local[None], (inner_count,) + weig...  17.4 us
    unnamed x38, local copies, waits for them, and re-layouts  15.7 us
    all_to_all x1, waiting for transfers between devices, body(): lax.all_to_all(jnp.broadcast_to(weight_inner[None], (outer_count,) + weig...  15.3 us
    all_to_all x1, starting transfers between devices, body(): lax.all_to_all(proj_parts.reshape(col_count, inner_count, -1), INNER, 1,...  9.95 us
    all_to_all x1, starting transfers between devices, body(): lax.all_to_all(jnp.broadcast_to(weight_inner[None], (outer_count,) + weig...  7.3 us
  transfers between devices with their start and end apart: 5, of which 4 were waited for; matrix products, arithmetic and copies ran while one was open for 12% of the time, Pallas kernels for 0%

profile of v8, /device:TPU:24, one launch (start us, length us, event | category | flops | bytes accessed | tf_op | source)
XLA Modules:
  0.0 278.2 jit_solution(17557747419275347208)
XLA Ops:
  7.9 17.4 %all_to_all.30 = bf16[8,32,256]{2,1,0:T(8,128)(2,1)S(1)} all-to-all(bf16[8,32,256]{2,1,0:T(8,128)(2,1)S(1)} %broadcast_in_dim.89), channel_id=1, replica_groups=mesh['dp'=2,'ylo'=2,'x'=4,'z'=8,'head'=2] {'z'}, dimensions={0} | all-to-all | bytes 262144 | tf_op jit(solution)/shard_map/all_to_all | solution.py:158
  26.9 7.3 %all-to-all-start.1 = ((bf16[16,8,32,256]{3,2,1,0:T(8,128)(2,1)}), bf16[16,8,32,256]{3,2,1,0:T(8,128)(2,1)S(1)}, u32[]{:S(2)}, u32[]{:S(2)}) async-start(bf16[16,8,32,256]{3,2,1,0:T(8,128)(2,1)} %broadcast_in_dim.90), calls=%async_computation.1 | async-start | bytes 4194304 | tf_op jit(solution)/shard_map/all_to_all | solution.py:165
  37.7 2.0 copy.45
  39.7 2.2 convert_element_type.120
  42.7 2.3 multiply_convert_fusion
  45.0 15.3 %all-to-all-done.1 = bf16[16,8,32,256]{3,2,1,0:T(8,128)(2,1)S(1)} async-done(((bf16[16,8,32,256]{3,2,1,0:T(8,128)(2,1)}), bf16[16,8,32,256]{3,2,1,0:T(8,128)(2,1)S(1)}, u32[]{:S(2)}, u32[]{:S(2)}) %all-to-all-start.1) | async-done | bytes 2097184 | tf_op jit(solution)/shard_map/all_to_all | solution.py:165
  66.4 56.9 %all_to_all.31 = f32[64,2,65,32]{2,3,1,0:T(8,128)S(1)} all-to-all(f32[64,2,65,32]{2,3,1,0:T(8,128)S(1)} %copy.47), channel_id=1, replica_groups=mesh['dp'=2,'ylo'=2,'x'=4,'z'=8,'head'=2] {'ylo','x','z'}, dimensions={0} | all-to-all | bytes 2129920 | tf_op jit(solution)/shard_map/all_to_all | solution.py:26
  128.2 2.6 copy.77
  130.7 3.5 %reshape.192 = f32[64,1,4096]{2,1,0:T(1,128)} reshape(f32[64,2,32,64]{3,2,1,0:T(8,128)} %bitcast.197) | data formatting | bytes 2097152
  134.2 6.6 %all-to-all-start.3 = ((f32[64,1,4096]{2,1,0:T(1,128)}), f32[64,1,4096]{2,1,0:T(1,128)}, u32[]{:S(2)}, u32[]{:S(2)}) async-start(f32[64,1,4096]{2,1,0:T(1,128)} %reshape.192), calls=%async_computation.3 | async-start | bytes 2097152 | tf_op jit(solution)/shard_map/all_to_all | solution.py:42
  140.8 2.3 copy.66
  150.2 19.3 %all-to-all-done.3 = f32[64,1,4096]{2,1,0:T(1,128)} async-done(((f32[64,1,4096]{2,1,0:T(1,128)}), f32[64,1,4096]{2,1,0:T(1,128)}, u32[]{:S(2)}, u32[]{:S(2)}) %all-to-all-start.3) | async-done | bytes 1048608 | tf_op jit(solution)/shard_map/all_to_all | solution.py:42
  170.0 5.4 %reduce.7 = f32[64,4096]{1,0:T(8,128)} reduce(f32[64,1,4096]{2,1,0:T(1,128)} %all-to-all-done.3, f32[]{:T(128)} %broadcast.68), dimensions={1}, to_apply=%all_to_all.21.reduce_sub_computation | reduce | bytes 2097156 | tf_op jit(solution)/shard_map/all_to_all | solution.py:42
  175.4 3.1 %reshape.193 = f32[64,2,32,64]{3,2,1,0:T(8,128)} reshape(f32[64,4096]{1,0:T(8,128)} %reduce.7) | data formatting | bytes 2097152
  181.4 1.9 fusion.12
  183.3 1.9 fusion.11
  185.2 2.7 fusion.54
  187.9 6.0 %all-to-all-start.4 = ((f32[256,16,256]{2,0,1:T(8,128)}), f32[256,16,256]{2,0,1:T(8,128)}, u32[]{:S(2)}, u32[]{:S(2)}) async-start(f32[256,16,256]{2,0,1:T(8,128)} %fusion.54), calls=%async_computation.5 | async-start | bytes 8388608 | tf_op jit(solution)/shard_map/all_to_all | solution.py:245
  196.0 2.8 %fusion.28 = f32[2,16,64,128]{3,2,1,0:T(8,128)} fusion(f32[64,2,16,64]{0,3,2,1:T(8,128)} %bitcast.192, bf16[1,128,2,2,64]{1,4,3,2,0:T(8,128)(2,1)S(1)} %bitcast.209), kind=kOutput, calls=%fused_computation.58 | convolution fusion | flops 201326592 | bytes 1605632 | tf_op jit(solution)/shard_map/tgn,ngkp->tgkp/dot_general | solution.py:121
  198.8 48.1 %all-to-all-done.4 = f32[256,16,256]{2,0,1:T(8,128)} async-done(((f32[256,16,256]{2,0,1:T(8,128)}), f32[256,16,256]{2,0,1:T(8,128)}, u32[]{:S(2)}, u32[]{:S(2)}) %all-to-all-start.4) | async-done | bytes 4194336 | tf_op jit(solution)/shard_map/all_to_all | solution.py:245
  247.0 2.5 reduce_sum.28
  250.3 10.0 %all-to-all-start.5 = ((f32[256,8,32]{0,2,1:T(8,128)}), f32[256,8,32]{0,2,1:T(8,128)S(1)}, u32[]{:S(2)}, u32[]{:S(2)}) async-start(f32[256,8,32]{0,2,1:T(8,128)} %bitcast.211), calls=%async_computation.6 | async-start | bytes 524288 | tf_op jit(solution)/shard_map/all_to_all | solution.py:248
  261.8 1.9 fusion.17
  265.7 5.0 %all-to-all-done.5 = f32[256,8,32]{0,2,1:T(8,128)S(1)} async-done(((f32[256,8,32]{0,2,1:T(8,128)}), f32[256,8,32]{0,2,1:T(8,128)S(1)}, u32[]{:S(2)}, u32[]{:S(2)}) %all-to-all-start.5) | async-done | bytes 262176 | tf_op jit(solution)/shard_map/all_to_all | solution.py:248
  (87 shorter events, 35.0 us)
Async XLA Ops:
  26.9 7.3 %copy-start.13 = (f32[1,32,128]{2,1,0:T(8,128)S(1)}, f32[1,32,128]{2,1,0:T(8,128)}, u32[]{:S(2)}) copy-start(f32[1,32,128]{2,1,0:T(8,128)} %param.11) | copy-start | bytes 49156
  26.9 7.7 %copy-start.11 = (bf16[1,128,2048]{2,1,0:T(8,128)(2,1)S(1)}, bf16[1,128,2048]{2,1,0:T(8,128)(2,1)}, u32[]{:S(2)}) copy-start(bf16[1,128,2048]{2,1,0:T(8,128)(2,1)} %param.9) | copy-start | bytes 1572868
  26.9 8.7 %copy-start.12 = (bf16[1,128,2048]{2,1,0:T(8,128)(2,1)S(1)}, bf16[1,128,2048]{2,1,0:T(8,128)(2,1)}, u32[]{:S(2)}) copy-start(bf16[1,128,2048]{2,1,0:T(8,128)(2,1)} %param.13) | copy-start | bytes 1572868
  26.9 33.5 %all-to-all-start.1 = ((bf16[16,8,32,256]{3,2,1,0:T(8,128)(2,1)}), bf16[16,8,32,256]{3,2,1,0:T(8,128)(2,1)S(1)}, u32[]{:S(2)}, u32[]{:S(2)}) async-start(bf16[16,8,32,256]{3,2,1,0:T(8,128)(2,1)} %broadcast_in_dim.90), calls=%async_computation.1 | async-start | bytes 4194304 | tf_op jit(solution)/shard_map/all_to_all | solution.py:165
  63.8 1.0 copy-start.4
  134.2 35.3 %all-to-all-start.3 = ((f32[64,1,4096]{2,1,0:T(1,128)}), f32[64,1,4096]{2,1,0:T(1,128)}, u32[]{:S(2)}, u32[]{:S(2)}) async-start(f32[64,1,4096]{2,1,0:T(1,128)} %reshape.192), calls=%async_computation.3 | async-start | bytes 2097152 | tf_op jit(solution)/shard_map/all_to_all | solution.py:42
  143.1 1.6 copy-start.5
  144.7 2.4 copy-start.14
  180.3 1.0 copy-start.7
  180.4 2.9 %copy-start.6 = (bf16[1,128,2048]{1,2,0:T(8,128)(2,1)S(1)}, bf16[1,128,2048]{1,2,0:T(8,128)(2,1)}, u32[]{:S(2)}) copy-start(bf16[1,128,2048]{1,2,0:T(8,128)(2,1)} %copy.43) | copy-start | bytes 1572868
  180.6 2.7 copy-start.1
  180.6 4.6 %copy-start.3 = (f32[1,64,64,32]{1,3,0,2:T(8,128)}, f32[1,64,64,32]{1,3,0,2:T(8,128)S(1)}, u32[]{:S(2)}) copy-start(f32[1,64,64,32]{1,3,0,2:T(8,128)S(1)} %get-tuple-element.29) | copy-start | bytes 1572868
  180.6 4.6 %copy-start.10 = (bf16[4096,128]{1,0:T(8,128)(2,1)S(1)}, bf16[4096,128]{1,0:T(8,128)(2,1)}, u32[]{:S(2)}) copy-start(bf16[4096,128]{1,0:T(8,128)(2,1)} %copy.66) | copy-start | bytes 3145732
  187.9 59.0 %all-to-all-start.4 = ((f32[256,16,256]{2,0,1:T(8,128)}), f32[256,16,256]{2,0,1:T(8,128)}, u32[]{:S(2)}, u32[]{:S(2)}) async-start(f32[256,16,256]{2,0,1:T(8,128)} %fusion.54), calls=%async_computation.5 | async-start | bytes 8388608 | tf_op jit(solution)/shard_map/all_to_all | solution.py:245
  193.9 77.5 %reduce-scatter.2.cloned.1.call-start = ((), (), s32[]{:S(2)}) async-start(), calls=%async_computation.7 | async-start | bytes 1572864 | tf_op jit(solution)/shard_map/reduce_scatter | solution.py:240
  198.8 61.4 %copy-start.2 = (f32[1,64,64,32]{1,3,0,2:T(8,128)S(1)}, f32[1,64,64,32]{1,3,0,2:T(8,128)}, u32[]{:S(2)}) copy-start(f32[1,64,64,32]{1,3,0,2:T(8,128)} %copy-done.1) | copy-start | bytes 1572868
  249.5 11.4 %copy-start = (f32[1,128,2048]{1,2,0:T(8,128)S(1)}, f32[1,128,2048]{1,2,0:T(8,128)}, u32[]{:S(2)}) copy-start(f32[1,128,2048]{1,2,0:T(8,128)} %convert_element_type.120) | copy-start | bytes 3145732
  250.3 20.4 %all-to-all-start.5 = ((f32[256,8,32]{0,2,1:T(8,128)}), f32[256,8,32]{0,2,1:T(8,128)S(1)}, u32[]{:S(2)}, u32[]{:S(2)}) async-start(f32[256,8,32]{0,2,1:T(8,128)} %bitcast.211), calls=%async_computation.6 | async-start | bytes 524288 | tf_op jit(solution)/shard_map/all_to_all | solution.py:248
  260.2 1.2 copy-start.8
  260.3 1.5 copy-start.9
Sparse Core Ops, SparseCore 0:
  197.8 11.2 reduce-scatter.1

commit v9 on v8

--- a/solution.py
+++ b/solution.py
@@ -40,8 +40,7 @@
         "ki,knc->inc", carry, got[:, 1, :rows], precision=lax.Precision.HIGHEST
     )
     back = lax.all_to_all(jnp.stack([fwd, bwd], 1), axis, 0, 0, tiled=True)
-    back = back.transpose(1, 2, 0, 3).reshape(2, rows, cols)
-    return back[0], back[1]
+    return back[:, 0], back[:, 1]
 
 
 def span_summary(b_vals, c_vals, x_vals, dy_round, rate_vals):
@@ -116,10 +115,11 @@
     (y_local, vals_local, c_local, b_local), state_in, adjoint_out = lax.optimization_barrier(
         ((y_local, vals_local, c_local, b_local), state_in, adjoint_out)
     )
-    state_four = state_in.reshape(STATE, group_count, per_group, HEAD_DIM)
-    adjoint_four = adjoint_out.reshape(STATE, group_count, per_group, HEAD_DIM)
+    width = state_in.shape[-1]
+    state_five = state_in.reshape(group_count, per_group, HEAD_DIM // width, STATE, width)
+    adjoint_five = adjoint_out.reshape(group_count, per_group, HEAD_DIM // width, STATE, width)
     y_inter = jnp.einsum(
-        "tgn,ngkp->tgkp", c_wide, state_four, precision=lax.Precision.HIGHEST
+        "tgn,gkhnc->tgkhc", c_wide, state_five, precision=lax.Precision.HIGHEST
     ).reshape(block_len, head_count, HEAD_DIM)
     output_pre = y_local + y_inter * from_start.T[:, :, None]
     gate_wide = gate_vals.astype(jnp.float32)
@@ -128,18 +128,20 @@
         dout_vals.astype(jnp.float32) * output_pre * gate_sig * (1.0 + gate_wide * (1.0 - gate_sig))
     ).astype(jnp.bfloat16)
     x_inter = jnp.einsum(
-        "sgn,ngkp->sgkp", b_wide, adjoint_four, precision=lax.Precision.HIGHEST
+        "sgn,gkhnc->sgkhc", b_wide, adjoint_five, precision=lax.Precision.HIGHEST
     ).reshape(block_len, head_count, HEAD_DIM)
     grad_vals = vals_local + x_inter * to_end.T[:, :, None]
     dy_scaled = (dy_wide * from_start.T[:, :, None]).reshape(
-        block_len, group_count, per_group, HEAD_DIM
-    )
-    x_scaled = (x_wide * to_end.T[:, :, None]).reshape(block_len, group_count, per_group, HEAD_DIM)
+        block_len, group_count, per_group, HEAD_DIM // width, width
+    )
+    x_scaled = (x_wide * to_end.T[:, :, None]).reshape(
+        block_len, group_count, per_group, HEAD_DIM // width, width
+    )
     c_grad = c_local + jnp.einsum(
-        "tgkp,ngkp->tgn", dy_scaled, state_four, precision=lax.Precision.HIGHEST
+        "tgkhc,gkhnc->tgn", dy_scaled, state_five, precision=lax.Precision.HIGHEST
     )
     b_grad = b_local + jnp.einsum(
-        "sgkp,ngkp->sgn", x_scaled, adjoint_four, precision=lax.Precision.HIGHEST
+        "sgkhc,gkhnc->sgn", x_scaled, adjoint_five, precision=lax.Precision.HIGHEST
     )
     return (grad_vals.astype(jnp.bfloat16), grad_gate, jnp.stack([b_grad, c_grad], axis=1))
 
@@ -199,16 +201,9 @@
             + summaries[block_id][2]
         )
     state_start, adjoint_end = carried_both(dev_log, dev_state, dev_adjoint, CTX)
-    running = state_start
-    block_id = 0
-    states_in = running
-    adjoints_out = [None] * nblocks
-    running = adjoint_end
-    for block_id in reversed(range(nblocks)):
-        adjoints_out[block_id] = running
-        running = (
-            running * jnp.repeat(summaries[block_id][0], HEAD_DIM)[None, :] + summaries[block_id][2]
-        )
+    assert nblocks == 1
+    states_in = state_start
+    adjoints_out = [adjoint_end]
     results = [
         span_full(
             bc_vals[0, :, 0],

time: 279 us -> 279 us (level)
  no operation moved by 1% of the time
where the time goes in v9:
time: 279 us; the launch traced here: 278 us
  waiting for transfers between devices  87.9 us (32%)
  blocking collectives  74.3 us (27%)
  starting transfers between devices  30.1 us (11%)
  local copies, waits for them, and re-layouts  27.7 us (10%)
  matrix products  24.3 us (9%)
  other arithmetic  19.2 us (7%)
  between operations  14.4 us (5%)
    all_to_all x1, blocking collectives, carried_both(): got = lax.all_to_all(packed, axis, 0, 0, tiled=True)  56.9 us
    all_to_all x1, waiting for transfers between devices, body(): lax.all_to_all(proj_terms.reshape(col_count, outer_count, -1), OUTER, 1,...  48.1 us
    all_to_all x1, waiting for transfers between devices, carried_both(): back = lax.all_to_all(jnp.stack([fwd, bwd], 1), axis, 0, 0, tiled=True)  19.3 us
    all_to_all x1, blocking collectives, body(): lax.all_to_all(jnp.broadcast_to(weight_local[None], (inner_count,) + weig...  17.4 us
    all_to_all x1, waiting for transfers between devices, body(): lax.all_to_all(jnp.broadcast_to(weight_inner[None], (outer_count,) + weig...  15.5 us
    unnamed x38, local copies, waits for them, and re-layouts  15.1 us
    all_to_all x1, starting transfers between devices, body(): lax.all_to_all(proj_parts.reshape(col_count, inner_count, -1), INNER, 1,...  9.95 us
    all_to_all x1, starting transfers between devices, body(): lax.all_to_all(jnp.broadcast_to(weight_inner[None], (outer_count,) + weig...  7.3 us
  transfers between devices with their start and end apart: 5, of which 4 were waited for; matrix products, arithmetic and copies ran while one was open for 12% of the time, Pallas kernels for 0%

profile of v9, /device:TPU:24, one launch (start us, length us, event | category | flops | bytes accessed | tf_op | source)
XLA Modules:
  0.0 277.9 jit_solution(7000396043906922280)
XLA Ops:
  7.9 17.4 %all_to_all.30 = bf16[8,32,256]{2,1,0:T(8,128)(2,1)S(1)} all-to-all(bf16[8,32,256]{2,1,0:T(8,128)(2,1)S(1)} %broadcast_in_dim.89), channel_id=1, replica_groups=mesh['dp'=2,'ylo'=2,'x'=4,'z'=8,'head'=2] {'z'}, dimensions={0} | all-to-all | bytes 262144 | tf_op jit(solution)/shard_map/all_to_all | solution.py:160
  26.9 7.3 %all-to-all-start.1 = ((bf16[16,8,32,256]{3,2,1,0:T(8,128)(2,1)}), bf16[16,8,32,256]{3,2,1,0:T(8,128)(2,1)S(1)}, u32[]{:S(2)}, u32[]{:S(2)}) async-start(bf16[16,8,32,256]{3,2,1,0:T(8,128)(2,1)} %broadcast_in_dim.90), calls=%async_computation.1 | async-start | bytes 4194304 | tf_op jit(solution)/shard_map/all_to_all | solution.py:167
  37.7 2.0 copy.53
  39.7 2.2 convert_element_type.152
  42.4 2.1 convert_element_type.153
  44.8 15.5 %all-to-all-done.1 = bf16[16,8,32,256]{3,2,1,0:T(8,128)(2,1)S(1)} async-done(((bf16[16,8,32,256]{3,2,1,0:T(8,128)(2,1)}), bf16[16,8,32,256]{3,2,1,0:T(8,128)(2,1)S(1)}, u32[]{:S(2)}, u32[]{:S(2)}) %all-to-all-start.1) | async-done | bytes 2097184 | tf_op jit(solution)/shard_map/all_to_all | solution.py:167
  62.1 2.1 fusion.18
  67.0 56.9 %all_to_all.31 = f32[64,2,65,32]{2,3,1,0:T(8,128)S(1)} all-to-all(f32[64,2,65,32]{2,3,1,0:T(8,128)S(1)} %copy.55), channel_id=1, replica_groups=mesh['dp'=2,'ylo'=2,'x'=4,'z'=8,'head'=2] {'ylo','x','z'}, dimensions={0} | all-to-all | bytes 2129920 | tf_op jit(solution)/shard_map/all_to_all | solution.py:26
  128.7 2.6 copy.103
  131.3 3.4 %reshape.203 = f32[64,1,4096]{2,1,0:T(1,128)} reshape(f32[64,2,32,64]{3,2,1,0:T(8,128)} %bitcast.189) | data formatting | bytes 2097152
  134.7 6.6 %all-to-all-start.3 = ((f32[64,1,4096]{2,1,0:T(1,128)}), f32[64,1,4096]{2,1,0:T(1,128)}, u32[]{:S(2)}, u32[]{:S(2)}) async-start(f32[64,1,4096]{2,1,0:T(1,128)} %reshape.203), calls=%async_computation.3 | async-start | bytes 2097152 | tf_op jit(solution)/shard_map/all_to_all | solution.py:42
  141.3 2.3 copy.84
  150.7 19.3 %all-to-all-done.3 = f32[64,1,4096]{2,1,0:T(1,128)} async-done(((f32[64,1,4096]{2,1,0:T(1,128)}), f32[64,1,4096]{2,1,0:T(1,128)}, u32[]{:S(2)}, u32[]{:S(2)}) %all-to-all-start.3) | async-done | bytes 1048608 | tf_op jit(solution)/shard_map/all_to_all | solution.py:42
  170.5 5.4 %reduce.7 = f32[64,4096]{1,0:T(8,128)} reduce(f32[64,1,4096]{2,1,0:T(1,128)} %all-to-all-done.3, f32[]{:T(128)} %broadcast.72), dimensions={1}, to_apply=%all_to_all.21.reduce_sub_computation | reduce | bytes 2097156 | tf_op jit(solution)/shard_map/all_to_all | solution.py:42
  175.9 3.1 %reshape.204 = f32[64,2,32,64]{3,2,1,0:T(8,128)} reshape(f32[64,4096]{1,0:T(8,128)} %reduce.7) | data formatting | bytes 2097152
  182.8 2.0 fusion.12
  184.9 2.7 fusion.52
  187.6 6.0 %all-to-all-start.4 = ((f32[256,16,256]{2,0,1:T(8,128)}), f32[256,16,256]{2,0,1:T(8,128)}, u32[]{:S(2)}, u32[]{:S(2)}) async-start(f32[256,16,256]{2,0,1:T(8,128)} %fusion.52), calls=%async_computation.5 | async-start | bytes 8388608 | tf_op jit(solution)/shard_map/all_to_all | solution.py:240
  195.7 2.8 %fusion.26 = f32[2,16,2,32,128]{4,3,2,1,0:T(8,128)} fusion(f32[2,16,2,64,32]{3,4,2,1,0:T(8,128)} %bitcast.199, bf16[1,128,2,2,64]{1,4,3,2,0:T(8,128)(2,1)S(1)} %bitcast.207), kind=kOutput, calls=%fused_computation.59 | convolution fusion | flops 201326592 | bytes 1605632 | tf_op jit(solution)/shard_map/tgn,gkhnc->tgkhc/dot_general | solution.py:121
  198.5 48.1 %all-to-all-done.4 = f32[256,16,256]{2,0,1:T(8,128)} async-done(((f32[256,16,256]{2,0,1:T(8,128)}), f32[256,16,256]{2,0,1:T(8,128)}, u32[]{:S(2)}, u32[]{:S(2)}) %all-to-all-start.4) | async-done | bytes 4194336 | tf_op jit(solution)/shard_map/all_to_all | solution.py:240
  246.6 2.5 reduce_sum.28
  249.9 10.0 %all-to-all-start.5 = ((f32[256,8,32]{0,2,1:T(8,128)}), f32[256,8,32]{0,2,1:T(8,128)S(1)}, u32[]{:S(2)}, u32[]{:S(2)}) async-start(f32[256,8,32]{0,2,1:T(8,128)} %bitcast.209), calls=%async_computation.6 | async-start | bytes 524288 | tf_op jit(solution)/shard_map/all_to_all | solution.py:243
  261.4 2.0 multiply_convert_fusion
  265.5 4.9 %all-to-all-done.5 = f32[256,8,32]{0,2,1:T(8,128)S(1)} async-done(((f32[256,8,32]{0,2,1:T(8,128)}), f32[256,8,32]{0,2,1:T(8,128)S(1)}, u32[]{:S(2)}, u32[]{:S(2)}) %all-to-all-start.5) | async-done | bytes 262176 | tf_op jit(solution)/shard_map/all_to_all | solution.py:243
  (86 shorter events, 34.4 us)
Async XLA Ops:
  26.9 7.3 %copy-start.13 = (f32[1,32,128]{2,1,0:T(8,128)S(1)}, f32[1,32,128]{2,1,0:T(8,128)}, u32[]{:S(2)}) copy-start(f32[1,32,128]{2,1,0:T(8,128)} %param.11) | copy-start | bytes 49156
  26.9 7.7 %copy-start.11 = (bf16[1,128,2048]{2,1,0:T(8,128)(2,1)S(1)}, bf16[1,128,2048]{2,1,0:T(8,128)(2,1)}, u32[]{:S(2)}) copy-start(bf16[1,128,2048]{2,1,0:T(8,128)(2,1)} %param.9) | copy-start | bytes 1572868
  26.9 8.7 %copy-start.12 = (bf16[1,128,2048]{2,1,0:T(8,128)(2,1)S(1)}, bf16[1,128,2048]{2,1,0:T(8,128)(2,1)}, u32[]{:S(2)}) copy-start(bf16[1,128,2048]{2,1,0:T(8,128)(2,1)} %param.13) | copy-start | bytes 1572868
  26.9 33.5 %all-to-all-start.1 = ((bf16[16,8,32,256]{3,2,1,0:T(8,128)(2,1)}), bf16[16,8,32,256]{3,2,1,0:T(8,128)(2,1)S(1)}, u32[]{:S(2)}, u32[]{:S(2)}) async-start(bf16[16,8,32,256]{3,2,1,0:T(8,128)(2,1)} %broadcast_in_dim.90), calls=%async_computation.1 | async-start | bytes 4194304 | tf_op jit(solution)/shard_map/all_to_all | solution.py:167
  64.2 1.2 copy-start.2
  134.7 35.3 %all-to-all-start.3 = ((f32[64,1,4096]{2,1,0:T(1,128)}), f32[64,1,4096]{2,1,0:T(1,128)}, u32[]{:S(2)}, u32[]{:S(2)}) async-start(f32[64,1,4096]{2,1,0:T(1,128)} %reshape.203), calls=%async_computation.3 | async-start | bytes 2097152 | tf_op jit(solution)/shard_map/all_to_all | solution.py:42
  143.6 1.6 copy-start.6
  145.2 2.4 copy-start.14
  179.0 1.9 copy-start.3
  180.8 4.0 %copy-start.4 = (f32[64,64,32]{1,2,0:T(8,128)}, f32[64,64,32]{1,2,0:T(8,128)S(1)}, u32[]{:S(2)}) copy-start(f32[64,64,32]{1,2,0:T(8,128)S(1)} %get-tuple-element.11) | copy-start | bytes 1572868
  180.8 4.0 %copy-start.10 = (f32[64,64,32]{1,2,0:T(8,128)}, f32[64,64,32]{1,2,0:T(8,128)S(1)}, u32[]{:S(2)}) copy-start(f32[64,64,32]{1,2,0:T(8,128)S(1)} %get-tuple-element.13) | copy-start | bytes 1572868
  180.8 2.0 copy-start
  182.8 2.1 copy-start.9
  187.6 59.0 %all-to-all-start.4 = ((f32[256,16,256]{2,0,1:T(8,128)}), f32[256,16,256]{2,0,1:T(8,128)}, u32[]{:S(2)}, u32[]{:S(2)}) async-start(f32[256,16,256]{2,0,1:T(8,128)} %fusion.52), calls=%async_computation.5 | async-start | bytes 8388608 | tf_op jit(solution)/shard_map/all_to_all | solution.py:240
  193.6 77.5 %reduce-scatter.2.cloned.1.call-start = ((), (), s32[]{:S(2)}) async-start(), calls=%async_computation.7 | async-start | bytes 1572864 | tf_op jit(solution)/shard_map/reduce_scatter | solution.py:235
  198.5 61.4 %copy-start.5 = (f32[64,64,32]{1,2,0:T(8,128)S(1)}, f32[64,64,32]{1,2,0:T(8,128)}, u32[]{:S(2)}) copy-start(f32[64,64,32]{1,2,0:T(8,128)} %copy-done.4) | copy-start | bytes 1572868
  249.1 11.4 %copy-start.1 = (f32[1,128,2048]{1,2,0:T(8,128)S(1)}, f32[1,128,2048]{1,2,0:T(8,128)}, u32[]{:S(2)}) copy-start(f32[1,128,2048]{1,2,0:T(8,128)} %convert_element_type.152) | copy-start | bytes 3145732
  249.9 20.4 %all-to-all-start.5 = ((f32[256,8,32]{0,2,1:T(8,128)}), f32[256,8,32]{0,2,1:T(8,128)S(1)}, u32[]{:S(2)}, u32[]{:S(2)}) async-start(f32[256,8,32]{0,2,1:T(8,128)} %bitcast.209), calls=%async_computation.6 | async-start | bytes 524288 | tf_op jit(solution)/shard_map/all_to_all | solution.py:243
  259.9 1.2 copy-start.7
  259.9 1.5 copy-start.8
Sparse Core Ops, SparseCore 0:
  197.4 11.2 reduce-scatter.1

commit v10 on v8

--- a/solution.py
+++ b/solution.py
@@ -23,7 +23,8 @@
         [jnp.concatenate([state, log_row], 0)[None], jnp.pad(adjoint, ((0, 1), (0, 0)))[None]], 0
     )
     packed = packed.reshape(2, rows + 1, count, chunk).transpose(2, 0, 1, 3)
-    got = lax.all_to_all(packed, axis, 0, 0, tiled=True)
+    got = lax.all_to_all(packed.reshape(count, 1, -1), axis, 0, 0, tiled=True)
+    got = got.reshape(count, 2, rows + 1, chunk)
     logs = got[:, 0, rows, 0]
     place = jnp.arange(count)
     before = place[None, :] < place[:, None]

time: 279 us -> 278 us (level)
  blocking collectives: 74.3 us -> 53.8 us
  local copies, waits for them, and re-layouts: 28.5 us -> 48.6 us
    all_to_all x1, blocking collectives: 56.9 us -> 36.5 us  [carried_both(): got = lax.all_to_all(packed.reshape(count, 1, -1), axis, 0, 0, tiled=True)]
    unnamed x38 -> x42, local copies, waits for them, and re-layouts: 15.7 us -> 21.2 us
    reshape x0 -> x1, local copies, waits for them, and re-layouts: none -> 3.99 us  [carried_both(): got = lax.all_to_all(packed.reshape(count, 1, -1), axis, 0, 0, tiled=True)]
    transpose x1, local copies, waits for them, and re-layouts: 0.24 us -> 4.23 us  [carried_both(): packed = packed.reshape(2, rows + 1, count, chunk).transpose(2, 0, 1, 3)]
    all_to_all x0 -> x1, local copies, waits for them, and re-layouts: none -> 3.93 us  [carried_both(): got = lax.all_to_all(packed.reshape(count, 1, -1), axis, 0, 0, tiled=True)]
    slice x1, local copies, waits for them, and re-layouts: 0.2 us -> 3.03 us  [carried_both(): got[:, 0, :rows]]
where the time goes in v10:
time: 278 us; the launch traced here: 277 us
  waiting for transfers between devices  87.8 us (32%)
  blocking collectives  53.8 us (19%)
  local copies, waits for them, and re-layouts  48.6 us (17%)
  starting transfers between devices  27.6 us (10%)
  matrix products  24 us (9%)
  other arithmetic  20.6 us (7%)
  between operations  14.4 us (5%)
    all_to_all x1, waiting for transfers between devices, body(): lax.all_to_all(proj_terms.reshape(col_count, outer_count, -1), OUTER, 1,...  48.3 us
    all_to_all x1, blocking collectives, carried_both(): got = lax.all_to_all(packed.reshape(count, 1, -1), axis, 0, 0, tiled=True)  36.5 us
    unnamed x42, local copies, waits for them, and re-layouts  21.2 us
    all_to_all x1, waiting for transfers between devices, carried_both(): back = lax.all_to_all(jnp.stack([fwd, bwd], 1), axis, 0, 0, tiled=True)  19.2 us
    all_to_all x1, blocking collectives, body(): lax.all_to_all(jnp.broadcast_to(weight_local[None], (inner_count,) + weig...  17.4 us
    all_to_all x1, waiting for transfers between devices, body(): lax.all_to_all(jnp.broadcast_to(weight_inner[None], (outer_count,) + weig...  15.3 us
    all_to_all x1, starting transfers between devices, body(): lax.all_to_all(proj_parts.reshape(col_count, inner_count, -1), INNER, 1,...  8.44 us
    all_to_all x1, starting transfers between devices, body(): lax.all_to_all(jnp.broadcast_to(weight_inner[None], (outer_count,) + weig...  7.3 us
  transfers between devices with their start and end apart: 5, of which 4 were waited for; matrix products, arithmetic and copies ran while one was open for 12% of the time, Pallas kernels for 0%

profile of v10, /device:TPU:24, one launch (start us, length us, event | category | flops | bytes accessed | tf_op | source)
XLA Modules:
  0.0 276.9 jit_solution(1885761237836482544)
XLA Ops:
  7.9 17.4 %all_to_all.30 = bf16[8,32,256]{2,1,0:T(8,128)(2,1)S(1)} all-to-all(bf16[8,32,256]{2,1,0:T(8,128)(2,1)S(1)} %broadcast_in_dim.89), channel_id=1, replica_groups=mesh['dp'=2,'ylo'=2,'x'=4,'z'=8,'head'=2] {'z'}, dimensions={0} | all-to-all | bytes 262144 | tf_op jit(solution)/shard_map/all_to_all | solution.py:159
  26.9 7.3 %all-to-all-start.1 = ((bf16[16,8,32,256]{3,2,1,0:T(8,128)(2,1)}), bf16[16,8,32,256]{3,2,1,0:T(8,128)(2,1)S(1)}, u32[]{:S(2)}, u32[]{:S(2)}) async-start(bf16[16,8,32,256]{3,2,1,0:T(8,128)(2,1)} %broadcast_in_dim.90), calls=%async_computation.1 | async-start | bytes 4194304 | tf_op jit(solution)/shard_map/all_to_all | solution.py:166
  45.0 15.3 %all-to-all-done.1 = bf16[16,8,32,256]{3,2,1,0:T(8,128)(2,1)S(1)} async-done(((bf16[16,8,32,256]{3,2,1,0:T(8,128)(2,1)}), bf16[16,8,32,256]{3,2,1,0:T(8,128)(2,1)S(1)}, u32[]{:S(2)}, u32[]{:S(2)}) %all-to-all-start.1) | async-done | bytes 2097184 | tf_op jit(solution)/shard_map/all_to_all | solution.py:166
  67.5 4.2 %copy.63 = f32[64,2,65,32]{0,3,2,1:T(8,128)} copy(f32[64,2,65,32]{2,3,0,1:T(8,128)} %maximum_bitcast_fusion) | data formatting | bytes 2129920 | tf_op jit(solution)/shard_map/transpose | solution.py:25
  71.7 4.0 %copy.64 = f32[64,1,4160]{2,1,0:T(1,128)} copy(f32[64,1,4160]{0,2,1:T(8,128)} %bitcast.197) | data formatting | bytes 2129920 | tf_op jit(solution)/shard_map/reshape | solution.py:26
  75.7 36.5 %all_to_all.31 = f32[64,1,4160]{2,1,0:T(1,128)} all-to-all(f32[64,1,4160]{2,1,0:T(1,128)} %copy.64), channel_id=1, replica_groups=mesh['dp'=2,'ylo'=2,'x'=4,'z'=8,'head'=2] {'ylo','x','z'}, dimensions={0} | all-to-all | bytes 2129920 | tf_op jit(solution)/shard_map/all_to_all | solution.py:26
  112.2 3.9 %copy.65 = f32[64,1,4160]{0,2,1:T(8,128)} copy(f32[64,1,4160]{2,1,0:T(1,128)} %all_to_all.31) | data formatting | bytes 2129920 | tf_op jit(solution)/shard_map/all_to_all | solution.py:26
  116.8 3.0 %fusion.54 = (f32[64,1,64,32]{0,3,2,1:T(8,128)}, f32[64,1,64,32]{0,3,2,1:T(8,128)}) fusion(f32[64,2,65,32]{0,3,2,1:T(8,128)} %bitcast.199), kind=kLoop, calls=%fused_computation.89 | loop fusion | bytes 2097152 | tf_op jit(solution)/shard_map/slice | solution.py:38
  120.0 2.7 copy.86
  122.8 2.8 %copy.85 = f32[64,1,64,32]{2,0,3,1:T(8,128)} copy(f32[64,1,64,32]{0,3,2,1:T(8,128)} %get-tuple-element.32) | data formatting | bytes 1048576
  125.6 2.3 convolution_bitcast_fusion
  129.2 2.6 copy.91
  131.8 3.4 %reshape.199 = f32[64,1,4096]{2,1,0:T(1,128)} reshape(f32[64,2,32,64]{3,2,1,0:T(8,128)} %bitcast.204) | data formatting | bytes 2097152
  135.2 5.6 %all-to-all-start.3 = ((f32[64,1,4096]{2,1,0:T(1,128)}), f32[64,1,4096]{2,1,0:T(1,128)}, u32[]{:S(2)}, u32[]{:S(2)}) async-start(f32[64,1,4096]{2,1,0:T(1,128)} %reshape.199), calls=%async_computation.3 | async-start | bytes 2097152 | tf_op jit(solution)/shard_map/all_to_all | solution.py:43
  150.3 19.2 %all-to-all-done.3 = f32[64,1,4096]{2,1,0:T(1,128)} async-done(((f32[64,1,4096]{2,1,0:T(1,128)}), f32[64,1,4096]{2,1,0:T(1,128)}, u32[]{:S(2)}, u32[]{:S(2)}) %all-to-all-start.3) | async-done | bytes 1048608 | tf_op jit(solution)/shard_map/all_to_all | solution.py:43
  170.0 5.4 %reduce.5 = f32[64,4096]{1,0:T(8,128)} reduce(f32[64,1,4096]{2,1,0:T(1,128)} %all-to-all-done.3, f32[]{:T(128)} %broadcast.67), dimensions={1}, to_apply=%all_to_all.21.reduce_sub_computation | reduce | bytes 2097156 | tf_op jit(solution)/shard_map/all_to_all | solution.py:43
  175.3 3.1 %reshape.200 = f32[64,2,32,64]{3,2,1,0:T(8,128)} reshape(f32[64,4096]{1,0:T(8,128)} %reduce.5) | data formatting | bytes 2097152
  185.2 2.7 fusion.56
  187.9 6.0 %all-to-all-start.4 = ((f32[256,16,256]{2,0,1:T(8,128)}), f32[256,16,256]{2,0,1:T(8,128)}, u32[]{:S(2)}, u32[]{:S(2)}) async-start(f32[256,16,256]{2,0,1:T(8,128)} %fusion.56), calls=%async_computation.5 | async-start | bytes 8388608 | tf_op jit(solution)/shard_map/all_to_all | solution.py:246
  196.0 2.8 %fusion.30 = f32[2,16,64,128]{3,2,1,0:T(8,128)} fusion(f32[64,2,16,64]{0,3,2,1:T(8,128)} %bitcast.196, bf16[1,128,2,2,64]{1,4,3,2,0:T(8,128)(2,1)S(1)} %bitcast.216), kind=kOutput, calls=%fused_computation.57 | convolution fusion | flops 201326592 | bytes 1605632 | tf_op jit(solution)/shard_map/tgn,ngkp->tgkp/dot_general | solution.py:122
  198.8 48.3 %all-to-all-done.4 = f32[256,16,256]{2,0,1:T(8,128)} async-done(((f32[256,16,256]{2,0,1:T(8,128)}), f32[256,16,256]{2,0,1:T(8,128)}, u32[]{:S(2)}, u32[]{:S(2)}) %all-to-all-start.4) | async-done | bytes 4194336 | tf_op jit(solution)/shard_map/all_to_all | solution.py:246
  247.1 2.5 reduce_sum.28
  250.5 8.4 %all-to-all-start.5 = ((f32[256,8,32]{0,2,1:T(8,128)}), f32[256,8,32]{0,2,1:T(8,128)S(1)}, u32[]{:S(2)}, u32[]{:S(2)}) async-start(f32[256,8,32]{0,2,1:T(8,128)} %bitcast.218), calls=%async_computation.6 | async-start | bytes 524288 | tf_op jit(solution)/shard_map/all_to_all | solution.py:249
  264.4 5.0 %all-to-all-done.5 = f32[256,8,32]{0,2,1:T(8,128)S(1)} async-done(((f32[256,8,32]{0,2,1:T(8,128)}), f32[256,8,32]{0,2,1:T(8,128)S(1)}, u32[]{:S(2)}, u32[]{:S(2)}) %all-to-all-start.5) | async-done | bytes 262176 | tf_op jit(solution)/shard_map/all_to_all | solution.py:249
  (93 shorter events, 48.0 us)
Async XLA Ops:
  26.9 7.3 %copy-start.14 = (f32[1,32,128]{2,1,0:T(8,128)S(1)}, f32[1,32,128]{2,1,0:T(8,128)}, u32[]{:S(2)}) copy-start(f32[1,32,128]{2,1,0:T(8,128)} %param.11) | copy-start | bytes 49156
  26.9 7.7 %copy-start.12 = (bf16[1,128,2048]{2,1,0:T(8,128)(2,1)S(1)}, bf16[1,128,2048]{2,1,0:T(8,128)(2,1)}, u32[]{:S(2)}) copy-start(bf16[1,128,2048]{2,1,0:T(8,128)(2,1)} %param.9) | copy-start | bytes 1572868
  26.9 8.7 %copy-start.13 = (bf16[1,128,2048]{2,1,0:T(8,128)(2,1)S(1)}, bf16[1,128,2048]{2,1,0:T(8,128)(2,1)}, u32[]{:S(2)}) copy-start(bf16[1,128,2048]{2,1,0:T(8,128)(2,1)} %param.13) | copy-start | bytes 1572868
  26.9 33.5 %all-to-all-start.1 = ((bf16[16,8,32,256]{3,2,1,0:T(8,128)(2,1)}), bf16[16,8,32,256]{3,2,1,0:T(8,128)(2,1)S(1)}, u32[]{:S(2)}, u32[]{:S(2)}) async-start(bf16[16,8,32,256]{3,2,1,0:T(8,128)(2,1)} %broadcast_in_dim.90), calls=%async_computation.1 | async-start | bytes 4194304 | tf_op jit(solution)/shard_map/all_to_all | solution.py:166
  63.8 1.0 copy-start.4
  125.6 2.3 copy-start.10
  135.2 34.2 %all-to-all-start.3 = ((f32[64,1,4096]{2,1,0:T(1,128)}), f32[64,1,4096]{2,1,0:T(1,128)}, u32[]{:S(2)}, u32[]{:S(2)}) async-start(f32[64,1,4096]{2,1,0:T(1,128)} %reshape.199), calls=%async_computation.3 | async-start | bytes 2097152 | tf_op jit(solution)/shard_map/all_to_all | solution.py:43
  143.1 1.6 copy-start.5
  144.7 2.4 copy-start.15
  180.3 1.0 copy-start.7
  180.3 2.9 %copy-start.6 = (bf16[1,128,2048]{1,2,0:T(8,128)(2,1)S(1)}, bf16[1,128,2048]{1,2,0:T(8,128)(2,1)}, u32[]{:S(2)}) copy-start(bf16[1,128,2048]{1,2,0:T(8,128)(2,1)} %copy.59) | copy-start | bytes 1572868
  180.5 2.7 copy-start.1
  180.5 4.6 %copy-start.3 = (f32[1,64,64,32]{1,3,0,2:T(8,128)}, f32[1,64,64,32]{1,3,0,2:T(8,128)S(1)}, u32[]{:S(2)}) copy-start(f32[1,64,64,32]{1,3,0,2:T(8,128)S(1)} %get-tuple-element.35) | copy-start | bytes 1572868
  180.5 4.6 %copy-start.11 = (bf16[4096,128]{1,0:T(8,128)(2,1)S(1)}, bf16[4096,128]{1,0:T(8,128)(2,1)}, u32[]{:S(2)}) copy-start(bf16[4096,128]{1,0:T(8,128)(2,1)} %copy.84) | copy-start | bytes 3145732
  187.9 59.3 %all-to-all-start.4 = ((f32[256,16,256]{2,0,1:T(8,128)}), f32[256,16,256]{2,0,1:T(8,128)}, u32[]{:S(2)}, u32[]{:S(2)}) async-start(f32[256,16,256]{2,0,1:T(8,128)} %fusion.56), calls=%async_computation.5 | async-start | bytes 8388608 | tf_op jit(solution)/shard_map/all_to_all | solution.py:246
  193.9 76.2 %reduce-scatter.2.cloned.1.call-start = ((), (), s32[]{:S(2)}) async-start(), calls=%async_computation.7 | async-start | bytes 1572864 | tf_op jit(solution)/shard_map/reduce_scatter | solution.py:241
  198.8 60.1 %copy-start.2 = (f32[1,64,64,32]{1,3,0,2:T(8,128)S(1)}, f32[1,64,64,32]{1,3,0,2:T(8,128)}, u32[]{:S(2)}) copy-start(f32[1,64,64,32]{1,3,0,2:T(8,128)} %copy-done.1) | copy-start | bytes 1572868
  249.6 9.9 %copy-start = (f32[1,128,2048]{1,2,0:T(8,128)S(1)}, f32[1,128,2048]{1,2,0:T(8,128)}, u32[]{:S(2)}) copy-start(f32[1,128,2048]{1,2,0:T(8,128)} %convert_element_type.120) | copy-start | bytes 3145732
  250.5 18.9 %all-to-all-start.5 = ((f32[256,8,32]{0,2,1:T(8,128)}), f32[256,8,32]{0,2,1:T(8,128)S(1)}, u32[]{:S(2)}, u32[]{:S(2)}) async-start(f32[256,8,32]{0,2,1:T(8,128)} %bitcast.218), calls=%async_computation.6 | async-start | bytes 524288 | tf_op jit(solution)/shard_map/all_to_all | solution.py:249
  258.9 1.2 copy-start.8
  258.9 1.5 copy-start.9
Sparse Core Ops, SparseCore 0:
  197.7 10.7 reduce-scatter.1

commit v11 on v8

--- a/solution.py
+++ b/solution.py
@@ -18,13 +18,17 @@
     rows, cols = state.shape
     chunk = cols // count
     assert HEAD_DIM % chunk == 0
-    log_row = jnp.repeat(log_total, cols // log_total.shape[0])[None, :]
+    flat = rows * chunk
+
+    def rows_of(a):
+        return a.reshape(rows, count, chunk).transpose(1, 0, 2).reshape(count, flat)
+
+    chunk_logs = jnp.repeat(log_total, cols // log_total.shape[0]).reshape(count, chunk)
     packed = jnp.concatenate(
-        [jnp.concatenate([state, log_row], 0)[None], jnp.pad(adjoint, ((0, 1), (0, 0)))[None]], 0
-    )
-    packed = packed.reshape(2, rows + 1, count, chunk).transpose(2, 0, 1, 3)
-    got = lax.all_to_all(packed, axis, 0, 0, tiled=True)
-    logs = got[:, 0, rows, 0]
+        [rows_of(state), rows_of(adjoint), chunk_logs, jnp.zeros_like(chunk_logs)], 1
+    )
+    got = lax.all_to_all(packed[:, None], axis, 0, 0, tiled=True)[:, 0]
+    logs = got[:, 2 * flat]
     place = jnp.arange(count)
     before = place[None, :] < place[:, None]
     gaps = jnp.dot(
@@ -33,14 +37,10 @@
         precision=lax.Precision.HIGHEST,
     )
     carry = jnp.where(before, jnp.exp(jnp.where(before, gaps, 0.0)), 0.0)
-    fwd = jnp.einsum(
-        "ik,knc->inc", carry, got[:, 0, :rows], precision=lax.Precision.HIGHEST
-    )
-    bwd = jnp.einsum(
-        "ki,knc->inc", carry, got[:, 1, :rows], precision=lax.Precision.HIGHEST
-    )
-    back = lax.all_to_all(jnp.stack([fwd, bwd], 1), axis, 0, 0, tiled=True)
-    back = back.transpose(1, 2, 0, 3).reshape(2, rows, cols)
+    fwd = jnp.dot(carry, got[:, :flat], precision=lax.Precision.HIGHEST)
+    bwd = jnp.dot(carry.T, got[:, flat : 2 * flat], precision=lax.Precision.HIGHEST)
+    back = lax.all_to_all(jnp.concatenate([fwd, bwd], 1)[:, None], axis, 0, 0, tiled=True)
+    back = back.reshape(count, 2, rows, chunk).transpose(1, 2, 0, 3).reshape(2, rows, cols)
     return back[0], back[1]
 
 

time: 279 us -> 273 us (0.978)
  blocking collectives: 74.3 us -> 53.7 us
  local copies, waits for them, and re-layouts: 28.5 us -> 39.8 us
  matrix products: 23.8 us -> 27.4 us
    all_to_all x1, blocking collectives: 56.9 us -> 36.4 us  [carried_both(): got = lax.all_to_all(packed[:, None], axis, 0, 0, tiled=True)[:, 0]]
    slice x1 -> x3, local copies, waits for them, and re-layouts: 0.2 us -> 9.49 us  [carried_both(): return (back[0], back[1])]
    unnamed x38 -> x29, local copies, waits for them, and re-layouts: 15.7 us -> 7.78 us
    reshape x0 -> x2, local copies, waits for them, and re-layouts: none -> 6.33 us  [the longest x1 3.19 us: span_summary(): adjoint_part.reshape(STATE, -1)]
    broadcast_in_dim x3 -> x5, local copies, waits for them, and re-layouts: 0.32 us -> 6.23 us  [the longest x1 4.01 us: carried_both(): got = lax.all_to_all(packed[:, None], axis, 0, 0, tiled=True)[:, 0]]
    all_to_all x1 -> x0, other arithmetic: 5.37 us -> none  [carried_both(): back = lax.all_to_all(jnp.stack([fwd, bwd], 1), axis, 0, 0, tiled=True)]
    broadcast_in_dim x0 -> x2, other arithmetic: none -> 5.08 us  [the longest x1 5.01 us: carried_both(): got = lax.all_to_all(packed[:, None], axis, 0, 0, tiled=True)[:, 0]]
    all_to_all x1, local copies, waits for them, and re-layouts: 0.51 us -> 3.92 us  [carried_both(): lax.all_to_all(jnp.concatenate([fwd, bwd], 1)[:, None], axis, 0, 0, tiled...]
where the time goes in v11:
time: 273 us; the launch traced here: 272 us
  waiting for transfers between devices  88.3 us (32%)
  blocking collectives  53.7 us (20%)
  local copies, waits for them, and re-layouts  39.8 us (15%)
  starting transfers between devices  28.6 us (10%)
  matrix products  27.4 us (10%)
  other arithmetic  19.6 us (7%)
  between operations  14.3 us (5%)
    all_to_all x1, waiting for transfers between devices, body(): lax.all_to_all(proj_terms.reshape(col_count, outer_count, -1), OUTER, 1,...  48.7 us
    all_to_all x1, blocking collectives, carried_both(): got = lax.all_to_all(packed[:, None], axis, 0, 0, tiled=True)[:, 0]  36.4 us
    all_to_all x1, waiting for transfers between devices, carried_both(): lax.all_to_all(jnp.concatenate([fwd, bwd], 1)[:, None], axis, 0, 0, tiled...  19.2 us
    all_to_all x1, blocking collectives, body(): lax.all_to_all(jnp.broadcast_to(weight_local[None], (inner_count,) + weig...  17.4 us
    all_to_all x1, waiting for transfers between devices, body(): lax.all_to_all(jnp.broadcast_to(weight_inner[None], (outer_count,) + weig...  15.4 us
    all_to_all x1, starting transfers between devices, body(): lax.all_to_all(proj_parts.reshape(col_count, inner_count, -1), INNER, 1,...  9.65 us
    slice x3, local copies, waits for them, and re-layouts, carried_both(): return (back[0], back[1])  9.49 us
    unnamed x29, local copies, waits for them, and re-layouts  7.78 us
  transfers between devices with their start and end apart: 5, of which 4 were waited for; matrix products, arithmetic and copies ran while one was open for 12% of the time, Pallas kernels for 0%

profile of v11, /device:TPU:24, one launch (start us, length us, event | category | flops | bytes accessed | tf_op | source)
XLA Modules:
  0.0 271.7 jit_solution(1702932619558617726)
XLA Ops:
  7.9 17.4 %all_to_all.30 = bf16[8,32,256]{2,1,0:T(8,128)(2,1)S(1)} all-to-all(bf16[8,32,256]{2,1,0:T(8,128)(2,1)S(1)} %broadcast_in_dim.94), channel_id=1, replica_groups=mesh['dp'=2,'ylo'=2,'x'=4,'z'=8,'head'=2] {'z'}, dimensions={0} | all-to-all | bytes 262144 | tf_op jit(solution)/shard_map/all_to_all | solution.py:158
  26.9 7.3 %all-to-all-start.1 = ((bf16[16,8,32,256]{3,2,1,0:T(8,128)(2,1)}), bf16[16,8,32,256]{3,2,1,0:T(8,128)(2,1)S(1)}, u32[]{:S(2)}, u32[]{:S(2)}) async-start(bf16[16,8,32,256]{3,2,1,0:T(8,128)(2,1)} %broadcast_in_dim.95), calls=%async_computation.1 | async-start | bytes 4194304 | tf_op jit(solution)/shard_map/all_to_all | solution.py:165
  44.9 15.4 %all-to-all-done.1 = bf16[16,8,32,256]{3,2,1,0:T(8,128)(2,1)S(1)} async-done(((bf16[16,8,32,256]{3,2,1,0:T(8,128)(2,1)}), bf16[16,8,32,256]{3,2,1,0:T(8,128)(2,1)S(1)}, u32[]{:S(2)}, u32[]{:S(2)}) %all-to-all-start.1) | async-done | bytes 2097184 | tf_op jit(solution)/shard_map/all_to_all | solution.py:165
  62.1 2.7 fusion.19
  64.8 3.1 %copy.64 = f32[64,64,32]{1,2,0:T(8,128)} copy(f32[64,64,32]{0,2,1:T(8,128)} %bitcast.196) | data formatting | bytes 1048576 | tf_op jit(solution)/shard_map/reshape | solution.py:66
  68.0 2.7 fusion.21
  70.6 3.2 %copy.65 = f32[64,64,32]{1,2,0:T(8,128)} copy(f32[64,64,32]{0,2,1:T(8,128)} %bitcast.197) | data formatting | bytes 1048576 | tf_op jit(solution)/shard_map/reshape | solution.py:66
  75.6 5.0 %maximum_bitcast_fusion = f32[64,1,4160]{0,2,1:T(8,128)} fusion(f32[64,32]{0,1:T(8,128)S(1)} %broadcast_in_dim.100, f32[64,2048]{0,1:T(8,128)S(1)} %bitcast.194, f32[64,2048]{0,1:T(8,128)S(1)} %bitcast.193, f32[4160]{0:T(1024)S(1)} %pad.7.clone), kind=kLoop, calls=%fused_computation.1 | loop fusion | flops 798720 | bytes 2138368 | tf_op jit(solution)/shard_map/broadcast_in_dim | solution.py:30
  80.6 4.0 %copy.66 = f32[64,1,4160]{2,1,0:T(1,128)} copy(f32[64,1,4160]{0,2,1:T(8,128)} %maximum_bitcast_fusion) | data formatting | bytes 2129920 | tf_op jit(solution)/shard_map/broadcast_in_dim | solution.py:30
  84.6 36.4 %all_to_all.31 = f32[64,1,4160]{2,1,0:T(1,128)S(1)} all-to-all(f32[64,1,4160]{2,1,0:T(1,128)} %copy.66), channel_id=1, replica_groups=mesh['dp'=2,'ylo'=2,'x'=4,'z'=8,'head'=2] {'ylo','x','z'}, dimensions={0} | all-to-all | bytes 2129920 | tf_op jit(solution)/shard_map/all_to_all | solution.py:30
  124.7 5.6 %all-to-all-start.3 = ((f32[64,1,4096]{2,1,0:T(1,128)}), f32[64,1,4096]{2,1,0:T(1,128)}, u32[]{:S(2)}, u32[]{:S(2)}) async-start(f32[64,1,4096]{2,1,0:T(1,128)} %copy.67), calls=%async_computation.3 | async-start | bytes 2097152 | tf_op jit(solution)/shard_map/all_to_all | solution.py:42
  139.7 19.2 %all-to-all-done.3 = f32[64,1,4096]{2,1,0:T(1,128)} async-done(((f32[64,1,4096]{2,1,0:T(1,128)}), f32[64,1,4096]{2,1,0:T(1,128)}, u32[]{:S(2)}, u32[]{:S(2)}) %all-to-all-start.3) | async-done | bytes 1048608 | tf_op jit(solution)/shard_map/all_to_all | solution.py:42
  158.9 3.9 %copy.68 = f32[64,1,4096]{0,2,1:T(8,128)} copy(f32[64,1,4096]{2,1,0:T(1,128)} %all-to-all-done.3) | data formatting | bytes 2097152 | tf_op jit(solution)/shard_map/all_to_all | solution.py:42
  162.8 3.1 %fusion.55 = (f32[1,64,64,32]{2,3,1,0:T(8,128)}, f32[1,64,64,32]{2,3,1,0:T(8,128)}) fusion(f32[2,64,64,32]{2,3,1,0:T(8,128)} %bitcast.189), kind=kLoop, calls=%fused_computation.89 | loop fusion | bytes 2097152 | tf_op jit(solution)/shard_map/slice | solution.py:44
  166.0 3.1 %copy.69 = f32[1,64,64,32]{1,3,2,0:T(8,128)} copy(f32[1,64,64,32]{2,3,1,0:T(8,128)} %get-tuple-element.33) | data formatting | bytes 1048576 | tf_op jit(solution)/shard_map/slice | solution.py:44
  169.1 3.2 %copy.70 = f32[1,64,64,32]{1,3,2,0:T(8,128)} copy(f32[1,64,64,32]{2,3,1,0:T(8,128)} %get-tuple-element.32) | data formatting | bytes 1048576 | tf_op jit(solution)/shard_map/slice | solution.py:44
  172.3 3.4 %fusion.11 = bf16[128,1,2,64]{0,3,2,1:T(8,128)(2,1)S(1)} fusion(f32[128,2,64]{0,2,1:T(8,128)S(1)} %convolution_bitcast_fusion.5, f32[64,2,16,64]{0,3,2,1:T(8,128)} %bitcast.183, bf16[128,2,16,64]{0,3,2,1:T(8,128)(2,1)} %multiply_convert_fusion, f32[128,2,16]{0,2,1:T(8,128)S(1)} %bitcast.215), kind=kOutput, calls=%fused_computation.24 | convolution fusion | flops 201883648 | bytes 1163264 | tf_op jit(solution)/shard_map/tgkp,ngkp->tgn/dot_general | solution.py:138
  175.7 2.9 %fusion.10 = bf16[128,1,2,64]{0,3,2,1:T(8,128)(2,1)S(1)} fusion(f32[128,2,64]{0,2,1:T(8,128)S(1)} %convolution_bitcast_fusion.4, f32[64,2,16,64]{0,3,2,1:T(8,128)S(1)} %bitcast.181, bf16[128,2,16,64]{0,3,2,1:T(8,128)(2,1)} %bitcast.186, f32[128,2,16]{0,2,1:T(8,128)S(1)} %bitcast.212), kind=kOutput, calls=%fused_computation.23 | convolution fusion | flops 201883648 | bytes 1163264 | tf_op jit(solution)/shard_map/sgkp,ngkp->sgn/dot_general | solution.py:141
  178.7 2.7 fusion.56
  181.3 6.0 %all-to-all-start.4 = ((f32[256,16,256]{2,0,1:T(8,128)}), f32[256,16,256]{2,0,1:T(8,128)}, u32[]{:S(2)}, u32[]{:S(2)}) async-start(f32[256,16,256]{2,0,1:T(8,128)} %fusion.56), calls=%async_computation.5 | async-start | bytes 8388608 | tf_op jit(solution)/shard_map/all_to_all | solution.py:245
  189.2 2.8 %fusion.31 = f32[2,16,64,128]{3,2,1,0:T(8,128)} fusion(f32[64,2,16,64]{0,3,2,1:T(8,128)} %bitcast.184, bf16[1,128,2,2,64]{1,4,3,2,0:T(8,128)(2,1)S(1)} %bitcast.206), kind=kOutput, calls=%fused_computation.58 | convolution fusion | flops 201326592 | bytes 1605632 | tf_op jit(solution)/shard_map/tgn,ngkp->tgkp/dot_general | solution.py:121
  192.0 48.7 %all-to-all-done.4 = f32[256,16,256]{2,0,1:T(8,128)} async-done(((f32[256,16,256]{2,0,1:T(8,128)}), f32[256,16,256]{2,0,1:T(8,128)}, u32[]{:S(2)}, u32[]{:S(2)}) %all-to-all-start.4) | async-done | bytes 4194336 | tf_op jit(solution)/shard_map/all_to_all | solution.py:245
  244.0 9.7 %all-to-all-start.5 = ((f32[256,8,32]{0,2,1:T(8,128)}), f32[256,8,32]{0,2,1:T(8,128)S(1)}, u32[]{:S(2)}, u32[]{:S(2)}) async-start(f32[256,8,32]{0,2,1:T(8,128)} %bitcast.208), calls=%async_computation.6 | async-start | bytes 524288 | tf_op jit(solution)/shard_map/all_to_all | solution.py:248
  259.2 5.0 %all-to-all-done.5 = f32[256,8,32]{0,2,1:T(8,128)S(1)} async-done(((f32[256,8,32]{0,2,1:T(8,128)}), f32[256,8,32]{0,2,1:T(8,128)S(1)}, u32[]{:S(2)}, u32[]{:S(2)}) %all-to-all-start.5) | async-done | bytes 262176 | tf_op jit(solution)/shard_map/all_to_all | solution.py:248
  (77 shorter events, 40.9 us)
Async XLA Ops:
  26.9 7.3 %copy-start.9 = (f32[1,32,128]{2,1,0:T(8,128)S(1)}, f32[1,32,128]{2,1,0:T(8,128)}, u32[]{:S(2)}) copy-start(f32[1,32,128]{2,1,0:T(8,128)} %param.11) | copy-start | bytes 49156
  26.9 7.7 %copy-start.7 = (bf16[1,128,2048]{2,1,0:T(8,128)(2,1)S(1)}, bf16[1,128,2048]{2,1,0:T(8,128)(2,1)}, u32[]{:S(2)}) copy-start(bf16[1,128,2048]{2,1,0:T(8,128)(2,1)} %param.9) | copy-start | bytes 1572868
  26.9 8.7 %copy-start.8 = (bf16[1,128,2048]{2,1,0:T(8,128)(2,1)S(1)}, bf16[1,128,2048]{2,1,0:T(8,128)(2,1)}, u32[]{:S(2)}) copy-start(bf16[1,128,2048]{2,1,0:T(8,128)(2,1)} %param.13) | copy-start | bytes 1572868
  26.9 33.5 %all-to-all-start.1 = ((bf16[16,8,32,256]{3,2,1,0:T(8,128)(2,1)}), bf16[16,8,32,256]{3,2,1,0:T(8,128)(2,1)S(1)}, u32[]{:S(2)}, u32[]{:S(2)}) async-start(bf16[16,8,32,256]{3,2,1,0:T(8,128)(2,1)} %broadcast_in_dim.95), calls=%async_computation.1 | async-start | bytes 4194304 | tf_op jit(solution)/shard_map/all_to_all | solution.py:165
  124.7 34.2 %all-to-all-start.3 = ((f32[64,1,4096]{2,1,0:T(1,128)}), f32[64,1,4096]{2,1,0:T(1,128)}, u32[]{:S(2)}, u32[]{:S(2)}) async-start(f32[64,1,4096]{2,1,0:T(1,128)} %copy.67), calls=%async_computation.3 | async-start | bytes 2097152 | tf_op jit(solution)/shard_map/all_to_all | solution.py:42
  132.6 1.6 copy-start.3
  134.2 2.4 copy-start.10
  172.3 3.4 %copy-start.1 = (f32[1,64,64,32]{1,3,2,0:T(8,128)S(1)}, f32[1,64,64,32]{1,3,2,0:T(8,128)}, u32[]{:S(2)}) copy-start(f32[1,64,64,32]{1,3,2,0:T(8,128)} %copy.70) | copy-start | bytes 1572868
  172.3 6.3 %copy-start.6 = (bf16[4096,128]{1,0:T(8,128)(2,1)S(1)}, bf16[4096,128]{1,0:T(8,128)(2,1)}, u32[]{:S(2)}) copy-start(bf16[4096,128]{1,0:T(8,128)(2,1)} %copy.83) | copy-start | bytes 3145732
  181.3 59.4 %all-to-all-start.4 = ((f32[256,16,256]{2,0,1:T(8,128)}), f32[256,16,256]{2,0,1:T(8,128)}, u32[]{:S(2)}, u32[]{:S(2)}) async-start(f32[256,16,256]{2,0,1:T(8,128)} %fusion.56), calls=%async_computation.5 | async-start | bytes 8388608 | tf_op jit(solution)/shard_map/all_to_all | solution.py:245
  187.3 77.5 %reduce-scatter.2.cloned.1.call-start = ((), (), s32[]{:S(2)}) async-start(), calls=%async_computation.7 | async-start | bytes 1572864 | tf_op jit(solution)/shard_map/reduce_scatter | solution.py:240
  192.0 61.7 %copy-start.2 = (f32[1,64,64,32]{1,3,2,0:T(8,128)S(1)}, f32[1,64,64,32]{1,3,2,0:T(8,128)}, u32[]{:S(2)}) copy-start(f32[1,64,64,32]{1,3,2,0:T(8,128)} %copy.70) | copy-start | bytes 1572868
  243.2 11.2 %copy-start = (f32[1,128,2048]{1,2,0:T(8,128)S(1)}, f32[1,128,2048]{1,2,0:T(8,128)}, u32[]{:S(2)}) copy-start(f32[1,128,2048]{1,2,0:T(8,128)} %convert_element_type.118) | copy-start | bytes 3145732
  244.0 20.1 %all-to-all-start.5 = ((f32[256,8,32]{0,2,1:T(8,128)}), f32[256,8,32]{0,2,1:T(8,128)S(1)}, u32[]{:S(2)}, u32[]{:S(2)}) async-start(f32[256,8,32]{0,2,1:T(8,128)} %bitcast.208), calls=%async_computation.6 | async-start | bytes 524288 | tf_op jit(solution)/shard_map/all_to_all | solution.py:248
  253.7 1.2 copy-start.4
  253.7 1.5 copy-start.5
Sparse Core Ops, SparseCore 0:
  191.2 11.2 reduce-scatter.1

commit v12 on v11

--- a/solution.py
+++ b/solution.py
@@ -13,22 +13,17 @@
 INNER = ROWS[-1]
 
 
-def carried_both(log_total, state, adjoint, axis):
+def carried_both(log_total, state_rows, adjoint_rows, axis, rows, cols):
     count = lax.axis_size(axis)
-    rows, cols = state.shape
     chunk = cols // count
     assert HEAD_DIM % chunk == 0
-    flat = rows * chunk
-
-    def rows_of(a):
-        return a.reshape(rows, count, chunk).transpose(1, 0, 2).reshape(count, flat)
 
     chunk_logs = jnp.repeat(log_total, cols // log_total.shape[0]).reshape(count, chunk)
     packed = jnp.concatenate(
-        [rows_of(state), rows_of(adjoint), chunk_logs, jnp.zeros_like(chunk_logs)], 1
+        [state_rows, adjoint_rows, chunk_logs, jnp.zeros_like(chunk_logs)], 1
     )
     got = lax.all_to_all(packed[:, None], axis, 0, 0, tiled=True)[:, 0]
-    logs = got[:, 2 * flat]
+    logs = got[:, 2 * rows * chunk]
     place = jnp.arange(count)
     before = place[None, :] < place[:, None]
     gaps = jnp.dot(
@@ -37,11 +32,34 @@
         precision=lax.Precision.HIGHEST,
     )
     carry = jnp.where(before, jnp.exp(jnp.where(before, gaps, 0.0)), 0.0)
+    flat = rows * chunk
     fwd = jnp.dot(carry, got[:, :flat], precision=lax.Precision.HIGHEST)
     bwd = jnp.dot(carry.T, got[:, flat : 2 * flat], precision=lax.Precision.HIGHEST)
     back = lax.all_to_all(jnp.concatenate([fwd, bwd], 1)[:, None], axis, 0, 0, tiled=True)
     back = back.reshape(count, 2, rows, chunk).transpose(1, 2, 0, 3).reshape(2, rows, cols)
     return back[0], back[1]
+
+
+def summary_rows(b_vals, c_vals, x_vals, dy_round, rate_vals, count):
+    block_len = x_vals.shape[0]
+    head_count = x_vals.shape[1]
+    group_count = b_vals.shape[1]
+    per_group = head_count // group_count
+    chunk = head_count * HEAD_DIM // count
+    cumlog = jnp.cumsum(rate_vals, axis=1)
+    final_log = cumlog[:, -1]
+    to_end = jnp.exp(final_log[:, None] - cumlog)
+    from_start = jnp.exp(cumlog)
+    shape = (block_len, group_count, per_group, HEAD_DIM // chunk, chunk)
+    x_scaled = (x_vals.astype(jnp.float32) * to_end.T[:, :, None]).reshape(shape)
+    dy_scaled = (dy_round.astype(jnp.float32) * from_start.T[:, :, None]).reshape(shape)
+    state_part = jnp.einsum(
+        "qgn,qgkhc->gkhnc", b_vals.astype(jnp.float32), x_scaled, precision=lax.Precision.HIGHEST
+    )
+    adjoint_part = jnp.einsum(
+        "qgn,qgkhc->gkhnc", c_vals.astype(jnp.float32), dy_scaled, precision=lax.Precision.HIGHEST
+    )
+    return state_part.reshape(count, -1), adjoint_part.reshape(count, -1)
 
 
 def span_summary(b_vals, c_vals, x_vals, dy_round, rate_vals):
@@ -181,34 +199,17 @@
         jnp.bfloat16
     )
     rate_vals = log_decay[0].reshape(head_count, nblocks, SPAN)
-    summaries = [
-        span_summary(bc_vals[0, :, 0], bc_vals[0, :, 1], x_vals[0], dy_round[0], rate_vals[:, 0])
-    ]
-    dev_decay = jnp.ones((head_count,), jnp.float32)
-    dev_state = jnp.zeros((STATE, head_count * HEAD_DIM), jnp.float32)
-    dev_adjoint = jnp.zeros((STATE, head_count * HEAD_DIM), jnp.float32)
-    block_id = 0
-    dev_state = (
-        dev_state * jnp.repeat(summaries[block_id][0], HEAD_DIM)[None, :] + summaries[block_id][1]
-    )
-    dev_decay = dev_decay * summaries[block_id][0]
+    assert nblocks == 1
     dev_log = jnp.sum(jnp.cumsum(rate_vals, axis=2)[:, :, -1], axis=1)
-    for block_id in reversed(range(nblocks)):
-        dev_adjoint = (
-            dev_adjoint * jnp.repeat(summaries[block_id][0], HEAD_DIM)[None, :]
-            + summaries[block_id][2]
-        )
-    state_start, adjoint_end = carried_both(dev_log, dev_state, dev_adjoint, CTX)
-    running = state_start
-    block_id = 0
-    states_in = running
-    adjoints_out = [None] * nblocks
-    running = adjoint_end
-    for block_id in reversed(range(nblocks)):
-        adjoints_out[block_id] = running
-        running = (
-            running * jnp.repeat(summaries[block_id][0], HEAD_DIM)[None, :] + summaries[block_id][2]
-        )
+    ctx_count = lax.axis_size(CTX)
+    state_rows, adjoint_rows = summary_rows(
+        bc_vals[0, :, 0], bc_vals[0, :, 1], x_vals[0], dy_round[0], rate_vals[:, 0], ctx_count
+    )
+    state_start, adjoint_end = carried_both(
+        dev_log, state_rows, adjoint_rows, CTX, STATE, head_count * HEAD_DIM
+    )
+    states_in = state_start
+    adjoints_out = [adjoint_end]
     results = [
         span_full(
             bc_vals[0, :, 0],

time: 273 us -> 273 us (level)
  other arithmetic: 19.6 us -> 12.7 us
  local copies, waits for them, and re-layouts: 39.8 us -> 46.2 us
    transpose x0 -> x2, local copies, waits for them, and re-layouts: none -> 6.37 us  [the longest x1 3.19 us: summary_rows(): jnp.einsum('qgn,qgkhc->gkhnc', c_vals.astype(jnp.float32), dy_scaled, pre...]
    broadcast_in_dim x1 -> x0, other arithmetic: 5.01 us -> none  [carried_both(): got = lax.all_to_all(packed[:, None], axis, 0, 0, tiled=True)[:, 0]]
    unnamed x29 -> x31, local copies, waits for them, and re-layouts: 7.78 us -> 7.79 us
where the time goes in v12:
time: 273 us; the launch traced here: 271 us
  waiting for transfers between devices  88.7 us (32%)
  blocking collectives  53.5 us (20%)
  local copies, waits for them, and re-layouts  46.2 us (17%)
  starting transfers between devices  28.6 us (10%)
  matrix products  27.2 us (10%)
  between operations  14.3 us (5%)
  other arithmetic  12.7 us (5%)
    all_to_all x1, waiting for transfers between devices, body(): lax.all_to_all(proj_terms.reshape(col_count, outer_count, -1), OUTER, 1,...  48.6 us
    all_to_all x1, blocking collectives, carried_both(): got = lax.all_to_all(packed[:, None], axis, 0, 0, tiled=True)[:, 0]  36.2 us
    all_to_all x1, waiting for transfers between devices, carried_both(): lax.all_to_all(jnp.concatenate([fwd, bwd], 1)[:, None], axis, 0, 0, tiled...  19.2 us
    all_to_all x1, blocking collectives, body(): lax.all_to_all(jnp.broadcast_to(weight_local[None], (inner_count,) + weig...  17.4 us
    all_to_all x1, waiting for transfers between devices, body(): lax.all_to_all(jnp.broadcast_to(weight_inner[None], (outer_count,) + weig...  15.9 us
    all_to_all x1, starting transfers between devices, body(): lax.all_to_all(proj_parts.reshape(col_count, inner_count, -1), INNER, 1,...  9.68 us
    slice x3, local copies, waits for them, and re-layouts, carried_both(): return (back[0], back[1])  9.4 us
    unnamed x31, local copies, waits for them, and re-layouts  7.79 us
  transfers between devices with their start and end apart: 5, of which 4 were waited for; matrix products, arithmetic and copies ran while one was open for 12% of the time, Pallas kernels for 0%

profile of v12, /device:TPU:24, one launch (start us, length us, event | category | flops | bytes accessed | tf_op | source)
XLA Modules:
  0.0 271.2 jit_solution(86578468014527265)
XLA Ops:
  7.9 17.4 %all_to_all.30 = bf16[8,32,256]{2,1,0:T(8,128)(2,1)S(1)} all-to-all(bf16[8,32,256]{2,1,0:T(8,128)(2,1)S(1)} %broadcast_in_dim.90), channel_id=1, replica_groups=mesh['dp'=2,'ylo'=2,'x'=4,'z'=8,'head'=2] {'z'}, dimensions={0} | all-to-all | bytes 262144 | tf_op jit(solution)/shard_map/all_to_all | solution.py:176
  26.9 7.3 %all-to-all-start.1 = ((bf16[16,8,32,256]{3,2,1,0:T(8,128)(2,1)}), bf16[16,8,32,256]{3,2,1,0:T(8,128)(2,1)S(1)}, u32[]{:S(2)}, u32[]{:S(2)}) async-start(bf16[16,8,32,256]{3,2,1,0:T(8,128)(2,1)} %broadcast_in_dim.91), calls=%async_computation.1 | async-start | bytes 4194304 | tf_op jit(solution)/shard_map/all_to_all | solution.py:183
  44.4 15.9 %all-to-all-done.1 = bf16[16,8,32,256]{3,2,1,0:T(8,128)(2,1)S(1)} async-done(((bf16[16,8,32,256]{3,2,1,0:T(8,128)(2,1)}), bf16[16,8,32,256]{3,2,1,0:T(8,128)(2,1)S(1)}, u32[]{:S(2)}, u32[]{:S(2)}) %all-to-all-start.1) | async-done | bytes 2097184 | tf_op jit(solution)/shard_map/all_to_all | solution.py:183
  62.1 2.8 %convolution_bitcast_fusion.1 = f32[2,16,2,64,32]{3,4,2,1,0:T(8,128)} fusion(f32[128,2,16,2,32]{0,4,3,2,1:T(8,128)} %bitcast.188, f32[128,2,16]{0,2,1:T(8,128)S(1)} %bitcast.215, bf16[1,128,2,2,64]{1,4,3,2,0:T(8,128)(2,1)S(1)} %bitcast.205), kind=kOutput, calls=%fused_computation.7 | convolution fusion | flops 201588736 | bytes 1622016 | tf_op jit(solution)/shard_map/qgn,qgkhc->gkhnc/dot_general | solution.py:56
  64.9 3.2 %copy.64 = f32[2,16,2,64,32]{4,3,2,1,0:T(8,128)} copy(f32[2,16,2,64,32]{3,4,2,1,0:T(8,128)} %convolution_bitcast_fusion.1) | data formatting | bytes 1048576 | tf_op jit(solution)/shard_map/qgn,qgkhc->gkhnc/transpose | solution.py:56
  68.1 3.1 %reshape.152 = f32[64,2048]{1,0:T(8,128)} reshape(f32[2,16,2,64,32]{4,3,2,1,0:T(8,128)} %copy.64) | data formatting | bytes 1048576 | tf_op jit(solution)/shard_map/reshape | solution.py:62
  71.2 3.1 %convolution_bitcast_fusion = f32[2,16,2,64,32]{3,4,2,1,0:T(8,128)} fusion(f32[128,2,16]{0,2,1:T(8,128)S(1)} %bitcast.221, f32[128,2,16,2,32]{0,4,3,2,1:T(8,128)S(1)} %bitcast.180, f32[128,2,16,2,32]{0,4,3,2,1:T(8,128)} %bitcast.184, bf16[1,128,2,2,64]{1,4,3,2,0:T(8,128)(2,1)S(1)} %bitcast.206), kind=kOutput, calls=%fused_computation.6 | convolution fusion | flops 203423744 | bytes 2670592 | tf_op jit(solution)/shard_map/qgn,qgkhc->gkhnc/dot_general | solution.py:59
  74.3 3.2 %copy.65 = f32[2,16,2,64,32]{4,3,2,1,0:T(8,128)} copy(f32[2,16,2,64,32]{3,4,2,1,0:T(8,128)} %convolution_bitcast_fusion) | data formatting | bytes 1048576 | tf_op jit(solution)/shard_map/qgn,qgkhc->gkhnc/transpose | solution.py:59
  77.5 3.1 %reshape.153 = f32[64,2048]{1,0:T(8,128)} reshape(f32[2,16,2,64,32]{4,3,2,1,0:T(8,128)} %copy.65) | data formatting | bytes 1048576 | tf_op jit(solution)/shard_map/reshape | solution.py:62
  85.1 36.2 %all_to_all.31 = f32[64,1,4160]{2,1,0:T(1,128)S(1)} all-to-all(f32[64,1,4160]{2,1,0:T(1,128)S(1)} %copy.66), channel_id=1, replica_groups=mesh['dp'=2,'ylo'=2,'x'=4,'z'=8,'head'=2] {'ylo','x','z'}, dimensions={0} | all-to-all | bytes 2129920 | tf_op jit(solution)/shard_map/all_to_all | solution.py:25
  125.0 5.6 %all-to-all-start.3 = ((f32[64,1,4096]{2,1,0:T(1,128)}), f32[64,1,4096]{2,1,0:T(1,128)}, u32[]{:S(2)}, u32[]{:S(2)}) async-start(f32[64,1,4096]{2,1,0:T(1,128)} %copy.67), calls=%async_computation.3 | async-start | bytes 2097152 | tf_op jit(solution)/shard_map/all_to_all | solution.py:38
  140.0 19.2 %all-to-all-done.3 = f32[64,1,4096]{2,1,0:T(1,128)} async-done(((f32[64,1,4096]{2,1,0:T(1,128)}), f32[64,1,4096]{2,1,0:T(1,128)}, u32[]{:S(2)}, u32[]{:S(2)}) %all-to-all-start.3) | async-done | bytes 1048608 | tf_op jit(solution)/shard_map/all_to_all | solution.py:38
  159.2 3.9 %copy.68 = f32[64,1,4096]{0,2,1:T(8,128)} copy(f32[64,1,4096]{2,1,0:T(1,128)} %all-to-all-done.3) | data formatting | bytes 2097152 | tf_op jit(solution)/shard_map/all_to_all | solution.py:38
  163.1 3.1 %fusion.61 = (f32[1,64,64,32]{2,3,1,0:T(8,128)}, f32[1,64,64,32]{2,3,1,0:T(8,128)}) fusion(f32[2,64,64,32]{2,3,1,0:T(8,128)} %bitcast.192), kind=kLoop, calls=%fused_computation.92 | loop fusion | bytes 2097152 | tf_op jit(solution)/shard_map/slice | solution.py:40
  166.2 3.1 %copy.69 = f32[1,64,64,32]{1,3,2,0:T(8,128)} copy(f32[1,64,64,32]{2,3,1,0:T(8,128)} %get-tuple-element.33) | data formatting | bytes 1048576 | tf_op jit(solution)/shard_map/slice | solution.py:40
  169.4 3.1 %copy.70 = f32[1,64,64,32]{1,3,2,0:T(8,128)} copy(f32[1,64,64,32]{2,3,1,0:T(8,128)} %get-tuple-element.32) | data formatting | bytes 1048576 | tf_op jit(solution)/shard_map/slice | solution.py:40
  172.5 3.6 %fusion.10 = bf16[128,1,2,64]{0,3,2,1:T(8,128)(2,1)S(1)} fusion(f32[128,2,64]{0,2,1:T(8,128)S(1)} %convolution_bitcast_fusion.6, f32[64,2,16,64]{0,3,2,1:T(8,128)} %bitcast.190, f32[128,2,16,64]{0,3,2,1:T(8,128)} %bitcast.189, f32[128,2,16]{0,2,1:T(8,128)S(1)} %bitcast.216), kind=kOutput, calls=%fused_computation.24 | convolution fusion | flops 201621504 | bytes 1687552 | tf_op jit(solution)/shard_map/sgkp,ngkp->sgn/dot_general | solution.py:159
  178.2 2.7 fusion.62
  180.8 6.0 %all-to-all-start.4 = ((f32[256,16,256]{2,0,1:T(8,128)}), f32[256,16,256]{2,0,1:T(8,128)}, u32[]{:S(2)}, u32[]{:S(2)}) async-start(f32[256,16,256]{2,0,1:T(8,128)} %fusion.62), calls=%async_computation.5 | async-start | bytes 8388608 | tf_op jit(solution)/shard_map/all_to_all | solution.py:246
  188.8 2.8 %fusion.35 = f32[2,16,64,128]{3,2,1,0:T(8,128)} fusion(f32[64,2,16,64]{0,3,2,1:T(8,128)} %bitcast.200, bf16[1,128,2,2,64]{1,4,3,2,0:T(8,128)(2,1)S(1)} %bitcast.210), kind=kOutput, calls=%fused_computation.60 | convolution fusion | flops 201326592 | bytes 1605632 | tf_op jit(solution)/shard_map/tgn,ngkp->tgkp/dot_general | solution.py:139
  191.6 48.6 %all-to-all-done.4 = f32[256,16,256]{2,0,1:T(8,128)} async-done(((f32[256,16,256]{2,0,1:T(8,128)}), f32[256,16,256]{2,0,1:T(8,128)}, u32[]{:S(2)}, u32[]{:S(2)}) %all-to-all-start.4) | async-done | bytes 4194336 | tf_op jit(solution)/shard_map/all_to_all | solution.py:246
  240.2 2.5 reduce_sum.28
  243.5 9.7 %all-to-all-start.5 = ((f32[256,8,32]{0,2,1:T(8,128)}), f32[256,8,32]{0,2,1:T(8,128)S(1)}, u32[]{:S(2)}, u32[]{:S(2)}) async-start(f32[256,8,32]{0,2,1:T(8,128)} %bitcast.212), calls=%async_computation.6 | async-start | bytes 524288 | tf_op jit(solution)/shard_map/all_to_all | solution.py:249
  258.7 5.0 %all-to-all-done.5 = f32[256,8,32]{0,2,1:T(8,128)S(1)} async-done(((f32[256,8,32]{0,2,1:T(8,128)}), f32[256,8,32]{0,2,1:T(8,128)S(1)}, u32[]{:S(2)}, u32[]{:S(2)}) %all-to-all-start.5) | async-done | bytes 262176 | tf_op jit(solution)/shard_map/all_to_all | solution.py:249
  (76 shorter events, 42.8 us)
Async XLA Ops:
  26.9 7.3 %copy-start.10 = (f32[1,32,128]{2,1,0:T(8,128)S(1)}, f32[1,32,128]{2,1,0:T(8,128)}, u32[]{:S(2)}) copy-start(f32[1,32,128]{2,1,0:T(8,128)} %param.11) | copy-start | bytes 49156
  26.9 7.7 %copy-start.8 = (bf16[1,128,2048]{2,1,0:T(8,128)(2,1)S(1)}, bf16[1,128,2048]{2,1,0:T(8,128)(2,1)}, u32[]{:S(2)}) copy-start(bf16[1,128,2048]{2,1,0:T(8,128)(2,1)} %param.9) | copy-start | bytes 1572868
  26.9 8.7 %copy-start.9 = (bf16[1,128,2048]{2,1,0:T(8,128)(2,1)S(1)}, bf16[1,128,2048]{2,1,0:T(8,128)(2,1)}, u32[]{:S(2)}) copy-start(bf16[1,128,2048]{2,1,0:T(8,128)(2,1)} %param.13) | copy-start | bytes 1572868
  26.9 33.5 %all-to-all-start.1 = ((bf16[16,8,32,256]{3,2,1,0:T(8,128)(2,1)}), bf16[16,8,32,256]{3,2,1,0:T(8,128)(2,1)S(1)}, u32[]{:S(2)}, u32[]{:S(2)}) async-start(bf16[16,8,32,256]{3,2,1,0:T(8,128)(2,1)} %broadcast_in_dim.91), calls=%async_computation.1 | async-start | bytes 4194304 | tf_op jit(solution)/shard_map/all_to_all | solution.py:183
  125.0 34.2 %all-to-all-start.3 = ((f32[64,1,4096]{2,1,0:T(1,128)}), f32[64,1,4096]{2,1,0:T(1,128)}, u32[]{:S(2)}, u32[]{:S(2)}) async-start(f32[64,1,4096]{2,1,0:T(1,128)} %copy.67), calls=%async_computation.3 | async-start | bytes 2097152 | tf_op jit(solution)/shard_map/all_to_all | solution.py:38
  132.9 1.6 copy-start.3
  134.5 2.4 copy-start.11
  172.5 3.6 %copy-start = (f32[1,128,2048]{1,2,0:T(8,128)S(1)}, f32[1,128,2048]{1,2,0:T(8,128)}, u32[]{:S(2)}) copy-start(f32[1,128,2048]{1,2,0:T(8,128)} %convert_element_type.150) | copy-start | bytes 3145732
  172.5 3.6 %copy-start.6 = (f32[1,64,64,32]{1,3,2,0:T(8,128)S(1)}, f32[1,64,64,32]{1,3,2,0:T(8,128)}, u32[]{:S(2)}) copy-start(f32[1,64,64,32]{1,3,2,0:T(8,128)} %copy.69) | copy-start | bytes 1572868
  176.1 2.0 copy-start.7
  180.8 59.3 %all-to-all-start.4 = ((f32[256,16,256]{2,0,1:T(8,128)}), f32[256,16,256]{2,0,1:T(8,128)}, u32[]{:S(2)}, u32[]{:S(2)}) async-start(f32[256,16,256]{2,0,1:T(8,128)} %fusion.62), calls=%async_computation.5 | async-start | bytes 8388608 | tf_op jit(solution)/shard_map/all_to_all | solution.py:246
  186.8 77.5 %reduce-scatter.2.cloned.1.call-start = ((), (), s32[]{:S(2)}) async-start(), calls=%async_computation.7 | async-start | bytes 1572864 | tf_op jit(solution)/shard_map/reduce_scatter | solution.py:241
  191.6 61.6 %copy-start.2 = (f32[1,64,64,32]{1,3,2,0:T(8,128)S(1)}, f32[1,64,64,32]{1,3,2,0:T(8,128)}, u32[]{:S(2)}) copy-start(f32[1,64,64,32]{1,3,2,0:T(8,128)} %copy.70) | copy-start | bytes 1572868
  242.7 11.2 %copy-start.1 = (f32[1,128,2048]{1,2,0:T(8,128)S(1)}, f32[1,128,2048]{1,2,0:T(8,128)}, u32[]{:S(2)}) copy-start(f32[1,128,2048]{1,2,0:T(8,128)} %convert_element_type.150) | copy-start | bytes 3145732
  243.5 20.2 %all-to-all-start.5 = ((f32[256,8,32]{0,2,1:T(8,128)}), f32[256,8,32]{0,2,1:T(8,128)S(1)}, u32[]{:S(2)}, u32[]{:S(2)}) async-start(f32[256,8,32]{0,2,1:T(8,128)} %bitcast.212), calls=%async_computation.6 | async-start | bytes 524288 | tf_op jit(solution)/shard_map/all_to_all | solution.py:249
  253.2 1.2 copy-start.4
  253.2 1.5 copy-start.5
Sparse Core Ops, SparseCore 0:
  190.7 11.2 reduce-scatter.1

commit v13 on v12

--- a/solution.py
+++ b/solution.py
@@ -36,8 +36,8 @@
     fwd = jnp.dot(carry, got[:, :flat], precision=lax.Precision.HIGHEST)
     bwd = jnp.dot(carry.T, got[:, flat : 2 * flat], precision=lax.Precision.HIGHEST)
     back = lax.all_to_all(jnp.concatenate([fwd, bwd], 1)[:, None], axis, 0, 0, tiled=True)
-    back = back.reshape(count, 2, rows, chunk).transpose(1, 2, 0, 3).reshape(2, rows, cols)
-    return back[0], back[1]
+    back = back.reshape(count, 2, rows, chunk)
+    return back[:, 0], back[:, 1]
 
 
 def summary_rows(b_vals, c_vals, x_vals, dy_round, rate_vals, count):
@@ -134,10 +134,11 @@
     (y_local, vals_local, c_local, b_local), state_in, adjoint_out = lax.optimization_barrier(
         ((y_local, vals_local, c_local, b_local), state_in, adjoint_out)
     )
-    state_four = state_in.reshape(STATE, group_count, per_group, HEAD_DIM)
-    adjoint_four = adjoint_out.reshape(STATE, group_count, per_group, HEAD_DIM)
+    width = state_in.shape[-1]
+    state_five = state_in.reshape(group_count, per_group, HEAD_DIM // width, STATE, width)
+    adjoint_five = adjoint_out.reshape(group_count, per_group, HEAD_DIM // width, STATE, width)
     y_inter = jnp.einsum(
-        "tgn,ngkp->tgkp", c_wide, state_four, precision=lax.Precision.HIGHEST
+        "tgn,gkhnc->tgkhc", c_wide, state_five, precision=lax.Precision.HIGHEST
     ).reshape(block_len, head_count, HEAD_DIM)
     output_pre = y_local + y_inter * from_start.T[:, :, None]
     gate_wide = gate_vals.astype(jnp.float32)
@@ -146,18 +147,20 @@
         dout_vals.astype(jnp.float32) * output_pre * gate_sig * (1.0 + gate_wide * (1.0 - gate_sig))
     ).astype(jnp.bfloat16)
     x_inter = jnp.einsum(
-        "sgn,ngkp->sgkp", b_wide, adjoint_four, precision=lax.Precision.HIGHEST
+        "sgn,gkhnc->sgkhc", b_wide, adjoint_five, precision=lax.Precision.HIGHEST
     ).reshape(block_len, head_count, HEAD_DIM)
     grad_vals = vals_local + x_inter * to_end.T[:, :, None]
     dy_scaled = (dy_wide * from_start.T[:, :, None]).reshape(
-        block_len, group_count, per_group, HEAD_DIM
-    )
-    x_scaled = (x_wide * to_end.T[:, :, None]).reshape(block_len, group_count, per_group, HEAD_DIM)
+        block_len, group_count, per_group, HEAD_DIM // width, width
+    )
+    x_scaled = (x_wide * to_end.T[:, :, None]).reshape(
+        block_len, group_count, per_group, HEAD_DIM // width, width
+    )
     c_grad = c_local + jnp.einsum(
-        "tgkp,ngkp->tgn", dy_scaled, state_four, precision=lax.Precision.HIGHEST
+        "tgkhc,gkhnc->tgn", dy_scaled, state_five, precision=lax.Precision.HIGHEST
     )
     b_grad = b_local + jnp.einsum(
-        "sgkp,ngkp->sgn", x_scaled, adjoint_four, precision=lax.Precision.HIGHEST
+        "sgkhc,gkhnc->sgn", x_scaled, adjoint_five, precision=lax.Precision.HIGHEST
     )
     return (grad_vals.astype(jnp.bfloat16), grad_gate, jnp.stack([b_grad, c_grad], axis=1))
 

time: 273 us -> 272 us (level)
    slice x3 -> x0, local copies, waits for them, and re-layouts: 9.4 us -> none  [carried_both(): return (back[0], back[1])]
    optimization_barrier x0 -> x2, local copies, waits for them, and re-layouts: none -> 6.28 us  [span_full(): lax.optimization_barrier(((y_local, vals_local, c_local, b_local), state_...]
    squeeze x0 -> x1, local copies, waits for them, and re-layouts: none -> 3.12 us  [carried_both(): return (back[:, 0], back[:, 1])]
where the time goes in v13:
time: 272 us; the launch traced here: 271 us
  waiting for transfers between devices  88.2 us (32%)
  blocking collectives  53.5 us (20%)
  local copies, waits for them, and re-layouts  46.2 us (17%)
  starting transfers between devices  28.6 us (11%)
  matrix products  26.7 us (10%)
  between operations  14.3 us (5%)
  other arithmetic  13.2 us (5%)
    all_to_all x1, waiting for transfers between devices, body(): lax.all_to_all(proj_terms.reshape(col_count, outer_count, -1), OUTER, 1,...  48.6 us
    all_to_all x1, blocking collectives, carried_both(): got = lax.all_to_all(packed[:, None], axis, 0, 0, tiled=True)[:, 0]  36.2 us
    all_to_all x1, waiting for transfers between devices, carried_both(): lax.all_to_all(jnp.concatenate([fwd, bwd], 1)[:, None], axis, 0, 0, tiled...  19.2 us
    all_to_all x1, blocking collectives, body(): lax.all_to_all(jnp.broadcast_to(weight_local[None], (inner_count,) + weig...  17.4 us
    all_to_all x1, waiting for transfers between devices, body(): lax.all_to_all(jnp.broadcast_to(weight_inner[None], (outer_count,) + weig...  15.4 us
    all_to_all x1, starting transfers between devices, body(): lax.all_to_all(proj_parts.reshape(col_count, inner_count, -1), INNER, 1,...  9.69 us
    unnamed x31, local copies, waits for them, and re-layouts  7.79 us
    all_to_all x1, starting transfers between devices, body(): lax.all_to_all(jnp.broadcast_to(weight_inner[None], (outer_count,) + weig...  7.3 us
  transfers between devices with their start and end apart: 5, of which 4 were waited for; matrix products, arithmetic and copies ran while one was open for 12% of the time, Pallas kernels for 0%

profile of v13, /device:TPU:24, one launch (start us, length us, event | category | flops | bytes accessed | tf_op | source)
XLA Modules:
  0.0 270.6 jit_solution(15856649506825513297)
XLA Ops:
  7.9 17.4 %all_to_all.30 = bf16[8,32,256]{2,1,0:T(8,128)(2,1)S(1)} all-to-all(bf16[8,32,256]{2,1,0:T(8,128)(2,1)S(1)} %broadcast_in_dim.90), channel_id=1, replica_groups=mesh['dp'=2,'ylo'=2,'x'=4,'z'=8,'head'=2] {'z'}, dimensions={0} | all-to-all | bytes 262144 | tf_op jit(solution)/shard_map/all_to_all | solution.py:179
  26.9 7.3 %all-to-all-start.1 = ((bf16[16,8,32,256]{3,2,1,0:T(8,128)(2,1)}), bf16[16,8,32,256]{3,2,1,0:T(8,128)(2,1)S(1)}, u32[]{:S(2)}, u32[]{:S(2)}) async-start(bf16[16,8,32,256]{3,2,1,0:T(8,128)(2,1)} %broadcast_in_dim.91), calls=%async_computation.1 | async-start | bytes 4194304 | tf_op jit(solution)/shard_map/all_to_all | solution.py:186
  42.3 2.5 convert_multiply_fusion.1
  44.9 15.4 %all-to-all-done.1 = bf16[16,8,32,256]{3,2,1,0:T(8,128)(2,1)S(1)} async-done(((bf16[16,8,32,256]{3,2,1,0:T(8,128)(2,1)}), bf16[16,8,32,256]{3,2,1,0:T(8,128)(2,1)S(1)}, u32[]{:S(2)}, u32[]{:S(2)}) %all-to-all-start.1) | async-done | bytes 2097184 | tf_op jit(solution)/shard_map/all_to_all | solution.py:186
  62.1 2.7 convolution_bitcast_fusion.1
  64.8 3.2 %copy.68 = f32[2,16,2,64,32]{4,3,2,1,0:T(8,128)} copy(f32[2,16,2,64,32]{3,4,2,1,0:T(8,128)} %convolution_bitcast_fusion.1) | data formatting | bytes 1048576 | tf_op jit(solution)/shard_map/qgn,qgkhc->gkhnc/transpose | solution.py:56
  68.0 3.1 %reshape.136 = f32[64,2048]{1,0:T(8,128)} reshape(f32[2,16,2,64,32]{4,3,2,1,0:T(8,128)} %copy.68) | data formatting | bytes 1048576 | tf_op jit(solution)/shard_map/reshape | solution.py:62
  71.1 2.8 %convolution_bitcast_fusion = f32[2,16,2,64,32]{3,4,2,1,0:T(8,128)} fusion(f32[128,2,16,2,32]{0,4,3,2,1:T(8,128)} %convert_multiply_fusion.1, bf16[1,128,2,2,64]{1,4,3,2,0:T(8,128)(2,1)S(1)} %bitcast.181), kind=kOutput, calls=%fused_computation.6 | convolution fusion | flops 201326592 | bytes 1605632 | tf_op jit(solution)/shard_map/qgn,qgkhc->gkhnc/dot_general | solution.py:59
  73.9 3.2 %copy.69 = f32[2,16,2,64,32]{4,3,2,1,0:T(8,128)} copy(f32[2,16,2,64,32]{3,4,2,1,0:T(8,128)} %convolution_bitcast_fusion) | data formatting | bytes 1048576 | tf_op jit(solution)/shard_map/qgn,qgkhc->gkhnc/transpose | solution.py:59
  77.1 3.1 %reshape.137 = f32[64,2048]{1,0:T(8,128)} reshape(f32[2,16,2,64,32]{4,3,2,1,0:T(8,128)} %copy.69) | data formatting | bytes 1048576 | tf_op jit(solution)/shard_map/reshape | solution.py:62
  84.7 36.2 %all_to_all.31 = f32[64,1,4160]{2,1,0:T(1,128)S(1)} all-to-all(f32[64,1,4160]{2,1,0:T(1,128)S(1)} %copy.70), channel_id=1, replica_groups=mesh['dp'=2,'ylo'=2,'x'=4,'z'=8,'head'=2] {'ylo','x','z'}, dimensions={0} | all-to-all | bytes 2129920 | tf_op jit(solution)/shard_map/all_to_all | solution.py:25
  124.6 5.6 %all-to-all-start.3 = ((f32[64,1,4096]{2,1,0:T(1,128)}), f32[64,1,4096]{2,1,0:T(1,128)}, u32[]{:S(2)}, u32[]{:S(2)}) async-start(f32[64,1,4096]{2,1,0:T(1,128)} %copy.71), calls=%async_computation.3 | async-start | bytes 2097152 | tf_op jit(solution)/shard_map/all_to_all | solution.py:38
  139.6 19.2 %all-to-all-done.3 = f32[64,1,4096]{2,1,0:T(1,128)} async-done(((f32[64,1,4096]{2,1,0:T(1,128)}), f32[64,1,4096]{2,1,0:T(1,128)}, u32[]{:S(2)}, u32[]{:S(2)}) %all-to-all-start.3) | async-done | bytes 1048608 | tf_op jit(solution)/shard_map/all_to_all | solution.py:38
  158.8 3.9 %copy.72 = f32[64,1,4096]{0,2,1:T(8,128)} copy(f32[64,1,4096]{2,1,0:T(1,128)} %all-to-all-done.3) | data formatting | bytes 2097152 | tf_op jit(solution)/shard_map/all_to_all | solution.py:38
  162.7 3.1 %slice_bitcast_fusion = (f32[64,64,32]{0,2,1:T(8,128)}, f32[64,64,32]{0,2,1:T(8,128)}) fusion(f32[64,2,64,32]{0,3,2,1:T(8,128)} %bitcast.169), kind=kLoop, calls=%fused_computation.27 | loop fusion | bytes 2097152 | tf_op jit(solution)/shard_map/squeeze | solution.py:40
  165.8 3.1 %copy.76 = f32[64,64,32]{1,2,0:T(8,128)} copy(f32[64,64,32]{0,2,1:T(8,128)} %get-tuple-element.13) | data formatting | bytes 1048576 | tf_op jit(solution)/shard_map/optimization_barrier | solution.py:134
  169.0 3.1 %copy.73 = f32[64,64,32]{1,2,0:T(8,128)} copy(f32[64,64,32]{0,2,1:T(8,128)} %get-tuple-element.11) | data formatting | bytes 1048576 | tf_op jit(solution)/shard_map/optimization_barrier | solution.py:134
  172.1 3.5 %fusion.11 = bf16[128,1,2,64]{0,3,2,1:T(8,128)(2,1)S(1)} fusion(f32[128,2,64]{0,2,1:T(8,128)S(1)} %convolution_bitcast_fusion.7, f32[128,2,16,2,32]{0,4,3,2,1:T(8,128)} %convert_multiply_fusion.1, f32[2,16,2,64,32]{3,4,2,1,0:T(8,128)} %bitcast.163), kind=kOutput, calls=%fused_computation.25 | convolution fusion | flops 201359360 | bytes 1671168 | tf_op jit(solution)/shard_map/tgkhc,gkhnc->tgn/dot_general | solution.py:159
  177.6 2.7 fusion.46
  180.3 6.0 %all-to-all-start.4 = ((f32[256,16,256]{2,0,1:T(8,128)}), f32[256,16,256]{2,0,1:T(8,128)}, u32[]{:S(2)}, u32[]{:S(2)}) async-start(f32[256,16,256]{2,0,1:T(8,128)} %fusion.46), calls=%async_computation.5 | async-start | bytes 8388608 | tf_op jit(solution)/shard_map/all_to_all | solution.py:249
  188.2 2.8 %fusion.22 = f32[2,16,2,32,128]{4,3,2,1,0:T(8,128)} fusion(f32[2,16,2,64,32]{3,4,2,1,0:T(8,128)} %bitcast.164, bf16[1,128,2,2,64]{1,4,3,2,0:T(8,128)(2,1)S(1)} %bitcast.185), kind=kOutput, calls=%fused_computation.50 | convolution fusion | flops 201326592 | bytes 1605632 | tf_op jit(solution)/shard_map/tgn,gkhnc->tgkhc/dot_general | solution.py:140
  191.0 48.6 %all-to-all-done.4 = f32[256,16,256]{2,0,1:T(8,128)} async-done(((f32[256,16,256]{2,0,1:T(8,128)}), f32[256,16,256]{2,0,1:T(8,128)}, u32[]{:S(2)}, u32[]{:S(2)}) %all-to-all-start.4) | async-done | bytes 4194336 | tf_op jit(solution)/shard_map/all_to_all | solution.py:249
  242.9 9.7 %all-to-all-start.5 = ((f32[256,8,32]{0,2,1:T(8,128)}), f32[256,8,32]{0,2,1:T(8,128)S(1)}, u32[]{:S(2)}, u32[]{:S(2)}) async-start(f32[256,8,32]{0,2,1:T(8,128)} %bitcast.187), calls=%async_computation.6 | async-start | bytes 524288 | tf_op jit(solution)/shard_map/all_to_all | solution.py:252
  258.2 4.9 %all-to-all-done.5 = f32[256,8,32]{0,2,1:T(8,128)S(1)} async-done(((f32[256,8,32]{0,2,1:T(8,128)}), f32[256,8,32]{0,2,1:T(8,128)S(1)}, u32[]{:S(2)}, u32[]{:S(2)}) %all-to-all-start.5) | async-done | bytes 262176 | tf_op jit(solution)/shard_map/all_to_all | solution.py:252
  (76 shorter events, 43.1 us)
Async XLA Ops:
  26.9 7.3 %copy-start.10 = (f32[1,32,128]{2,1,0:T(8,128)S(1)}, f32[1,32,128]{2,1,0:T(8,128)}, u32[]{:S(2)}) copy-start(f32[1,32,128]{2,1,0:T(8,128)} %param.11) | copy-start | bytes 49156
  26.9 7.7 %copy-start.8 = (bf16[1,128,2048]{2,1,0:T(8,128)(2,1)S(1)}, bf16[1,128,2048]{2,1,0:T(8,128)(2,1)}, u32[]{:S(2)}) copy-start(bf16[1,128,2048]{2,1,0:T(8,128)(2,1)} %param.9) | copy-start | bytes 1572868
  26.9 8.7 %copy-start.9 = (bf16[1,128,2048]{2,1,0:T(8,128)(2,1)S(1)}, bf16[1,128,2048]{2,1,0:T(8,128)(2,1)}, u32[]{:S(2)}) copy-start(bf16[1,128,2048]{2,1,0:T(8,128)(2,1)} %param.13) | copy-start | bytes 1572868
  26.9 33.5 %all-to-all-start.1 = ((bf16[16,8,32,256]{3,2,1,0:T(8,128)(2,1)}), bf16[16,8,32,256]{3,2,1,0:T(8,128)(2,1)S(1)}, u32[]{:S(2)}, u32[]{:S(2)}) async-start(bf16[16,8,32,256]{3,2,1,0:T(8,128)(2,1)} %broadcast_in_dim.91), calls=%async_computation.1 | async-start | bytes 4194304 | tf_op jit(solution)/shard_map/all_to_all | solution.py:186
  124.6 34.2 %all-to-all-start.3 = ((f32[64,1,4096]{2,1,0:T(1,128)}), f32[64,1,4096]{2,1,0:T(1,128)}, u32[]{:S(2)}, u32[]{:S(2)}) async-start(f32[64,1,4096]{2,1,0:T(1,128)} %copy.71), calls=%async_computation.3 | async-start | bytes 2097152 | tf_op jit(solution)/shard_map/all_to_all | solution.py:38
  132.5 1.6 copy-start.3
  134.1 2.4 copy-start.11
  172.1 3.6 %copy-start.1 = (f32[64,64,32]{1,2,0:T(8,128)S(1)}, f32[64,64,32]{1,2,0:T(8,128)}, u32[]{:S(2)}) copy-start(f32[64,64,32]{1,2,0:T(8,128)} %copy.73) | copy-start | bytes 1572868
  172.1 3.6 %copy-start.4 = (bf16[1,128,2048]{1,2,0:T(8,128)(2,1)S(1)}, bf16[1,128,2048]{1,2,0:T(8,128)(2,1)}, u32[]{:S(2)}) copy-start(bf16[1,128,2048]{1,2,0:T(8,128)(2,1)} %copy.64) | copy-start | bytes 1572868
  172.1 5.5 %copy-start.7 = (bf16[4096,128]{1,0:T(8,128)(2,1)S(1)}, bf16[4096,128]{1,0:T(8,128)(2,1)}, u32[]{:S(2)}) copy-start(bf16[4096,128]{1,0:T(8,128)(2,1)} %copy.87) | copy-start | bytes 3145732
  180.3 59.3 %all-to-all-start.4 = ((f32[256,16,256]{2,0,1:T(8,128)}), f32[256,16,256]{2,0,1:T(8,128)}, u32[]{:S(2)}, u32[]{:S(2)}) async-start(f32[256,16,256]{2,0,1:T(8,128)} %fusion.46), calls=%async_computation.5 | async-start | bytes 8388608 | tf_op jit(solution)/shard_map/all_to_all | solution.py:249
  186.3 77.5 %reduce-scatter.2.cloned.1.call-start = ((), (), s32[]{:S(2)}) async-start(), calls=%async_computation.7 | async-start | bytes 1572864 | tf_op jit(solution)/shard_map/reduce_scatter | solution.py:244
  191.0 61.6 %copy-start.2 = (f32[64,64,32]{1,2,0:T(8,128)S(1)}, f32[64,64,32]{1,2,0:T(8,128)}, u32[]{:S(2)}) copy-start(f32[64,64,32]{1,2,0:T(8,128)} %copy.73) | copy-start | bytes 1572868
  242.1 11.2 %copy-start = (f32[1,128,2048]{1,2,0:T(8,128)S(1)}, f32[1,128,2048]{1,2,0:T(8,128)}, u32[]{:S(2)}) copy-start(f32[1,128,2048]{1,2,0:T(8,128)} %convert_element_type.118) | copy-start | bytes 3145732
  242.9 20.2 %all-to-all-start.5 = ((f32[256,8,32]{0,2,1:T(8,128)}), f32[256,8,32]{0,2,1:T(8,128)S(1)}, u32[]{:S(2)}, u32[]{:S(2)}) async-start(f32[256,8,32]{0,2,1:T(8,128)} %bitcast.187), calls=%async_computation.6 | async-start | bytes 524288 | tf_op jit(solution)/shard_map/all_to_all | solution.py:252
  252.6 1.2 copy-start.5
  252.6 1.5 copy-start.6
Sparse Core Ops, SparseCore 0:
  190.1 11.2 reduce-scatter.1

commit v14 on v13

--- a/solution.py
+++ b/solution.py
@@ -245,14 +245,18 @@
         input_terms.astype(jnp.bfloat16), "head", scatter_dimension=1, tiled=True
     )[None]
     scale = 1.0 / (lax.axis_size(ROWS) * tok_rows)
-    proj_terms = jnp.einsum("tc,td->cd", grad_flat, tokens, preferred_element_type=jnp.float32)
+    tokens_z = (
+        tokens.reshape(tok_rows, outer_count, inner_count, -1)
+        .transpose(0, 2, 1, 3)
+        .reshape(tok_rows, -1)
+    )
+    proj_terms = jnp.einsum("tc,td->cd", grad_flat, tokens_z, preferred_element_type=jnp.float32)
     proj_parts = lax.all_to_all(
-        proj_terms.reshape(col_count, outer_count, -1), OUTER, 1, 1, tiled=True
+        proj_terms.reshape(col_count, inner_count, -1), INNER, 1, 1, tiled=True
     ).sum(axis=1)
     proj_parts = lax.all_to_all(
-        proj_parts.reshape(col_count, inner_count, -1), INNER, 1, 1, tiled=True
-    )
-    proj_parts = proj_parts.sum(axis=1).T[None]
+        proj_parts.T.reshape(outer_count, -1, col_count), OUTER, 0, 0, tiled=True
+    )
     grad_proj = proj_parts.sum(axis=0) * scale
     grad_proj = grad_proj.reshape(-1, 2, col_count // 2)
     return (grad_input, grad_values, grad_gate, grad_proj)

time: 272 us -> 311 us (1.14)
  waiting for transfers between devices: 88.2 us -> 126 us
  starting transfers between devices: 28.6 us -> 23.5 us
  local copies, waits for them, and re-layouts: 46.2 us -> 50 us
    all_to_all x2, waiting for transfers between devices: 53.5 us -> 92.7 us  [the longest x1 88.6 us: body(): lax.all_to_all(proj_terms.reshape(col_count, inner_count, -1), INNER, 1,...]
    all_to_all x2, starting transfers between devices: 15.7 us -> 10.6 us  [the longest x1 6.02 us: body(): lax.all_to_all(proj_parts.T.reshape(outer_count, -1, col_count), OUTER, 0...]
    transpose x0 -> x2, local copies, waits for them, and re-layouts: none -> 4.6 us  [the longest x1 2.43 us: body(): tokens_z = tokens.reshape(tok_rows, outer_count, inner_count, -1).transpo...]
    unnamed x31 -> x34, local copies, waits for them, and re-layouts: 7.79 us -> 10.1 us
where the time goes in v14:
time: 311 us; the launch traced here: 308 us
  waiting for transfers between devices  126 us (41%)
  blocking collectives  53.5 us (17%)
  local copies, waits for them, and re-layouts  50 us (16%)
  matrix products  26.6 us (9%)
  starting transfers between devices  23.5 us (8%)
  between operations  14.3 us (5%)
  other arithmetic  14 us (5%)
    all_to_all x1, waiting for transfers between devices, body(): lax.all_to_all(proj_terms.reshape(col_count, inner_count, -1), INNER, 1,...  88.6 us
    all_to_all x1, blocking collectives, carried_both(): got = lax.all_to_all(packed[:, None], axis, 0, 0, tiled=True)[:, 0]  36.2 us
    all_to_all x1, waiting for transfers between devices, carried_both(): lax.all_to_all(jnp.concatenate([fwd, bwd], 1)[:, None], axis, 0, 0, tiled...  18 us
    all_to_all x1, blocking collectives, body(): lax.all_to_all(jnp.broadcast_to(weight_local[None], (inner_count,) + weig...  17.4 us
    all_to_all x1, waiting for transfers between devices, body(): lax.all_to_all(jnp.broadcast_to(weight_inner[None], (outer_count,) + weig...  15.4 us
    unnamed x34, local copies, waits for them, and re-layouts  10.1 us
    all_to_all x1, starting transfers between devices, body(): lax.all_to_all(jnp.broadcast_to(weight_inner[None], (outer_count,) + weig...  7.3 us
    optimization_barrier x2, local copies, waits for them, and re-layouts, span_full(): lax.optimization_barrier(((y_local, vals_local, c_local, b_local), state_...  6.35 us
  transfers between devices with their start and end apart: 5, of which 4 were waited for; matrix products, arithmetic and copies ran while one was open for 12% of the time, Pallas kernels for 0%

profile of v14, /device:TPU:24, one launch (start us, length us, event | category | flops | bytes accessed | tf_op | source)
XLA Modules:
  0.0 308.1 jit_solution(14553573138288677125)
XLA Ops:
  7.9 17.4 %all_to_all.30 = bf16[8,32,256]{2,1,0:T(8,128)(2,1)S(1)} all-to-all(bf16[8,32,256]{2,1,0:T(8,128)(2,1)S(1)} %broadcast_in_dim.89), channel_id=1, replica_groups=mesh['dp'=2,'ylo'=2,'x'=4,'z'=8,'head'=2] {'z'}, dimensions={0} | all-to-all | bytes 262144 | tf_op jit(solution)/shard_map/all_to_all | solution.py:179
  26.9 7.3 %all-to-all-start.1 = ((bf16[16,8,32,256]{3,2,1,0:T(8,128)(2,1)}), bf16[16,8,32,256]{3,2,1,0:T(8,128)(2,1)S(1)}, u32[]{:S(2)}, u32[]{:S(2)}) async-start(bf16[16,8,32,256]{3,2,1,0:T(8,128)(2,1)} %broadcast_in_dim.90), calls=%async_computation.1 | async-start | bytes 4194304 | tf_op jit(solution)/shard_map/all_to_all | solution.py:186
  44.9 15.4 %all-to-all-done.1 = bf16[16,8,32,256]{3,2,1,0:T(8,128)(2,1)S(1)} async-done(((bf16[16,8,32,256]{3,2,1,0:T(8,128)(2,1)}), bf16[16,8,32,256]{3,2,1,0:T(8,128)(2,1)S(1)}, u32[]{:S(2)}, u32[]{:S(2)}) %all-to-all-start.1) | async-done | bytes 2097184 | tf_op jit(solution)/shard_map/all_to_all | solution.py:186
  62.1 2.7 convolution_bitcast_fusion.1
  64.8 3.2 %copy.69 = f32[2,16,2,64,32]{4,3,2,1,0:T(8,128)} copy(f32[2,16,2,64,32]{3,4,2,1,0:T(8,128)} %convolution_bitcast_fusion.1) | data formatting | bytes 1048576 | tf_op jit(solution)/shard_map/qgn,qgkhc->gkhnc/transpose | solution.py:56
  68.0 3.1 %reshape.137 = f32[64,2048]{1,0:T(8,128)} reshape(f32[2,16,2,64,32]{4,3,2,1,0:T(8,128)} %copy.69) | data formatting | bytes 1048576 | tf_op jit(solution)/shard_map/reshape | solution.py:62
  71.1 2.8 convolution_bitcast_fusion
  73.9 3.2 %copy.70 = f32[2,16,2,64,32]{4,3,2,1,0:T(8,128)} copy(f32[2,16,2,64,32]{3,4,2,1,0:T(8,128)} %convolution_bitcast_fusion) | data formatting | bytes 1048576 | tf_op jit(solution)/shard_map/qgn,qgkhc->gkhnc/transpose | solution.py:59
  77.1 3.1 %reshape.138 = f32[64,2048]{1,0:T(8,128)} reshape(f32[2,16,2,64,32]{4,3,2,1,0:T(8,128)} %copy.70) | data formatting | bytes 1048576 | tf_op jit(solution)/shard_map/reshape | solution.py:62
  84.7 36.2 %all_to_all.31 = f32[64,1,4160]{2,1,0:T(1,128)S(1)} all-to-all(f32[64,1,4160]{2,1,0:T(1,128)S(1)} %copy.71), channel_id=1, replica_groups=mesh['dp'=2,'ylo'=2,'x'=4,'z'=8,'head'=2] {'ylo','x','z'}, dimensions={0} | all-to-all | bytes 2129920 | tf_op jit(solution)/shard_map/all_to_all | solution.py:25
  124.6 5.6 %all-to-all-start.3 = ((f32[64,1,4096]{2,1,0:T(1,128)}), f32[64,1,4096]{2,1,0:T(1,128)}, u32[]{:S(2)}, u32[]{:S(2)}) async-start(f32[64,1,4096]{2,1,0:T(1,128)} %copy.72), calls=%async_computation.3 | async-start | bytes 2097152 | tf_op jit(solution)/shard_map/all_to_all | solution.py:38
  140.8 18.0 %all-to-all-done.3 = f32[64,1,4096]{2,1,0:T(1,128)} async-done(((f32[64,1,4096]{2,1,0:T(1,128)}), f32[64,1,4096]{2,1,0:T(1,128)}, u32[]{:S(2)}, u32[]{:S(2)}) %all-to-all-start.3) | async-done | bytes 1048608 | tf_op jit(solution)/shard_map/all_to_all | solution.py:38
  158.8 3.9 %copy.73 = f32[64,1,4096]{0,2,1:T(8,128)} copy(f32[64,1,4096]{2,1,0:T(1,128)} %all-to-all-done.3) | data formatting | bytes 2097152 | tf_op jit(solution)/shard_map/all_to_all | solution.py:38
  162.7 3.1 %slice_bitcast_fusion = (f32[64,64,32]{0,2,1:T(8,128)}, f32[64,64,32]{0,2,1:T(8,128)}) fusion(f32[64,2,64,32]{0,3,2,1:T(8,128)} %bitcast.173), kind=kLoop, calls=%fused_computation.27 | loop fusion | bytes 2097152 | tf_op jit(solution)/shard_map/squeeze | solution.py:40
  165.8 3.1 %copy.77 = f32[64,64,32]{1,2,0:T(8,128)} copy(f32[64,64,32]{0,2,1:T(8,128)} %get-tuple-element.13) | data formatting | bytes 1048576 | tf_op jit(solution)/shard_map/optimization_barrier | solution.py:134
  169.0 3.2 %copy.74 = f32[64,64,32]{1,2,0:T(8,128)} copy(f32[64,64,32]{0,2,1:T(8,128)} %get-tuple-element.11) | data formatting | bytes 1048576 | tf_op jit(solution)/shard_map/optimization_barrier | solution.py:134
  172.2 3.5 %fusion.11 = bf16[128,1,2,64]{0,3,2,1:T(8,128)(2,1)S(1)} fusion(f32[128,2,64]{0,2,1:T(8,128)S(1)} %convolution_bitcast_fusion.7, f32[128,2,16,2,32]{0,4,3,2,1:T(8,128)} %convert_multiply_fusion.1, f32[2,16,2,64,32]{3,4,2,1,0:T(8,128)} %bitcast.167), kind=kOutput, calls=%fused_computation.25 | convolution fusion | flops 201359360 | bytes 1671168 | tf_op jit(solution)/shard_map/tgkhc,gkhnc->tgn/dot_general | solution.py:159
  177.7 2.7 fusion.46
  180.3 4.5 %all-to-all-start.4 = ((f32[256,8,512]{2,0,1:T(8,128)}), f32[256,8,512]{2,0,1:T(8,128)}, u32[]{:S(2)}, u32[]{:S(2)}) async-start(f32[256,8,512]{2,0,1:T(8,128)} %fusion.46), calls=%async_computation.5 | async-start | bytes 8388608 | tf_op jit(solution)/shard_map/all_to_all | solution.py:254
  186.8 2.8 fusion.22
  189.6 88.6 %all-to-all-done.4 = f32[256,8,512]{2,0,1:T(8,128)} async-done(((f32[256,8,512]{2,0,1:T(8,128)}), f32[256,8,512]{2,0,1:T(8,128)}, u32[]{:S(2)}, u32[]{:S(2)}) %all-to-all-start.4) | async-done | bytes 4194336 | tf_op jit(solution)/shard_map/all_to_all | solution.py:254
  278.3 3.5 %reduce_sum.32 = f32[256,512]{1,0:T(8,128)} reduce(f32[256,8,512]{2,0,1:T(8,128)} %all-to-all-done.4, f32[]{:T(128)} %constant.8.clone.1), dimensions={1}, to_apply=%region_4.5 | reduce | flops 917504 | bytes 4718596 | tf_op jit(solution)/shard_map/reduce_sum | solution.py:256
  283.9 6.0 %all-to-all-start.5 = ((f32[16,32,256]{2,1,0:T(8,128)}), f32[16,32,256]{2,1,0:T(8,128)}, u32[]{:S(2)}, u32[]{:S(2)}) async-start(f32[16,32,256]{2,1,0:T(8,128)} %bitcast.185), calls=%async_computation.6 | async-start | bytes 1048576 | tf_op jit(solution)/shard_map/all_to_all | solution.py:257
  295.5 4.0 %all-to-all-done.5 = f32[16,32,256]{2,1,0:T(8,128)} async-done(((f32[16,32,256]{2,1,0:T(8,128)}), f32[16,32,256]{2,1,0:T(8,128)}, u32[]{:S(2)}, u32[]{:S(2)}) %all-to-all-start.5) | async-done | bytes 524320 | tf_op jit(solution)/shard_map/all_to_all | solution.py:257
  (79 shorter events, 46.7 us)
Async XLA Ops:
  26.9 7.3 %copy-start.11 = (f32[1,32,128]{2,1,0:T(8,128)S(1)}, f32[1,32,128]{2,1,0:T(8,128)}, u32[]{:S(2)}) copy-start(f32[1,32,128]{2,1,0:T(8,128)} %param.11) | copy-start | bytes 49156
  26.9 7.7 %copy-start.9 = (bf16[1,128,2048]{2,1,0:T(8,128)(2,1)S(1)}, bf16[1,128,2048]{2,1,0:T(8,128)(2,1)}, u32[]{:S(2)}) copy-start(bf16[1,128,2048]{2,1,0:T(8,128)(2,1)} %param.9) | copy-start | bytes 1572868
  26.9 8.7 %copy-start.10 = (bf16[1,128,2048]{2,1,0:T(8,128)(2,1)S(1)}, bf16[1,128,2048]{2,1,0:T(8,128)(2,1)}, u32[]{:S(2)}) copy-start(bf16[1,128,2048]{2,1,0:T(8,128)(2,1)} %param.13) | copy-start | bytes 1572868
  26.9 33.5 %all-to-all-start.1 = ((bf16[16,8,32,256]{3,2,1,0:T(8,128)(2,1)}), bf16[16,8,32,256]{3,2,1,0:T(8,128)(2,1)S(1)}, u32[]{:S(2)}, u32[]{:S(2)}) async-start(bf16[16,8,32,256]{3,2,1,0:T(8,128)(2,1)} %broadcast_in_dim.90), calls=%async_computation.1 | async-start | bytes 4194304 | tf_op jit(solution)/shard_map/all_to_all | solution.py:186
  124.6 34.2 %all-to-all-start.3 = ((f32[64,1,4096]{2,1,0:T(1,128)}), f32[64,1,4096]{2,1,0:T(1,128)}, u32[]{:S(2)}, u32[]{:S(2)}) async-start(f32[64,1,4096]{2,1,0:T(1,128)} %copy.72), calls=%async_computation.3 | async-start | bytes 2097152 | tf_op jit(solution)/shard_map/all_to_all | solution.py:38
  132.5 2.5 copy-start
  132.5 2.8 copy-start.4
  135.2 2.4 copy-start.12
  172.2 3.6 %copy-start.2 = (f32[64,64,32]{1,2,0:T(8,128)S(1)}, f32[64,64,32]{1,2,0:T(8,128)}, u32[]{:S(2)}) copy-start(f32[64,64,32]{1,2,0:T(8,128)} %copy.74) | copy-start | bytes 1572868
  172.2 3.6 %copy-start.5 = (bf16[1,128,2048]{1,2,0:T(8,128)(2,1)S(1)}, bf16[1,128,2048]{1,2,0:T(8,128)(2,1)}, u32[]{:S(2)}) copy-start(bf16[1,128,2048]{1,2,0:T(8,128)(2,1)} %copy.65) | copy-start | bytes 1572868
  172.2 5.5 %copy-start.8 = (bf16[128,8,16,32]{0,3,2,1:T(8,128)(2,1)S(1)}, bf16[128,8,16,32]{0,3,2,1:T(8,128)(2,1)}, u32[]{:S(2)}) copy-start(bf16[128,8,16,32]{0,3,2,1:T(8,128)(2,1)} %copy.81) | copy-start | bytes 3145732
  180.3 97.9 %all-to-all-start.4 = ((f32[256,8,512]{2,0,1:T(8,128)}), f32[256,8,512]{2,0,1:T(8,128)}, u32[]{:S(2)}, u32[]{:S(2)}) async-start(f32[256,8,512]{2,0,1:T(8,128)} %fusion.46), calls=%async_computation.5 | async-start | bytes 8388608 | tf_op jit(solution)/shard_map/all_to_all | solution.py:254
  184.9 116.4 %reduce-scatter.2.cloned.1.call-start = ((), (), s32[]{:S(2)}) async-start(), calls=%async_computation.7 | async-start | bytes 1572864 | tf_op jit(solution)/shard_map/reduce_scatter | solution.py:244
  281.7 8.2 %copy-start.3 = (f32[64,64,32]{1,2,0:T(8,128)S(1)}, f32[64,64,32]{1,2,0:T(8,128)}, u32[]{:S(2)}) copy-start(f32[64,64,32]{1,2,0:T(8,128)} %copy.74) | copy-start | bytes 1572868
  281.7 8.8 %copy-start.1 = (f32[1,128,2048]{1,2,0:T(8,128)S(1)}, f32[1,128,2048]{1,2,0:T(8,128)}, u32[]{:S(2)}) copy-start(f32[1,128,2048]{1,2,0:T(8,128)} %convert_element_type.118) | copy-start | bytes 3145732
  283.9 15.6 %all-to-all-start.5 = ((f32[16,32,256]{2,1,0:T(8,128)}), f32[16,32,256]{2,1,0:T(8,128)}, u32[]{:S(2)}, u32[]{:S(2)}) async-start(f32[16,32,256]{2,1,0:T(8,128)} %bitcast.185), calls=%async_computation.6 | async-start | bytes 1048576 | tf_op jit(solution)/shard_map/all_to_all | solution.py:257
  289.9 1.2 copy-start.6
  289.9 1.5 copy-start.7
Sparse Core Ops, SparseCore 0:
  188.8 13.8 reduce-scatter.1

commit v15 on v13

--- a/solution.py
+++ b/solution.py
@@ -176,13 +176,7 @@
     col_count = weight_local.shape[1]
     inner_count = lax.axis_size(INNER)
     outer_count = lax.axis_size(OUTER)
-    weight_inner = lax.all_to_all(
-        jnp.broadcast_to(weight_local[None], (inner_count,) + weight_local.shape),
-        INNER,
-        0,
-        0,
-        tiled=True,
-    )
+    weight_inner = lax.all_gather(weight_local, INNER, axis=0)
     weight_full = lax.all_to_all(
         jnp.broadcast_to(weight_inner[None], (outer_count,) + weight_inner.shape),
         OUTER,

time: 272 us -> 256 us (0.941)
  waiting for transfers between devices: 88.2 us -> 72.3 us
  starting transfers between devices: 28.6 us -> 22.3 us
  blocking collectives: 53.5 us -> 59.6 us
    all_gather x0 -> x1, blocking collectives: none -> 28.3 us  [body(): weight_inner = lax.all_gather(weight_local, INNER, axis=0)]
    all_to_all x1 -> x0, blocking collectives: 17.4 us -> none  [body(): lax.all_to_all(jnp.broadcast_to(weight_local[None], (inner_count,) + weig...]
    all_to_all x1, waiting for transfers between devices: 48.6 us -> 41.5 us  [body(): lax.all_to_all(proj_terms.reshape(col_count, outer_count, -1), OUTER, 1,...]
    all_to_all x1, starting transfers between devices: 9.69 us -> 3.41 us  [body(): lax.all_to_all(proj_parts.reshape(col_count, inner_count, -1), INNER, 1,...]
    all_to_all x1, waiting for transfers between devices: 19.2 us -> 13.5 us  [carried_both(): lax.all_to_all(jnp.concatenate([fwd, bwd], 1)[:, None], axis, 0, 0, tiled...]
    all_to_all x1, blocking collectives: 36.2 us -> 31.3 us  [carried_both(): got = lax.all_to_all(packed[:, None], axis, 0, 0, tiled=True)[:, 0]]
    all_to_all x1, waiting for transfers between devices: 15.4 us -> 12.5 us  [body(): lax.all_to_all(jnp.broadcast_to(weight_inner[None], (outer_count,) + weig...]
    unnamed x31 -> x30, local copies, waits for them, and re-layouts: 7.79 us -> 7.06 us
  transfers between devices with their start and end apart: 5 -> 5, of which waited for: 4 -> 4; matrix products, arithmetic and copies ran while one was open for 12% -> 13% of each run, Pallas kernels for 0% -> 0%
where the time goes in v15:
time: 256 us; the launch traced here: 255 us
  waiting for transfers between devices  72.3 us (28%)
  blocking collectives  59.6 us (23%)
  local copies, waits for them, and re-layouts  46.2 us (18%)
  matrix products  26.7 us (10%)
  starting transfers between devices  22.3 us (9%)
  between operations  14.3 us (6%)
  other arithmetic  13.2 us (5%)
    all_to_all x1, waiting for transfers between devices, body(): lax.all_to_all(proj_terms.reshape(col_count, outer_count, -1), OUTER, 1,...  41.5 us
    all_to_all x1, blocking collectives, carried_both(): got = lax.all_to_all(packed[:, None], axis, 0, 0, tiled=True)[:, 0]  31.3 us
    all_gather x1, blocking collectives, body(): weight_inner = lax.all_gather(weight_local, INNER, axis=0)  28.3 us
    all_to_all x1, waiting for transfers between devices, carried_both(): lax.all_to_all(jnp.concatenate([fwd, bwd], 1)[:, None], axis, 0, 0, tiled...  13.5 us
    all_to_all x1, waiting for transfers between devices, body(): lax.all_to_all(jnp.broadcast_to(weight_inner[None], (outer_count,) + weig...  12.5 us
    all_to_all x1, starting transfers between devices, body(): lax.all_to_all(jnp.broadcast_to(weight_inner[None], (outer_count,) + weig...  7.3 us
    unnamed x30, local copies, waits for them, and re-layouts  7.06 us
    optimization_barrier x2, local copies, waits for them, and re-layouts, span_full(): lax.optimization_barrier(((y_local, vals_local, c_local, b_local), state_...  6.28 us
  transfers between devices with their start and end apart: 5, of which 4 were waited for; matrix products, arithmetic and copies ran while one was open for 13% of the time, Pallas kernels for 0%

profile of v15, /device:TPU:24, one launch (start us, length us, event | category | flops | bytes accessed | tf_op | source)
XLA Modules:
  0.0 254.6 jit_solution(11899957417151915511)
XLA Ops:
  7.9 28.3 %all_gather.3 = bf16[8,32,256]{2,1,0:T(8,128)(2,1)S(1)} all-gather(bf16[1,32,256]{2,1,0:T(8,128)(2,1)S(1)} %all_gather_reshape.3), channel_id=1, replica_groups=mesh['dp'=2,'ylo'=2,'x'=4,'z'=8,'head'=2] {'z'}, dimensions={0}, use_global_device_ids=true | all-gather | bytes 147456 | tf_op jit(solution)/shard_map/all_gather | solution.py:179
  37.8 7.3 %all-to-all-start = ((bf16[16,8,32,256]{3,2,1,0:T(8,128)(2,1)}), bf16[16,8,32,256]{3,2,1,0:T(8,128)(2,1)S(1)}, u32[]{:S(2)}, u32[]{:S(2)}) async-start(bf16[16,8,32,256]{3,2,1,0:T(8,128)(2,1)} %broadcast_in_dim.82), calls=%async_computation | async-start | bytes 4194304 | tf_op jit(solution)/shard_map/all_to_all | solution.py:180
  53.3 2.5 %convert_multiply_fusion.1 = f32[128,2,16,2,32]{0,4,3,2,1:T(8,128)} fusion(f32[128,2,16]{0,2,1:T(8,128)S(1)} %bitcast.189, f32[128,2,16,2,32]{0,4,3,2,1:T(8,128)S(1)} %bitcast.151, f32[128,2,16,2,32]{0,4,3,2,1:T(8,128)} %bitcast.154), kind=kLoop, calls=%fused_computation.38 | loop fusion | flops 2097152 | bytes 3162112 | tf_op jit(solution)/shard_map/mul | solution.py:55
  55.8 12.5 %all-to-all-done = bf16[16,8,32,256]{3,2,1,0:T(8,128)(2,1)S(1)} async-done(((bf16[16,8,32,256]{3,2,1,0:T(8,128)(2,1)}), bf16[16,8,32,256]{3,2,1,0:T(8,128)(2,1)S(1)}, u32[]{:S(2)}, u32[]{:S(2)}) %all-to-all-start) | async-done | bytes 2097184 | tf_op jit(solution)/shard_map/all_to_all | solution.py:180
  70.1 2.7 %convolution_bitcast_fusion.1 = f32[2,16,2,64,32]{3,4,2,1,0:T(8,128)} fusion(bf16[128,2,16,2,32]{0,4,3,2,1:T(8,128)(2,1)} %bitcast.161, f32[128,2,16]{0,2,1:T(8,128)S(1)} %bitcast.186, bf16[1,128,2,2,64]{1,4,3,2,0:T(8,128)(2,1)S(1)} %bitcast.176), kind=kOutput, calls=%fused_computation.7 | convolution fusion | flops 201850880 | bytes 1097728 | tf_op jit(solution)/shard_map/qgn,qgkhc->gkhnc/dot_general | solution.py:56
  72.8 3.2 %copy.68 = f32[2,16,2,64,32]{4,3,2,1,0:T(8,128)} copy(f32[2,16,2,64,32]{3,4,2,1,0:T(8,128)} %convolution_bitcast_fusion.1) | data formatting | bytes 1048576 | tf_op jit(solution)/shard_map/qgn,qgkhc->gkhnc/transpose | solution.py:56
  76.0 3.1 %reshape.135 = f32[64,2048]{1,0:T(8,128)} reshape(f32[2,16,2,64,32]{4,3,2,1,0:T(8,128)} %copy.68) | data formatting | bytes 1048576 | tf_op jit(solution)/shard_map/reshape | solution.py:62
  79.1 2.8 %convolution_bitcast_fusion = f32[2,16,2,64,32]{3,4,2,1,0:T(8,128)} fusion(f32[128,2,16,2,32]{0,4,3,2,1:T(8,128)} %convert_multiply_fusion.1, bf16[1,128,2,2,64]{1,4,3,2,0:T(8,128)(2,1)S(1)} %bitcast.177), kind=kOutput, calls=%fused_computation.6 | convolution fusion | flops 201326592 | bytes 1605632 | tf_op jit(solution)/shard_map/qgn,qgkhc->gkhnc/dot_general | solution.py:59
  81.9 3.2 %copy.69 = f32[2,16,2,64,32]{4,3,2,1,0:T(8,128)} copy(f32[2,16,2,64,32]{3,4,2,1,0:T(8,128)} %convolution_bitcast_fusion) | data formatting | bytes 1048576 | tf_op jit(solution)/shard_map/qgn,qgkhc->gkhnc/transpose | solution.py:59
  85.1 3.1 %reshape.136 = f32[64,2048]{1,0:T(8,128)} reshape(f32[2,16,2,64,32]{4,3,2,1,0:T(8,128)} %copy.69) | data formatting | bytes 1048576 | tf_op jit(solution)/shard_map/reshape | solution.py:62
  92.7 31.3 %all_to_all.25 = f32[64,1,4160]{2,1,0:T(1,128)S(1)} all-to-all(f32[64,1,4160]{2,1,0:T(1,128)S(1)} %copy.70), channel_id=1, replica_groups=mesh['dp'=2,'ylo'=2,'x'=4,'z'=8,'head'=2] {'ylo','x','z'}, dimensions={0} | all-to-all | bytes 2129920 | tf_op jit(solution)/shard_map/all_to_all | solution.py:25
  127.7 5.6 %all-to-all-start.2 = ((f32[64,1,4096]{2,1,0:T(1,128)}), f32[64,1,4096]{2,1,0:T(1,128)}, u32[]{:S(2)}, u32[]{:S(2)}) async-start(f32[64,1,4096]{2,1,0:T(1,128)} %copy.71), calls=%async_computation.2 | async-start | bytes 2097152 | tf_op jit(solution)/shard_map/all_to_all | solution.py:38
  142.7 13.5 %all-to-all-done.2 = f32[64,1,4096]{2,1,0:T(1,128)} async-done(((f32[64,1,4096]{2,1,0:T(1,128)}), f32[64,1,4096]{2,1,0:T(1,128)}, u32[]{:S(2)}, u32[]{:S(2)}) %all-to-all-start.2) | async-done | bytes 1048608 | tf_op jit(solution)/shard_map/all_to_all | solution.py:38
  156.2 3.9 %copy.72 = f32[64,1,4096]{0,2,1:T(8,128)} copy(f32[64,1,4096]{2,1,0:T(1,128)} %all-to-all-done.2) | data formatting | bytes 2097152 | tf_op jit(solution)/shard_map/all_to_all | solution.py:38
  160.1 3.1 %slice_bitcast_fusion = (f32[64,64,32]{0,2,1:T(8,128)}, f32[64,64,32]{0,2,1:T(8,128)}) fusion(f32[64,2,64,32]{0,3,2,1:T(8,128)} %bitcast.165), kind=kLoop, calls=%fused_computation.27 | loop fusion | bytes 2097152 | tf_op jit(solution)/shard_map/squeeze | solution.py:40
  163.2 3.1 %copy.76 = f32[64,64,32]{1,2,0:T(8,128)} copy(f32[64,64,32]{0,2,1:T(8,128)} %get-tuple-element.13) | data formatting | bytes 1048576 | tf_op jit(solution)/shard_map/optimization_barrier | solution.py:134
  166.4 3.1 %copy.73 = f32[64,64,32]{1,2,0:T(8,128)} copy(f32[64,64,32]{0,2,1:T(8,128)} %get-tuple-element.11) | data formatting | bytes 1048576 | tf_op jit(solution)/shard_map/optimization_barrier | solution.py:134
  169.5 3.5 %fusion.11 = bf16[128,1,2,64]{0,3,2,1:T(8,128)(2,1)S(1)} fusion(f32[128,2,64]{0,2,1:T(8,128)S(1)} %convolution_bitcast_fusion.7, f32[128,2,16,2,32]{0,4,3,2,1:T(8,128)} %convert_multiply_fusion.1, f32[2,16,2,64,32]{3,4,2,1,0:T(8,128)} %bitcast.159), kind=kOutput, calls=%fused_computation.25 | convolution fusion | flops 201359360 | bytes 1671168 | tf_op jit(solution)/shard_map/tgkhc,gkhnc->tgn/dot_general | solution.py:159
  175.0 2.7 %fusion.46 = f32[256,16,256]{2,0,1:T(8,128)} fusion(bf16[128,256,1]{0,1,2:T(8,128)(2,1)S(1)} %bitcast.184, bf16[16,256,128]{2,1,0:T(8,128)(2,1)S(1)} %bitcast.173), kind=kOutput, calls=%fused_computation.79 | convolution fusion | flops 268435456 | bytes 5308416 | tf_op jit(solution)/shard_map/tc,td->cd/dot_general | solution.py:242
  177.7 6.0 %all-to-all-start.3 = ((f32[256,16,256]{2,0,1:T(8,128)}), f32[256,16,256]{2,0,1:T(8,128)}, u32[]{:S(2)}, u32[]{:S(2)}) async-start(f32[256,16,256]{2,0,1:T(8,128)} %fusion.46), calls=%async_computation.4 | async-start | bytes 8388608 | tf_op jit(solution)/shard_map/all_to_all | solution.py:243
  185.6 2.8 %fusion.22 = f32[2,16,2,32,128]{4,3,2,1,0:T(8,128)} fusion(f32[2,16,2,64,32]{3,4,2,1,0:T(8,128)} %bitcast.160, bf16[1,128,2,2,64]{1,4,3,2,0:T(8,128)(2,1)S(1)} %bitcast.181), kind=kOutput, calls=%fused_computation.50 | convolution fusion | flops 201326592 | bytes 1605632 | tf_op jit(solution)/shard_map/tgn,gkhnc->tgkhc/dot_general | solution.py:140
  188.4 41.5 %all-to-all-done.3 = f32[256,16,256]{2,0,1:T(8,128)} async-done(((f32[256,16,256]{2,0,1:T(8,128)}), f32[256,16,256]{2,0,1:T(8,128)}, u32[]{:S(2)}, u32[]{:S(2)}) %all-to-all-start.3) | async-done | bytes 4194336 | tf_op jit(solution)/shard_map/all_to_all | solution.py:243
  233.3 3.4 %all-to-all-start.4 = ((f32[256,8,32]{0,2,1:T(8,128)}), f32[256,8,32]{0,2,1:T(8,128)S(1)}, u32[]{:S(2)}, u32[]{:S(2)}) async-start(f32[256,8,32]{0,2,1:T(8,128)} %bitcast.183), calls=%async_computation.5 | async-start | bytes 524288 | tf_op jit(solution)/shard_map/all_to_all | solution.py:246
  242.2 4.8 %all-to-all-done.4 = f32[256,8,32]{0,2,1:T(8,128)S(1)} async-done(((f32[256,8,32]{0,2,1:T(8,128)}), f32[256,8,32]{0,2,1:T(8,128)S(1)}, u32[]{:S(2)}, u32[]{:S(2)}) %all-to-all-start.4) | async-done | bytes 262176 | tf_op jit(solution)/shard_map/all_to_all | solution.py:246
  (75 shorter events, 43.1 us)
Async XLA Ops:
  37.8 7.3 %copy-start.10 = (f32[1,32,128]{2,1,0:T(8,128)S(1)}, f32[1,32,128]{2,1,0:T(8,128)}, u32[]{:S(2)}) copy-start(f32[1,32,128]{2,1,0:T(8,128)} %param.11) | copy-start | bytes 49156
  37.8 7.7 %copy-start.8 = (bf16[1,128,2048]{2,1,0:T(8,128)(2,1)S(1)}, bf16[1,128,2048]{2,1,0:T(8,128)(2,1)}, u32[]{:S(2)}) copy-start(bf16[1,128,2048]{2,1,0:T(8,128)(2,1)} %param.9) | copy-start | bytes 1572868
  37.8 8.7 %copy-start.9 = (bf16[1,128,2048]{2,1,0:T(8,128)(2,1)S(1)}, bf16[1,128,2048]{2,1,0:T(8,128)(2,1)}, u32[]{:S(2)}) copy-start(bf16[1,128,2048]{2,1,0:T(8,128)(2,1)} %param.13) | copy-start | bytes 1572868
  37.8 30.6 %all-to-all-start = ((bf16[16,8,32,256]{3,2,1,0:T(8,128)(2,1)}), bf16[16,8,32,256]{3,2,1,0:T(8,128)(2,1)S(1)}, u32[]{:S(2)}, u32[]{:S(2)}) async-start(bf16[16,8,32,256]{3,2,1,0:T(8,128)(2,1)} %broadcast_in_dim.82), calls=%async_computation | async-start | bytes 4194304 | tf_op jit(solution)/shard_map/all_to_all | solution.py:180
  127.7 28.5 %all-to-all-start.2 = ((f32[64,1,4096]{2,1,0:T(1,128)}), f32[64,1,4096]{2,1,0:T(1,128)}, u32[]{:S(2)}, u32[]{:S(2)}) async-start(f32[64,1,4096]{2,1,0:T(1,128)} %copy.71), calls=%async_computation.2 | async-start | bytes 2097152 | tf_op jit(solution)/shard_map/all_to_all | solution.py:38
  135.6 1.6 copy-start.3
  137.2 2.4 copy-start.11
  169.5 3.6 %copy-start.1 = (f32[64,64,32]{1,2,0:T(8,128)S(1)}, f32[64,64,32]{1,2,0:T(8,128)}, u32[]{:S(2)}) copy-start(f32[64,64,32]{1,2,0:T(8,128)} %copy.73) | copy-start | bytes 1572868
  169.5 3.6 %copy-start.4 = (bf16[1,128,2048]{1,2,0:T(8,128)(2,1)S(1)}, bf16[1,128,2048]{1,2,0:T(8,128)(2,1)}, u32[]{:S(2)}) copy-start(bf16[1,128,2048]{1,2,0:T(8,128)(2,1)} %copy.64) | copy-start | bytes 1572868
  169.5 5.5 %copy-start.7 = (bf16[4096,128]{1,0:T(8,128)(2,1)S(1)}, bf16[4096,128]{1,0:T(8,128)(2,1)}, u32[]{:S(2)}) copy-start(bf16[4096,128]{1,0:T(8,128)(2,1)} %copy.87) | copy-start | bytes 3145732
  177.7 52.3 %all-to-all-start.3 = ((f32[256,16,256]{2,0,1:T(8,128)}), f32[256,16,256]{2,0,1:T(8,128)}, u32[]{:S(2)}, u32[]{:S(2)}) async-start(f32[256,16,256]{2,0,1:T(8,128)} %fusion.46), calls=%async_computation.4 | async-start | bytes 8388608 | tf_op jit(solution)/shard_map/all_to_all | solution.py:243
  183.7 64.1 %reduce-scatter.2.cloned.1.call-start = ((), (), s32[]{:S(2)}) async-start(), calls=%async_computation.6 | async-start | bytes 1572864 | tf_op jit(solution)/shard_map/reduce_scatter | solution.py:238
  188.4 48.3 %copy-start.2 = (f32[64,64,32]{1,2,0:T(8,128)S(1)}, f32[64,64,32]{1,2,0:T(8,128)}, u32[]{:S(2)}) copy-start(f32[64,64,32]{1,2,0:T(8,128)} %copy.73) | copy-start | bytes 1572868
  232.4 4.9 %copy-start = (f32[1,128,2048]{1,2,0:T(8,128)S(1)}, f32[1,128,2048]{1,2,0:T(8,128)}, u32[]{:S(2)}) copy-start(f32[1,128,2048]{1,2,0:T(8,128)} %convert_element_type.118) | copy-start | bytes 3145732
  233.3 13.8 %all-to-all-start.4 = ((f32[256,8,32]{0,2,1:T(8,128)}), f32[256,8,32]{0,2,1:T(8,128)S(1)}, u32[]{:S(2)}, u32[]{:S(2)}) async-start(f32[256,8,32]{0,2,1:T(8,128)} %bitcast.183), calls=%async_computation.5 | async-start | bytes 524288 | tf_op jit(solution)/shard_map/all_to_all | solution.py:246
  236.7 1.2 copy-start.5
  236.7 1.5 copy-start.6
Sparse Core Ops, SparseCore 0:
  187.5 10.5 reduce-scatter.1

commit v16 on v15

--- a/solution.py
+++ b/solution.py
@@ -177,13 +177,7 @@
     inner_count = lax.axis_size(INNER)
     outer_count = lax.axis_size(OUTER)
     weight_inner = lax.all_gather(weight_local, INNER, axis=0)
-    weight_full = lax.all_to_all(
-        jnp.broadcast_to(weight_inner[None], (outer_count,) + weight_inner.shape),
-        OUTER,
-        0,
-        0,
-        tiled=True,
-    ).reshape(-1, col_count)
+    weight_full = lax.all_gather(weight_inner, OUTER, axis=0).reshape(-1, col_count)
     bc_sums = jnp.dot(tokens, weight_full, preferred_element_type=jnp.float32)
     group_count = col_count // (2 * STATE)
     head_count = values_in.shape[2] // HEAD_DIM

time: 256 us -> 295 us (1.15)
  waiting for transfers between devices: 72.3 us -> 111 us
  blocking collectives: 59.6 us -> 68.8 us
  other arithmetic: 13.2 us -> 7.99 us
    all_gather x0 -> x1, waiting for transfers between devices: none -> 42.4 us  [body(): lax.all_gather(weight_inner, OUTER, axis=0).reshape(-1, col_count)]
    all_to_all x1 -> x0, waiting for transfers between devices: 12.5 us -> none  [body(): lax.all_to_all(jnp.broadcast_to(weight_inner[None], (outer_count,) + weig...]
    all_to_all x1, blocking collectives: 31.3 us -> 38.6 us  [carried_both(): got = lax.all_to_all(packed[:, None], axis, 0, 0, tiled=True)[:, 0]]
    all_to_all x1 -> x0, starting transfers between devices: 7.3 us -> none  [body(): lax.all_to_all(jnp.broadcast_to(weight_inner[None], (outer_count,) + weig...]
    all_to_all x1, starting transfers between devices: 3.41 us -> 9.06 us  [body(): lax.all_to_all(proj_parts.reshape(col_count, inner_count, -1), INNER, 1,...]
    all_to_all x1, waiting for transfers between devices: 13.5 us -> 18.6 us  [carried_both(): lax.all_to_all(jnp.concatenate([fwd, bwd], 1)[:, None], axis, 0, 0, tiled...]
    all_to_all x1, waiting for transfers between devices: 41.5 us -> 44.9 us  [body(): lax.all_to_all(proj_terms.reshape(col_count, outer_count, -1), OUTER, 1,...]
    unnamed x30 -> x24, local copies, waits for them, and re-layouts: 7.06 us -> 7.36 us
  transfers between devices with their start and end apart: 5 -> 5, of which waited for: 4 -> 4; matrix products, arithmetic and copies ran while one was open for 13% -> 10% of each run, Pallas kernels for 0% -> 0%
where the time goes in v16:
time: 295 us; the launch traced here: 294 us
  waiting for transfers between devices  111 us (38%)
  blocking collectives  68.8 us (23%)
  local copies, waits for them, and re-layouts  45 us (15%)
  matrix products  26.5 us (9%)
  starting transfers between devices  20.7 us (7%)
  between operations  14.3 us (5%)
  other arithmetic  7.99 us (3%)
    all_to_all x1, waiting for transfers between devices, body(): lax.all_to_all(proj_terms.reshape(col_count, outer_count, -1), OUTER, 1,...  44.9 us
    all_gather x1, waiting for transfers between devices, body(): lax.all_gather(weight_inner, OUTER, axis=0).reshape(-1, col_count)  42.4 us
    all_to_all x1, blocking collectives, carried_both(): got = lax.all_to_all(packed[:, None], axis, 0, 0, tiled=True)[:, 0]  38.6 us
    all_gather x1, blocking collectives, body(): weight_inner = lax.all_gather(weight_local, INNER, axis=0)  30.2 us
    all_to_all x1, waiting for transfers between devices, carried_both(): lax.all_to_all(jnp.concatenate([fwd, bwd], 1)[:, None], axis, 0, 0, tiled...  18.6 us
    all_to_all x1, starting transfers between devices, body(): lax.all_to_all(proj_parts.reshape(col_count, inner_count, -1), INNER, 1,...  9.06 us
    unnamed x24, local copies, waits for them, and re-layouts  7.36 us
    optimization_barrier x2, local copies, waits for them, and re-layouts, span_full(): lax.optimization_barrier(((y_local, vals_local, c_local, b_local), state_...  6.36 us
  transfers between devices with their start and end apart: 5, of which 4 were waited for; matrix products, arithmetic and copies ran while one was open for 10% of the time, Pallas kernels for 0%

profile of v16, /device:TPU:24, one launch (start us, length us, event | category | flops | bytes accessed | tf_op | source)
XLA Modules:
  0.0 294.3 jit_solution(989417348677434550)
XLA Ops:
  8.0 30.2 %all_gather.9 = bf16[8,32,256]{2,1,0:T(8,128)(2,1)} all-gather(bf16[1,32,256]{2,1,0:T(8,128)(2,1)S(1)} %all_gather_reshape.3), channel_id=1, replica_groups=mesh['dp'=2,'ylo'=2,'x'=4,'z'=8,'head'=2] {'z'}, dimensions={0}, use_global_device_ids=true | all-gather | bytes 147456 | tf_op jit(solution)/shard_map/all_gather | solution.py:179
  44.7 42.4 %all-gather.3.cloned.1.call-done = bf16[128,32,256]{2,1,0:T(8,128)(2,1)} async-done(((bf16[8,32,256]{2,1,0:T(8,128)(2,1)}), bf16[128,32,256]{2,1,0:T(8,128)(2,1)}) %all-gather.3.cloned.1.call-update) | async-done | bytes 2097168 | tf_op jit(solution)/shard_map/all_gather | solution.py:180
  87.1 2.4 convolution_convert_fusion.1
  91.2 3.2 %copy.69 = f32[2,16,2,64,32]{4,3,2,1,0:T(8,128)} copy(f32[2,16,2,64,32]{3,4,2,1,0:T(8,128)} %convolution_bitcast_fusion) | data formatting | bytes 1048576 | tf_op jit(solution)/shard_map/qgn,qgkhc->gkhnc/transpose | solution.py:59
  94.4 3.1 %reshape.135 = f32[64,2048]{1,0:T(8,128)} reshape(f32[2,16,2,64,32]{4,3,2,1,0:T(8,128)} %copy.69) | data formatting | bytes 1048576 | tf_op jit(solution)/shard_map/reshape | solution.py:62
  97.5 2.7 convolution_bitcast_fusion.1
  100.2 3.2 %copy.68 = f32[2,16,2,64,32]{4,3,2,1,0:T(8,128)} copy(f32[2,16,2,64,32]{3,4,2,1,0:T(8,128)} %convolution_bitcast_fusion.1) | data formatting | bytes 1048576 | tf_op jit(solution)/shard_map/qgn,qgkhc->gkhnc/transpose | solution.py:56
  103.4 3.1 %reshape.134 = f32[64,2048]{1,0:T(8,128)} reshape(f32[2,16,2,64,32]{4,3,2,1,0:T(8,128)} %copy.68) | data formatting | bytes 1048576 | tf_op jit(solution)/shard_map/reshape | solution.py:62
  108.7 2.3 copy.70
  111.0 38.6 %all_to_all.20 = f32[64,1,4160]{2,1,0:T(1,128)S(1)} all-to-all(f32[64,1,4160]{2,1,0:T(1,128)S(1)} %copy.70), channel_id=1, replica_groups=mesh['dp'=2,'ylo'=2,'x'=4,'z'=8,'head'=2] {'ylo','x','z'}, dimensions={0} | all-to-all | bytes 2129920 | tf_op jit(solution)/shard_map/all_to_all | solution.py:25
  153.3 5.6 %all-to-all-start.1 = ((f32[64,1,4096]{2,1,0:T(1,128)}), f32[64,1,4096]{2,1,0:T(1,128)}, u32[]{:S(2)}, u32[]{:S(2)}) async-start(f32[64,1,4096]{2,1,0:T(1,128)} %copy.71), calls=%async_computation.1 | async-start | bytes 2097152 | tf_op jit(solution)/shard_map/all_to_all | solution.py:38
  167.8 18.6 %all-to-all-done.1 = f32[64,1,4096]{2,1,0:T(1,128)} async-done(((f32[64,1,4096]{2,1,0:T(1,128)}), f32[64,1,4096]{2,1,0:T(1,128)}, u32[]{:S(2)}, u32[]{:S(2)}) %all-to-all-start.1) | async-done | bytes 1048608 | tf_op jit(solution)/shard_map/all_to_all | solution.py:38
  186.4 3.9 %copy.72 = f32[64,1,4096]{0,2,1:T(8,128)} copy(f32[64,1,4096]{2,1,0:T(1,128)} %all-to-all-done.1) | data formatting | bytes 2097152 | tf_op jit(solution)/shard_map/all_to_all | solution.py:38
  190.4 3.1 %slice_bitcast_fusion = (f32[64,64,32]{0,2,1:T(8,128)}, f32[64,64,32]{0,2,1:T(8,128)}) fusion(f32[64,2,64,32]{0,3,2,1:T(8,128)} %bitcast.165), kind=kLoop, calls=%fused_computation.27 | loop fusion | bytes 2097152 | tf_op jit(solution)/shard_map/squeeze | solution.py:40
  193.4 3.2 %copy.73 = f32[64,64,32]{1,2,0:T(8,128)} copy(f32[64,64,32]{0,2,1:T(8,128)} %get-tuple-element.11) | data formatting | bytes 1048576 | tf_op jit(solution)/shard_map/optimization_barrier | solution.py:134
  196.6 3.2 %copy.76 = f32[64,64,32]{1,2,0:T(8,128)} copy(f32[64,64,32]{0,2,1:T(8,128)} %get-tuple-element.13) | data formatting | bytes 1048576 | tf_op jit(solution)/shard_map/optimization_barrier | solution.py:134
  199.8 3.4 %fusion.10 = bf16[128,1,2,64]{0,3,2,1:T(8,128)(2,1)S(1)} fusion(f32[128,2,64]{0,2,1:T(8,128)S(1)} %convolution_bitcast_fusion.6, f32[2,16,2,64,32]{3,4,2,1,0:T(8,128)} %bitcast.157, bf16[128,2,16,2,32]{0,4,3,2,1:T(8,128)(2,1)} %bitcast.160, f32[128,2,16]{0,2,1:T(8,128)S(1)} %bitcast.187), kind=kOutput, calls=%fused_computation.24 | convolution fusion | flops 201883648 | bytes 1163264 | tf_op jit(solution)/shard_map/sgkhc,gkhnc->sgn/dot_general | solution.py:162
  205.1 2.7 fusion.46
  207.7 6.0 %all-to-all-start.2 = ((f32[256,16,256]{2,0,1:T(8,128)}), f32[256,16,256]{2,0,1:T(8,128)}, u32[]{:S(2)}, u32[]{:S(2)}) async-start(f32[256,16,256]{2,0,1:T(8,128)} %fusion.46), calls=%async_computation.3 | async-start | bytes 8388608 | tf_op jit(solution)/shard_map/all_to_all | solution.py:237
  213.8 3.5 %convolution_convert_fusion = bf16[128,4096]{1,0:T(8,128)(2,1)} fusion(bf16[128,256]{0,1:T(8,128)(2,1)S(1)} %bitcast.185, bf16[4096,256]{1,0:T(8,128)(2,1)} %bitcast.164), kind=kOutput, calls=%fused_computation | convolution fusion | flops 268959744 | bytes 3211264 | tf_op jit(solution)/shard_map/tc,dc->td/dot_general | solution.py:229
  219.0 44.9 %all-to-all-done.2 = f32[256,16,256]{2,0,1:T(8,128)} async-done(((f32[256,16,256]{2,0,1:T(8,128)}), f32[256,16,256]{2,0,1:T(8,128)}, u32[]{:S(2)}, u32[]{:S(2)}) %all-to-all-start.2) | async-done | bytes 4194336 | tf_op jit(solution)/shard_map/all_to_all | solution.py:237
  263.9 2.5 reduce_sum.28
  267.2 9.1 %all-to-all-start.3 = ((f32[256,8,32]{0,2,1:T(8,128)}), f32[256,8,32]{0,2,1:T(8,128)S(1)}, u32[]{:S(2)}, u32[]{:S(2)}) async-start(f32[256,8,32]{0,2,1:T(8,128)} %bitcast.183), calls=%async_computation.4 | async-start | bytes 524288 | tf_op jit(solution)/shard_map/all_to_all | solution.py:240
  281.8 4.9 %all-to-all-done.3 = f32[256,8,32]{0,2,1:T(8,128)S(1)} async-done(((f32[256,8,32]{0,2,1:T(8,128)}), f32[256,8,32]{0,2,1:T(8,128)S(1)}, u32[]{:S(2)}, u32[]{:S(2)}) %all-to-all-start.3) | async-done | bytes 262176 | tf_op jit(solution)/shard_map/all_to_all | solution.py:240
  (69 shorter events, 34.3 us)
Async XLA Ops:
  7.2 36.5 %copy-start.7 = (bf16[1,128,2048]{2,1,0:T(8,128)(2,1)S(1)}, bf16[1,128,2048]{2,1,0:T(8,128)(2,1)}, u32[]{:S(2)}) copy-start(bf16[1,128,2048]{2,1,0:T(8,128)(2,1)} %param.13) | copy-start | bytes 1572868
  7.2 79.9 %all-gather.3.cloned.1.call-start = ((), (), s32[]{:S(2)}) async-start(), calls=%async_computation.6 | async-start | bytes 2228224 | tf_op jit(solution)/shard_map/all_gather | solution.py:180
  153.3 33.1 %all-to-all-start.1 = ((f32[64,1,4096]{2,1,0:T(1,128)}), f32[64,1,4096]{2,1,0:T(1,128)}, u32[]{:S(2)}, u32[]{:S(2)}) async-start(f32[64,1,4096]{2,1,0:T(1,128)} %copy.71), calls=%async_computation.1 | async-start | bytes 2097152 | tf_op jit(solution)/shard_map/all_to_all | solution.py:38
  161.2 1.0 copy-start.3
  162.3 2.3 copy-start.8
  199.8 3.4 %copy-start = (f32[64,64,32]{1,2,0:T(8,128)S(1)}, f32[64,64,32]{1,2,0:T(8,128)}, u32[]{:S(2)}) copy-start(f32[64,64,32]{1,2,0:T(8,128)} %copy.76) | copy-start | bytes 1572868
  199.8 5.3 %copy-start.6 = (bf16[4096,128]{1,0:T(8,128)(2,1)S(1)}, bf16[4096,128]{1,0:T(8,128)(2,1)}, u32[]{:S(2)}) copy-start(bf16[4096,128]{1,0:T(8,128)(2,1)} %copy.87) | copy-start | bytes 3145732
  207.7 56.1 %all-to-all-start.2 = ((f32[256,16,256]{2,0,1:T(8,128)}), f32[256,16,256]{2,0,1:T(8,128)}, u32[]{:S(2)}, u32[]{:S(2)}) async-start(f32[256,16,256]{2,0,1:T(8,128)} %fusion.46), calls=%async_computation.3 | async-start | bytes 8388608 | tf_op jit(solution)/shard_map/all_to_all | solution.py:237
  213.7 73.7 %reduce-scatter.2.cloned.1.call-start = ((), (), s32[]{:S(2)}) async-start(), calls=%async_computation.5 | async-start | bytes 1572864 | tf_op jit(solution)/shard_map/reduce_scatter | solution.py:232
  213.8 3.5 %copy-start.2 = (f32[64,64,32]{1,2,0:T(8,128)S(1)}, f32[64,64,32]{1,2,0:T(8,128)}, u32[]{:S(2)}) copy-start(f32[64,64,32]{1,2,0:T(8,128)} %copy.73) | copy-start | bytes 1572868
  219.0 57.3 %copy-start.1 = (f32[64,64,32]{1,2,0:T(8,128)S(1)}, f32[64,64,32]{1,2,0:T(8,128)}, u32[]{:S(2)}) copy-start(f32[64,64,32]{1,2,0:T(8,128)} %copy.76) | copy-start | bytes 1572868
  267.2 19.5 %all-to-all-start.3 = ((f32[256,8,32]{0,2,1:T(8,128)}), f32[256,8,32]{0,2,1:T(8,128)S(1)}, u32[]{:S(2)}, u32[]{:S(2)}) async-start(f32[256,8,32]{0,2,1:T(8,128)} %bitcast.183), calls=%async_computation.4 | async-start | bytes 524288 | tf_op jit(solution)/shard_map/all_to_all | solution.py:240
  276.3 1.2 copy-start.4
  276.3 1.5 copy-start.5
Sparse Core Ops, SparseCore 0:
  38.4 48.6 all-gather.2
  217.6 10.5 reduce-scatter.1
